TPU v7x, 32 devices: a whole 2x2x4 slice. The times are simulated.
32 devices in a mesh: hyper: 2 (over x), row: 16 (over z, y, core).
Axes of the slice: x: 2, y: 2, z: 4, core: 2. Of those that a mesh axis runs over, the one named last changes fastest.
Arguments:
- carried_block: float32 [8192, 4096], P(('hyper', 'row')), parts along dimension 0, as said below
- coupling_values: float32 [8192, 256], P(('hyper', 'row')), parts along dimension 0, may hold values from -0.15 to 0.15
- block_cols: int32 [128, 8], P('row'), may hold values from 0 to 127, as said below
- next_block: float32 [8192, 4096], P(('hyper', 'row')), parts along dimension 0, as said below
- fixed_rows: float32 [32, 4096], P('hyper', 'row'), parts along dimension 0, may hold values from -0.1875 to 0.1875
- fixed_next: float32 [32, 4096], P('hyper', 'row'), parts along dimension 0, may hold values from -6 to 6
- tip_block: float32 [32, 16], P('hyper'), parts along dimension 0, as said below
Outputs:
- factor_state: float32 [8192, 4096], P(('hyper', 'row')), parts along dimension 0
- coupling_factor: float32 [8192, 4096], P(('hyper', 'row')), parts along dimension 0
- carried_next: float32 [8192, 4096], P(('hyper', 'row')), parts along dimension 0
- fixed_factor: float32 [32, 4096], P('hyper', 'row'), parts along dimension 0
- fixed_carried: float32 [32, 4096], P('hyper', 'row'), parts along dimension 0
- tip_next: float32 [32, 16], P('hyper'), parts along dimension 0
There are 2 independent parts, one for each index of `hyper`. A program takes and returns all parts, laid end to end along the dimension named above; an argument that names none is the same for every part. Nothing has to cross between parts.
Inputs may be any that keep to these rules, and one draw needn't show every extreme that they name: `block_cols`: row r lists 8 distinct block columns; the first is r itself, the others lie within 32 blocks of r, cyclically. `carried_block`: symmetric positive definite. `next_block`: symmetric positive definite. `tip_block`: Symmetric.
All inputs are finite; a program needn't handle non-finite values.
Results may differ from a plain program's by a relative error of at most 0.0001.
Values sent between devices are 32-bit elements; how exact they have to be, the bound alone decides.
No kernel may reach another device: no remote copies, remote signals or barrier semaphores. Data moves between devices by JAX's collectives and lax.ppermute only.
A program may use at most 128 MiB of HBM per device.

v0:
```python
import jax
import jax.numpy as jnp
from jax import lax
from jax.sharding import PartitionSpec as P

PANELS = 4
NB = 128


def broadcast(block, axis, owner):
    block = jnp.where(lax.axis_index(axis) == owner, block, jnp.zeros_like(block))
    return lax.psum(block, axis)


def matmul(left, right):
    return jnp.dot(left, right, precision=lax.Precision.HIGHEST, preferred_element_type=jnp.float32)


def assemble(block_cols, values):
    block_rows, nonzero = block_cols.shape
    width = values.shape[1] // nonzero
    columns = jnp.arange(NB, dtype=jnp.int32)
    onehot = (block_cols[:, :, None] == columns[None, None, :]).astype(values.dtype)
    shaped = values.reshape(block_rows, width, nonzero, width)
    dense = jnp.einsum("bsn,btsc->btnc", onehot, shaped, precision=lax.Precision.HIGHEST)
    return dense.reshape(block_rows * width, NB * width)


def lower_solve(tile, right):
    return jax.scipy.linalg.solve_triangular(tile, right, lower=True)


def on_device(
    carried_block, coupling_values, block_cols, next_block, fixed_rows, fixed_next, tip_block
):
    local_rows = carried_block.shape[0]
    own_index = lax.axis_index("row")
    column = jnp.arange(carried_block.shape[1], dtype=jnp.int32)
    identity_tile = jnp.eye(local_rows, dtype=jnp.float32)
    coupled_start = assemble(block_cols, coupling_values)

    def step(panel, carry_in):
        state, coupled, carried, fixed, fixed_carry, partial_value = carry_in
        begin = panel * local_rows
        own_cols = lax.dynamic_slice_in_dim(state, begin, local_rows, 1)
        coupled_cols = lax.dynamic_slice_in_dim(coupled, begin, local_rows, 1)
        is_owner = own_index == panel
        tile_input = jnp.where(is_owner, own_cols, identity_tile)
        own_tile = jnp.linalg.cholesky(tile_input)
        own_fixed = lower_solve(own_tile, fixed.T).T
        tile, fixed_panel = (broadcast(own_tile, "row", panel), broadcast(own_fixed, "row", panel))
        solved_mine = lower_solve(tile, own_cols.T)
        solved_mine = jnp.where(own_index > panel, solved_mine, jnp.where(is_owner, tile.T, 0.0))
        coupled_mine = lower_solve(tile, coupled_cols.T)
        lower_rows = solved_mine.T
        coupled_rows = coupled_mine.T
        piece = lax.all_gather(jnp.stack([solved_mine, coupled_mine]), "row", axis=2, tiled=True)
        updates = jnp.stack(
            [
                matmul(lower_rows, piece[0]),
                matmul(coupled_rows, piece[0]),
                matmul(coupled_rows, piece[1]),
            ]
        )
        state = state - updates[0]
        state = lax.dynamic_update_slice_in_dim(state, lower_rows, begin, 1)
        state = jnp.where(is_owner & (column[None, :] >= begin + local_rows), 0.0, state)
        coupled = coupled - updates[1]
        coupled = lax.dynamic_update_slice_in_dim(coupled, coupled_rows, begin, 1)
        carried = carried - updates[2]
        fixed = fixed - matmul(fixed_panel, solved_mine)
        fixed = jnp.where(is_owner, fixed_panel, fixed)
        fixed_carry = fixed_carry - matmul(fixed_panel, coupled_mine)
        square = matmul(fixed_panel, fixed_panel.T)
        partial_value = partial_value + jnp.where(is_owner, square, 0.0)
        return (state, coupled, carried, fixed, fixed_carry, partial_value)

    start_state = (
        carried_block,
        coupled_start,
        next_block,
        fixed_rows,
        fixed_next,
        jnp.zeros_like(tip_block),
    )
    state, coupled, carried, fixed, fixed_carry, partial_value = lax.fori_loop(
        0, PANELS, step, start_state
    )
    tip_next = tip_block - lax.psum(partial_value, "row")
    return (state, coupled, carried, fixed, fixed_carry, tip_next)


def solution(mesh):
    return jax.shard_map(
        on_device,
        mesh=mesh,
        in_specs=(
            P(("hyper", "row"), None),
            P(("hyper", "row"), None),
            P("row", None),
            P(("hyper", "row"), None),
            P("hyper", "row"),
            P("hyper", "row"),
            P("hyper", None),
        ),
        out_specs=(
            P(("hyper", "row"), None),
            P(("hyper", "row"), None),
            P(("hyper", "row"), None),
            P("hyper", "row"),
            P("hyper", "row"),
            P("hyper", None),
        ),
        check_vma=False,
    )
```

profile of v0, /device:TPU:0, one launch (start us, length us, event | category | flops | bytes accessed | tf_op | source)
XLA Modules:
  0.0 1204.6 jit_solution(10268459732138265144)
XLA Ops:
  7.2 4.7 copy.107
  12.2 5.1 convolution_bitcast_fusion
  17.2 10.4 copy.37
  27.7 13.0 %reshape.75 = f32[256,4096]{1,0:T(8,128)} reshape(f32[8,32,128,32]{3,2,1,0:T(8,128)} %copy.37) | data formatting | bytes 8388608 | tf_op jit(solution)/shard_map/reshape | solution.py:26
  40.7 5.6 copy.38
  46.3 1115.2 %while.34 = (s32[]{:T(128)}, f32[256,4096]{0,1:T(8,128)}, f32[256,4096]{1,0:T(8,128)}, f32[256,4096]{1,0:T(8,128)}, f32[16,256]{1,0:T(8,128)S(1)}, /*index=5*/f3...) while((s32[]{:T(128)}, f32[256,4096]{0,1:T(8,128)}, ...), condition=%wide.region_7.9_spmd.clone, body=%wide.region_0.8_spmd.clone.sunk | while | flops 10057272320 | bytes 141284144 | solution.py:86
  47.8 11.7 cholesky.232
  59.5 9.8 custom-call.43
  70.0 11.7 cholesky.234
  85.6 90.5 %all-reduce.3.cloned.1.call-done = f32[256,256]{0,1:T(8,128)} async-done(((f32[256,256]{0,1:T(8,128)}), f32[256,256]{0,1:T(8,128)}) %all-reduce.3.cloned.1.call-update) | async-done | bytes 262160 | tf_op jit(solution)/shard_map/while/body/eval_jaxpr/psum | solution.py:12
  177.2 4.2 while.35
  181.5 19.7 %custom-call.44 = f32[2,128,128]{1,2,0:T(8,128)S(1)} custom-call(f32[2,128,128]{2,1,0:T(8,128)S(1)} %get-tuple-element.487), custom_call_target="InvertDiagBlocksLowerTriangular" | custom-call | tf_op jit(solution)/shard_map/while/body/eval_jaxpr/jit(_solve_triangular)/triangular_solve | solution.py:30
  204.1 5.6 copy.53
  209.7 4.3 while.36
  214.0 19.7 %custom-call.45 = f32[2,128,128]{1,2,0:T(8,128)S(1)} custom-call(f32[2,128,128]{2,1,0:T(8,128)S(1)} %get-tuple-element.491), custom_call_target="InvertDiagBlocksLowerTriangular" | custom-call | tf_op jit(solution)/shard_map/while/body/eval_jaxpr/jit(_solve_triangular)/triangular_solve | solution.py:30
  234.2 61.5 %psum.35 = f32[16,256]{1,0:T(8,128)S(1)} all-reduce(f32[16,256]{1,0:T(8,128)S(1)} %fusion.126), channel_id=1, replica_groups=mesh['hyper'=2,'row'=16] {'row'}, use_global_device_ids=true, to_apply=%region_6.7 | all-reduce | flops 4096 | bytes 32768 | tf_op jit(solution)/shard_map/while/body/eval_jaxpr/psum | solution.py:12
  296.6 7.5 convolution_subtract_fusion.20
  306.5 5.6 copy.59
  312.1 8.9 convolution_subtract_fusion.21
  321.7 5.7 convolution_subtract_fusion.22
  330.7 11.7 cholesky.232
  342.4 9.8 custom-call.43
  352.9 11.7 cholesky.234
  368.5 85.0 %all-reduce.3.cloned.1.call-done = f32[256,256]{0,1:T(8,128)} async-done(((f32[256,256]{0,1:T(8,128)}), f32[256,256]{0,1:T(8,128)}) %all-reduce.3.cloned.1.call-update) | async-done | bytes 262160 | tf_op jit(solution)/shard_map/while/body/eval_jaxpr/psum | solution.py:12
  454.6 4.2 while.35
  458.8 19.7 %custom-call.44 = f32[2,128,128]{1,2,0:T(8,128)S(1)} custom-call(f32[2,128,128]{2,1,0:T(8,128)S(1)} %get-tuple-element.487), custom_call_target="InvertDiagBlocksLowerTriangular" | custom-call | tf_op jit(solution)/shard_map/while/body/eval_jaxpr/jit(_solve_triangular)/triangular_solve | solution.py:30
  481.5 5.6 copy.53
  487.1 4.3 while.36
  491.4 19.7 %custom-call.45 = f32[2,128,128]{1,2,0:T(8,128)S(1)} custom-call(f32[2,128,128]{2,1,0:T(8,128)S(1)} %get-tuple-element.491), custom_call_target="InvertDiagBlocksLowerTriangular" | custom-call | tf_op jit(solution)/shard_map/while/body/eval_jaxpr/jit(_solve_triangular)/triangular_solve | solution.py:30
  511.6 61.5 %psum.35 = f32[16,256]{1,0:T(8,128)S(1)} all-reduce(f32[16,256]{1,0:T(8,128)S(1)} %fusion.126), channel_id=1, replica_groups=mesh['hyper'=2,'row'=16] {'row'}, use_global_device_ids=true, to_apply=%region_6.7 | all-reduce | flops 4096 | bytes 32768 | tf_op jit(solution)/shard_map/while/body/eval_jaxpr/psum | solution.py:12
  574.0 7.5 convolution_subtract_fusion.20
  583.8 5.6 copy.59
  589.4 8.9 convolution_subtract_fusion.21
  599.1 5.7 convolution_subtract_fusion.22
  608.0 11.7 cholesky.232
  619.8 9.8 custom-call.43
  630.3 11.7 cholesky.234
  645.9 85.0 %all-reduce.3.cloned.1.call-done = f32[256,256]{0,1:T(8,128)} async-done(((f32[256,256]{0,1:T(8,128)}), f32[256,256]{0,1:T(8,128)}) %all-reduce.3.cloned.1.call-update) | async-done | bytes 262160 | tf_op jit(solution)/shard_map/while/body/eval_jaxpr/psum | solution.py:12
  731.9 4.2 while.35
  736.2 19.7 %custom-call.44 = f32[2,128,128]{1,2,0:T(8,128)S(1)} custom-call(f32[2,128,128]{2,1,0:T(8,128)S(1)} %get-tuple-element.487), custom_call_target="InvertDiagBlocksLowerTriangular" | custom-call | tf_op jit(solution)/shard_map/while/body/eval_jaxpr/jit(_solve_triangular)/triangular_solve | solution.py:30
  758.8 5.6 copy.53
  764.4 4.3 while.36
  768.7 19.7 %custom-call.45 = f32[2,128,128]{1,2,0:T(8,128)S(1)} custom-call(f32[2,128,128]{2,1,0:T(8,128)S(1)} %get-tuple-element.491), custom_call_target="InvertDiagBlocksLowerTriangular" | custom-call | tf_op jit(solution)/shard_map/while/body/eval_jaxpr/jit(_solve_triangular)/triangular_solve | solution.py:30
  788.9 61.5 %psum.35 = f32[16,256]{1,0:T(8,128)S(1)} all-reduce(f32[16,256]{1,0:T(8,128)S(1)} %fusion.126), channel_id=1, replica_groups=mesh['hyper'=2,'row'=16] {'row'}, use_global_device_ids=true, to_apply=%region_6.7 | all-reduce | flops 4096 | bytes 32768 | tf_op jit(solution)/shard_map/while/body/eval_jaxpr/psum | solution.py:12
  851.3 7.5 convolution_subtract_fusion.20
  861.2 5.6 copy.59
  866.8 8.9 convolution_subtract_fusion.21
  876.4 5.7 convolution_subtract_fusion.22
  885.4 11.7 cholesky.232
  897.1 9.8 custom-call.43
  907.6 11.7 cholesky.234
  923.2 85.0 %all-reduce.3.cloned.1.call-done = f32[256,256]{0,1:T(8,128)} async-done(((f32[256,256]{0,1:T(8,128)}), f32[256,256]{0,1:T(8,128)}) %all-reduce.3.cloned.1.call-update) | async-done | bytes 262160 | tf_op jit(solution)/shard_map/while/body/eval_jaxpr/psum | solution.py:12
  1009.3 4.2 while.35
  1013.5 19.7 %custom-call.44 = f32[2,128,128]{1,2,0:T(8,128)S(1)} custom-call(f32[2,128,128]{2,1,0:T(8,128)S(1)} %get-tuple-element.487), custom_call_target="InvertDiagBlocksLowerTriangular" | custom-call | tf_op jit(solution)/shard_map/while/body/eval_jaxpr/jit(_solve_triangular)/triangular_solve | solution.py:30
  1036.1 5.6 copy.53
  1041.8 4.3 while.36
  1046.0 19.7 %custom-call.45 = f32[2,128,128]{1,2,0:T(8,128)S(1)} custom-call(f32[2,128,128]{2,1,0:T(8,128)S(1)} %get-tuple-element.491), custom_call_target="InvertDiagBlocksLowerTriangular" | custom-call | tf_op jit(solution)/shard_map/while/body/eval_jaxpr/jit(_solve_triangular)/triangular_solve | solution.py:30
  1066.2 61.5 %psum.35 = f32[16,256]{1,0:T(8,128)S(1)} all-reduce(f32[16,256]{1,0:T(8,128)S(1)} %fusion.126), channel_id=1, replica_groups=mesh['hyper'=2,'row'=16] {'row'}, use_global_device_ids=true, to_apply=%region_6.7 | all-reduce | flops 4096 | bytes 32768 | tf_op jit(solution)/shard_map/while/body/eval_jaxpr/psum | solution.py:12
  1128.6 7.5 convolution_subtract_fusion.20
  1138.5 5.6 copy.59
  1144.1 8.9 convolution_subtract_fusion.21
  1153.8 5.7 convolution_subtract_fusion.22
  1161.5 5.6 copy.39
  1167.1 30.0 %psum.29 = f32[16,16]{1,0:T(8,128)S(1)} all-reduce(f32[16,16]{1,0:T(8,128)S(1)} %get-tuple-element.186), channel_id=1, replica_groups=mesh['hyper'=2,'row'=16] {'row'}, use_global_device_ids=true, to_apply=%region_8.10 | all-reduce | flops 256 | bytes 2048 | tf_op jit(solution)/shard_map/psum | solution.py:89
  (317 shorter events, 93.7 us)
Async XLA Ops:
  7.2 4.7 copy-start.7
  7.2 5.0 copy-start.9
  40.7 5.6 copy-start.4
  40.7 5.6 copy-start.6
  46.5 129.6 %all-reduce.3.cloned.1.call-start = ((), (), s32[]{:S(2)}) async-start(), calls=%async_computation | async-start | bytes 524288 | tf_op jit(solution)/shard_map/while/body/eval_jaxpr/psum | solution.py:12
  84.6 212.0 %all-gather.2.cloned.1.call-start = ((), (), s32[]{:S(2)}) async-start(), calls=%async_computation.1 | async-start | bytes 8912896 | tf_op jit(solution)/shard_map/while/body/eval_jaxpr/all_gather | solution.py:57
  176.1 27.0 %copy-start.2 = (f32[256,256]{0,1:T(8,128)S(1)}, f32[256,256]{0,1:T(8,128)}, u32[]{:S(2)}) copy-start(f32[256,256]{0,1:T(8,128)} %all-reduce.3.cloned.1.call-done) | copy-start | bytes 786436 | tf_op jit(solution)/shard_map/while
  312.1 9.7 copy-start
  327.5 2.0 copy-start.1
  329.5 124.0 %all-reduce.3.cloned.1.call-start = ((), (), s32[]{:S(2)}) async-start(), calls=%async_computation | async-start | bytes 524288 | tf_op jit(solution)/shard_map/while/body/eval_jaxpr/psum | solution.py:12
  367.4 206.5 %all-gather.2.cloned.1.call-start = ((), (), s32[]{:S(2)}) async-start(), calls=%async_computation.1 | async-start | bytes 8912896 | tf_op jit(solution)/shard_map/while/body/eval_jaxpr/all_gather | solution.py:57
  453.5 27.0 %copy-start.2 = (f32[256,256]{0,1:T(8,128)S(1)}, f32[256,256]{0,1:T(8,128)}, u32[]{:S(2)}) copy-start(f32[256,256]{0,1:T(8,128)} %all-reduce.3.cloned.1.call-done) | copy-start | bytes 786436 | tf_op jit(solution)/shard_map/while
  589.4 9.7 copy-start
  604.8 2.0 copy-start.1
  606.8 124.0 %all-reduce.3.cloned.1.call-start = ((), (), s32[]{:S(2)}) async-start(), calls=%async_computation | async-start | bytes 524288 | tf_op jit(solution)/shard_map/while/body/eval_jaxpr/psum | solution.py:12
  644.8 206.5 %all-gather.2.cloned.1.call-start = ((), (), s32[]{:S(2)}) async-start(), calls=%async_computation.1 | async-start | bytes 8912896 | tf_op jit(solution)/shard_map/while/body/eval_jaxpr/all_gather | solution.py:57
  730.8 27.0 %copy-start.2 = (f32[256,256]{0,1:T(8,128)S(1)}, f32[256,256]{0,1:T(8,128)}, u32[]{:S(2)}) copy-start(f32[256,256]{0,1:T(8,128)} %all-reduce.3.cloned.1.call-done) | copy-start | bytes 786436 | tf_op jit(solution)/shard_map/while
  866.8 9.7 copy-start
  882.2 2.0 copy-start.1
  884.2 124.0 %all-reduce.3.cloned.1.call-start = ((), (), s32[]{:S(2)}) async-start(), calls=%async_computation | async-start | bytes 524288 | tf_op jit(solution)/shard_map/while/body/eval_jaxpr/psum | solution.py:12
  922.1 206.5 %all-gather.2.cloned.1.call-start = ((), (), s32[]{:S(2)}) async-start(), calls=%async_computation.1 | async-start | bytes 8912896 | tf_op jit(solution)/shard_map/while/body/eval_jaxpr/all_gather | solution.py:57
  1008.2 27.0 %copy-start.2 = (f32[256,256]{0,1:T(8,128)S(1)}, f32[256,256]{0,1:T(8,128)}, u32[]{:S(2)}) copy-start(f32[256,256]{0,1:T(8,128)} %all-reduce.3.cloned.1.call-done) | copy-start | bytes 786436 | tf_op jit(solution)/shard_map/while
  1144.1 9.7 copy-start
  1159.5 2.0 copy-start.1
  1161.5 5.6 copy-start.3
  1161.5 5.6 copy-start.5
  1161.5 35.6 %copy-start.8 = (f32[16,16]{1,0:T(8,128)S(1)}, f32[16,16]{1,0:T(8,128)}, u32[]{:S(2)}) copy-start(f32[16,16]{1,0:T(8,128)} %param.17) | copy-start | bytes 3076
Sparse Core Ops, SparseCore 0:
  84.7 91.3 all-reduce.2
  204.2 79.6 all-gather.1
  367.6 85.8 all-reduce.2
  481.6 79.6 all-gather.1
  644.9 85.8 all-reduce.2
  758.9 79.6 all-gather.1
  922.3 85.8 all-reduce.2
  1036.3 79.6 all-gather.1
where the time goes:
time: 1210 us; the launch traced here: 1200 us
  waiting for transfers between devices  346 us (29%)
  other arithmetic  318 us (26%)
  blocking collectives  276 us (23%)
  local copies, waits for them, and re-layouts  136 us (11%)
  matrix products  108 us (9%)
  between operations  14.1 us (1%)
    psum x4, waiting for transfers between devices, broadcast(): return lax.psum(block, axis)  345 us
    psum x4, blocking collectives, broadcast(): return lax.psum(block, axis)  246 us
    another operation x20, other arithmetic, lower_solve(): return jax.scipy.linalg.solve_triangular(tile, right, lower=True)  165 us
    another operation x24, other arithmetic, step(): own_tile = jnp.linalg.cholesky(tile_input)  136 us
    dot_general x24, matrix products, matmul(): jnp.dot(left, right, precision=lax.Precision.HIGHEST, preferred_element_t...  90.8 us
    while x32, local copies, waits for them, and re-layouts  52.9 us
    psum x1, blocking collectives, on_device(): tip_next = tip_block - lax.psum(partial_value, 'row')  30 us
  transfers between devices with their start and end apart: 8, of which 4 were waited for; matrix products, arithmetic and copies ran while one was open for 11% of the time, Pallas kernels for 0%

commit v1 on v0

v1 whole, which is shorter than its diff:
```python
import jax
import jax.numpy as jnp
from jax import lax
from jax.sharding import PartitionSpec as P

PANELS = 4
HIGHEST = lax.Precision.HIGHEST


def mdot(left, right):
    return jnp.dot(left, right, precision=HIGHEST, preferred_element_type=jnp.float32)


def tdot(left, right):
    return lax.dot_general(
        left, right, (((1,), (1,)), ((), ())), precision=HIGHEST, preferred_element_type=jnp.float32
    )


def assemble(block_cols, values, col_blocks):
    block_rows, nonzero = block_cols.shape
    width = values.shape[1] // nonzero
    span = col_blocks * width
    shaped = values.reshape(block_rows, width, nonzero, 1, width)
    shaped = jnp.broadcast_to(shaped, (block_rows, width, nonzero, col_blocks, width))
    shaped = shaped.reshape(block_rows, width, nonzero, span)
    lane_block = jnp.arange(span, dtype=jnp.int32) // width
    hit = block_cols[:, None, :, None] == lane_block[None, None, None, :]
    dense = jnp.where(hit, shaped, 0.0).sum(axis=2)
    return dense.reshape(block_rows * width, span)


def on_device(
    carried_block, coupling_values, block_cols, next_block, fixed_rows, fixed_next, tip_block
):
    rows, size = carried_block.shape
    width = coupling_values.shape[1] // block_cols.shape[1]
    factored = PANELS * rows
    me = lax.axis_index("row")
    is_top = me < PANELS
    top_at = jnp.minimum(me, PANELS - 1) * rows

    own_cols = carried_block[:, :factored]
    gathered_cols = lax.all_gather(own_cols, "row", axis=0, tiled=True)
    all_values = lax.all_gather(coupling_values, "row", axis=0, tiled=True)
    all_block_cols = lax.all_gather(block_cols, "row", axis=0, tiled=True)
    all_fixed = lax.all_gather(fixed_rows, "row", axis=1, tiled=True)

    head = gathered_cols[:factored]
    below = gathered_cols[factored:]
    head_factor = jnp.linalg.cholesky(head)
    head_inverse = jax.scipy.linalg.solve_triangular(
        head_factor, jnp.eye(factored, dtype=jnp.float32), lower=True
    )

    lower = tdot(own_cols, head_inverse)
    lower = jnp.where(is_top, lax.dynamic_slice_in_dim(head_factor, top_at, rows, 0), lower)
    lower_scaled = mdot(lower, head_inverse)
    state_rest = carried_block[:, factored:] - tdot(lower_scaled, below)
    state_rest = jnp.where(is_top, 0.0, state_rest)
    factor_state = jnp.concatenate([lower, state_rest], axis=1)

    coupled = assemble(block_cols, coupling_values, size // width)
    coupled_panel = tdot(coupled[:, :factored], head_inverse)
    coupled_scaled = mdot(coupled_panel, head_inverse)
    coupled_rest = coupled[:, factored:] - tdot(coupled_scaled, below)
    coupling_factor = jnp.concatenate([coupled_panel, coupled_rest], axis=1)

    head_blocks = factored // width
    block_rows, nonzero = all_block_cols.shape
    scaled_blocks = coupled_scaled.T.reshape(head_blocks, width, rows)
    scaled_blocks = jnp.concatenate(
        [scaled_blocks, jnp.zeros((1, width, rows), jnp.float32)], axis=0
    )
    picks = jnp.where(all_block_cols < head_blocks, all_block_cols, head_blocks)
    picked = jnp.take(scaled_blocks, picks, axis=0).reshape(block_rows, nonzero * width, rows)
    values_rows = all_values.reshape(block_rows, width, nonzero * width)
    carry = jnp.einsum(
        "rts,rsi->rti", values_rows, picked, precision=HIGHEST, preferred_element_type=jnp.float32
    )
    carried_next = next_block - carry.reshape(block_rows * width, rows).T

    fixed_panel = tdot(all_fixed[:, :factored], head_inverse)
    own_fixed_panel = lax.dynamic_slice_in_dim(fixed_panel, top_at, rows, 1)
    fixed_factor = jnp.where(is_top, own_fixed_panel, fixed_rows - tdot(fixed_panel, lower))
    fixed_carried = fixed_next - tdot(fixed_panel, coupled_panel)
    tip_next = tip_block - tdot(fixed_panel, fixed_panel)
    return (factor_state, coupling_factor, carried_next, fixed_factor, fixed_carried, tip_next)


def solution(mesh):
    return jax.shard_map(
        on_device,
        mesh=mesh,
        in_specs=(
            P(("hyper", "row"), None),
            P(("hyper", "row"), None),
            P("row", None),
            P(("hyper", "row"), None),
            P("hyper", "row"),
            P("hyper", "row"),
            P("hyper", None),
        ),
        out_specs=(
            P(("hyper", "row"), None),
            P(("hyper", "row"), None),
            P(("hyper", "row"), None),
            P("hyper", "row"),
            P("hyper", "row"),
            P("hyper", None),
        ),
        check_vma=False,
    )
```

time: 1210 us -> 657 us (0.54)
  waiting for transfers between devices: 346 us -> 52.7 us
  blocking collectives: 276 us -> 43.1 us
  local copies, waits for them, and re-layouts: 136 us -> 99.7 us
  matrix products: 108 us -> 124 us
    psum x4 -> x0, waiting for transfers between devices: 345 us -> none  [broadcast(): return lax.psum(block, axis)]
    psum x5 -> x0, blocking collectives: 276 us -> none  [the longest x4 246 us: broadcast(): return lax.psum(block, axis)]
    while x32 -> x0, local copies, waits for them, and re-layouts: 52.9 us -> none
    all_gather x4 -> x2, waiting for transfers between devices: 0.08 us -> 52 us  [the longest x1 52 us: on_device(): gathered_cols = lax.all_gather(own_cols, 'row', axis=0, tiled=True)]
    another operation x48 -> x33, other arithmetic: 304 us -> 259 us  [the longest x30 173 us: on_device(): head_factor = jnp.linalg.cholesky(head)]
    all_gather x0 -> x2, blocking collectives: none -> 43.1 us  [the longest x1 23.6 us: on_device(): all_block_cols = lax.all_gather(block_cols, 'row', axis=0, tiled=True)]
    another operation x44 -> x29, matrix products: 11.6 us -> 44.9 us  [the longest x14 22.7 us: on_device(): head_factor = jnp.linalg.cholesky(head)]
    gather x0 -> x1, local copies, waits for them, and re-layouts: none -> 19.3 us  [on_device(): jnp.take(scaled_blocks, picks, axis=0)]
  transfers between devices with their start and end apart: 8 -> 2, of which waited for: 4 -> 1; matrix products, arithmetic and copies ran while one was open for 11% -> 76% of each run, Pallas kernels for 0% -> 0%
where the time goes in v1:
time: 657 us; the launch traced here: 651 us
  other arithmetic  312 us (47%)
  matrix products  124 us (19%)
  local copies, waits for them, and re-layouts  99.7 us (15%)
  waiting for transfers between devices  52.7 us (8%)
  blocking collectives  43.1 us (7%)
  between operations  19.9 us (3%)
    another operation x30, other arithmetic, on_device(): head_factor = jnp.linalg.cholesky(head)  173 us
    another operation x3, other arithmetic, on_device(): jax.scipy.linalg.solve_triangular(head_factor, jnp.eye(factored, dtype=jn...  86.4 us
    all_gather x1, waiting for transfers between devices, on_device(): gathered_cols = lax.all_gather(own_cols, 'row', axis=0, tiled=True)  52 us
    dot_general x8, matrix products, tdot(): lax.dot_general(left, right, (((1,), (1,)), ((), ())), precision=HIGHEST,...  46 us
    another operation x24, local copies, waits for them, and re-layouts  28 us
    dot_general x1, matrix products, on_device(): jnp.einsum('rts,rsi->rti', values_rows, picked, precision=HIGHEST, prefer...  25.5 us
    all_gather x1, blocking collectives, on_device(): all_block_cols = lax.all_gather(block_cols, 'row', axis=0, tiled=True)  23.6 us
    another operation x14, matrix products, on_device(): head_factor = jnp.linalg.cholesky(head)  22.7 us
  transfers between devices with their start and end apart: 2, of which 1 were waited for; matrix products, arithmetic and copies ran while one was open for 76% of the time, Pallas kernels for 0%

profile of v1, /device:TPU:0, one launch (start us, length us, event | category | flops | bytes accessed | tf_op | source)
XLA Modules:
  0.0 651.1 jit_solution(3717933076730545486)
XLA Ops:
  10.7 23.6 %all_gather.13 = s32[128,8]{1,0:T(8,128)S(1)} all-gather(s32[8,8]{1,0:T(8,128)S(1)} %copy-done.9), channel_id=1, replica_groups=mesh['hyper'=2,'row'=16] {'row'}, dimensions={0}, use_global_device_ids=true | all-gather | bytes 4352 | tf_op jit(solution)/shard_map/all_gather | solution.py:46
  35.0 2.5 fusion.37
  38.1 19.5 %all_gather.15 = f32[16,4096]{1,0:T(8,128)S(1)} all-gather(f32[16,256]{1,0:T(8,128)S(1)} %copy-done.7), channel_id=1, replica_groups=mesh['hyper'=2,'row'=16] {'row'}, dimensions={1}, use_global_device_ids=true | all-gather | bytes 278528 | tf_op jit(solution)/shard_map/all_gather | solution.py:47
  57.5 12.2 %select_reduce_fusion = f32[8,32,128,32]{2,3,1,0:T(8,128)} fusion(f32[8,32,8,32]{3,2,1,0:T(8,128)S(1)} %broadcast_in_dim.48, pred[8,8,128,32]{2,3,1,0:T(8,128)(4,1)S(1)} %broadcast_compare_fusion), kind=kLoop, calls=%fused_computation.4 | loop fusion | flops 15728640 | bytes 4718592 | tf_op jit(solution)/shard_map/reduce_sum | solution.py:29
  69.8 10.6 %copy.49 = f32[8,32,128,32]{3,2,1,0:T(8,128)} copy(f32[8,32,128,32]{2,3,1,0:T(8,128)} %select_reduce_fusion) | data formatting | bytes 8388608 | tf_op jit(solution)/shard_map/reduce_sum | solution.py:29
  80.3 13.1 %reshape.138 = f32[256,4096]{1,0:T(8,128)} reshape(f32[8,32,128,32]{3,2,1,0:T(8,128)} %copy.49) | data formatting | bytes 8388608 | tf_op jit(solution)/shard_map/reshape | solution.py:30
  93.4 52.0 %all-gather.3.cloned.1.call-done = f32[4096,1024]{0,1:T(8,128)} async-done(((f32[256,1024]{0,1:T(8,128)}), f32[4096,1024]{0,1:T(8,128)}) %all-gather.3.cloned.1.call-update) | async-done | bytes 16777232 | tf_op jit(solution)/shard_map/all_gather | solution.py:44
  145.4 4.8 slice.287
  150.2 5.7 copy.40
  155.8 4.4 fusion.4
  160.3 2.0 copy-done.4
  162.3 11.7 %cholesky.223 = f32[128,128]{1,0:T(8,128)S(1)} custom-call(f32[128,128]{1,0:T(8,128)S(1)} %cholesky.580), custom_call_target="Cholesky" | custom-call | tf_op jit(solution)/shard_map/jit(cholesky)/cholesky | solution.py:51
  174.1 9.8 %custom-call.63 = f32[1,128,128]{1,2,0:T(8,128)S(1)} custom-call(f32[1,128,128]{2,1,0:T(8,128)S(1)} %get-tuple-element.72), custom_call_target="InvertDiagBlocksLowerTriangular" | custom-call | tf_op jit(solution)/shard_map/jit(cholesky)/cholesky | solution.py:51
  185.6 1.9 convolution_subtract_fusion.5
  187.7 12.2 %cholesky.244 = f32[128,128]{1,0:T(8,128)S(1)} custom-call(f32[128,128]{1,0:T(8,128)S(1)} %cholesky.584), custom_call_target="Cholesky" | custom-call | tf_op jit(solution)/shard_map/jit(cholesky)/cholesky | solution.py:51
  199.9 2.5 cholesky.255
  203.9 9.8 %custom-call.64 = f32[1,128,128]{1,2,0:T(8,128)S(1)} custom-call(f32[1,128,128]{2,1,0:T(8,128)S(1)} %get-tuple-element.69), custom_call_target="InvertDiagBlocksLowerTriangular" | custom-call | tf_op jit(solution)/shard_map/jit(cholesky)/cholesky | solution.py:51
  214.9 2.1 convolution_subtract_fusion.6
  217.0 11.7 %cholesky.468 = f32[128,128]{1,0:T(8,128)S(1)} custom-call(f32[128,128]{1,0:T(8,128)S(1)} %cholesky.589), custom_call_target="Cholesky" | custom-call | tf_op jit(solution)/shard_map/jit(cholesky)/cholesky | solution.py:51
  230.0 9.8 %custom-call.65 = f32[1,128,128]{1,2,0:T(8,128)S(1)} custom-call(f32[1,128,128]{2,1,0:T(8,128)S(1)} %get-tuple-element.66), custom_call_target="InvertDiagBlocksLowerTriangular" | custom-call | tf_op jit(solution)/shard_map/jit(cholesky)/cholesky | solution.py:51
  241.0 2.3 convolution_subtract_fusion.7
  243.3 11.9 %cholesky.487 = f32[128,128]{1,0:T(8,128)S(1)} custom-call(f32[128,128]{1,0:T(8,128)S(1)} %cholesky.594), custom_call_target="Cholesky" | custom-call | tf_op jit(solution)/shard_map/jit(cholesky)/cholesky | solution.py:51
  256.5 9.8 %custom-call.66 = f32[1,128,128]{1,2,0:T(8,128)S(1)} custom-call(f32[1,128,128]{2,1,0:T(8,128)S(1)} %get-tuple-element.63), custom_call_target="InvertDiagBlocksLowerTriangular" | custom-call | tf_op jit(solution)/shard_map/jit(cholesky)/cholesky | solution.py:51
  267.4 2.3 convolution_subtract_fusion.8
  269.7 11.7 %cholesky.506 = f32[128,128]{1,0:T(8,128)S(1)} custom-call(f32[128,128]{1,0:T(8,128)S(1)} %cholesky.599), custom_call_target="Cholesky" | custom-call | tf_op jit(solution)/shard_map/jit(cholesky)/cholesky | solution.py:51
  282.7 10.0 %custom-call.67 = f32[1,128,128]{1,2,0:T(8,128)S(1)} custom-call(f32[1,128,128]{2,1,0:T(8,128)S(1)} %get-tuple-element.60), custom_call_target="InvertDiagBlocksLowerTriangular" | custom-call | tf_op jit(solution)/shard_map/jit(cholesky)/cholesky | solution.py:51
  293.7 2.3 convolution_subtract_fusion.9
  296.1 11.7 %cholesky.526 = f32[128,128]{1,0:T(8,128)S(1)} custom-call(f32[128,128]{1,0:T(8,128)S(1)} %cholesky.604), custom_call_target="Cholesky" | custom-call | tf_op jit(solution)/shard_map/jit(cholesky)/cholesky | solution.py:51
  309.1 9.8 %custom-call.68 = f32[1,128,128]{1,2,0:T(8,128)S(1)} custom-call(f32[1,128,128]{2,1,0:T(8,128)S(1)} %get-tuple-element.57), custom_call_target="InvertDiagBlocksLowerTriangular" | custom-call | tf_op jit(solution)/shard_map/jit(cholesky)/cholesky | solution.py:51
  319.9 2.0 convolution_subtract_fusion.10
  321.9 12.1 %cholesky.546 = f32[128,128]{1,0:T(8,128)S(1)} custom-call(f32[128,128]{1,0:T(8,128)S(1)} %cholesky.609), custom_call_target="Cholesky" | custom-call | tf_op jit(solution)/shard_map/jit(cholesky)/cholesky | solution.py:51
  335.3 9.8 %custom-call.69 = f32[1,128,128]{1,2,0:T(8,128)S(1)} custom-call(f32[1,128,128]{2,1,0:T(8,128)S(1)} %get-tuple-element.54), custom_call_target="InvertDiagBlocksLowerTriangular" | custom-call | tf_op jit(solution)/shard_map/jit(cholesky)/cholesky | solution.py:51
  347.8 11.7 %cholesky.564 = f32[128,128]{1,0:T(8,128)S(1)} custom-call(f32[128,128]{1,0:T(8,128)S(1)} %convolution_subtract_fusion.11), custom_call_target="Cholesky" | custom-call | tf_op jit(solution)/shard_map/jit(cholesky)/cholesky | solution.py:51
  366.5 6.8 %fusion.5 = (f32[1024,1024]{1,0:T(8,128)}, f32[1024,1024]{1,0:T(8,128)}) fusion(f32[1024,1024]{1,0:T(8,128)} %get-tuple-element.52, pred[]{:T(512)S(6)} %cholesky.579), kind=kLoop, calls=%fused_computation.17 | loop fusion | flops 4194304 | bytes 12582913 | tf_op jit(solution)/shard_map/jit(_solve_triangular)/triangular_solve | solution.py:52
  373.3 28.0 %while.1 = (s32[]{:T(128)}, f32[1024,1024]{1,0:T(8,128)}, s32[8,2]{0,1:T(2,128)S(1)}, f32[8,128,128]{2,1,0:T(8,128)}, s32[]{:T(128)}) while((s32[]{:T(128)}, f32[1024,1024]{1,0:T(8,128)}, s32[8,2]{0,1:T(2,128)S(1)}, f32[8,128,128]{2,1,0:T(8,128)}, s32[]{:T(128)}) %tuple.61), condition=%wide.while_cond, body=%wide.while_body.sunk | while | flops 2 | bytes 132205 | solution.py:52
  373.9 2.9 bitcast_dynamic-update-slice_fusion.2
  377.4 2.9 bitcast_dynamic-update-slice_fusion.2
  380.9 2.9 bitcast_dynamic-update-slice_fusion.2
  384.4 2.9 bitcast_dynamic-update-slice_fusion.2
  387.9 2.9 bitcast_dynamic-update-slice_fusion.2
  391.4 2.9 bitcast_dynamic-update-slice_fusion.2
  394.9 2.9 bitcast_dynamic-update-slice_fusion.2
  398.4 2.8 bitcast_dynamic-update-slice_fusion.2
  401.3 79.6 %custom-call.70 = f32[8,128,128]{1,2,0:T(8,128)S(1)} custom-call(f32[8,128,128]{2,1,0:T(8,128)} %get-tuple-element.13), custom_call_target="InvertDiagBlocksLowerTriangular" | custom-call | tf_op jit(solution)/shard_map/jit(_solve_triangular)/triangular_solve | solution.py:52
  481.4 1.9 convolution_subtract_fusion.4
  486.5 2.0 fusion.30
  489.3 2.2 fusion.33
  492.2 2.7 convolution_subtract_fusion.2
  495.6 2.8 convolution_subtract_fusion.1
  499.1 3.5 convolution_subtract_fusion.3
  503.2 5.8 fusion.38
  509.0 3.7 fusion.94
  515.4 19.3 %gather_fusion = f32[1024,32,256]{2,1,0:T(8,128)} fusion(f32[33,32,256]{2,1,0:T(8,128)S(1)} %concatenate.38, s32[1024]{0:T(1024)S(1)} %broadcast_clamp_fusion), kind=kCustom, calls=%fused_computation | custom fusion | bytes 67112960 | tf_op jit(solution)/shard_map/jit(_take)/gather | solution.py:76
  534.6 5.9 fusion.69
  541.4 5.4 fusion.29
  550.0 3.7 fusion.93
  553.7 13.7 %fusion.9 = f32[256,3072]{1,0:T(8,128)S(1)} fusion(f32[256,1024]{1,0:T(8,128)S(1)} %fusion.93, f32[4096,1024]{0,1:T(8,128)} %all-gather.3.cloned.1.call-done, f32[256,4096]{1,0:T(8,128)S(1)} %copy-done.5, pred[]{:T(512)S(6)} %lt.21), kind=kOutput, calls=%fused_computation.19 | convolution fusion | flops 9665249280 | bytes 19922944 | tf_op jit(solution)/shard_map/dot_general | solution.py:15
  567.5 2.4 pad_maximum_fusion
  571.2 11.3 %fusion.12 = f32[256,3072]{1,0:T(8,128)S(1)} fusion(f32[256,1024]{1,0:T(8,128)S(1)} %fusion.94, f32[4096,1024]{0,1:T(8,128)S(1)} %bitcast.138, f32[256,4096]{1,0:T(8,128)S(1)} %copy-done.2), kind=kOutput, calls=%fused_computation.20 | convolution fusion | flops 9664462848 | bytes 19922944 | tf_op jit(solution)/shard_map/dot_general | solution.py:15
  582.5 2.3 pad_maximum_fusion.1
  584.8 22.0 %bitcast_select_fusion = f32[128,256,256]{2,1,0:T(8,128)} fusion(pred[128,256]{1,0:T(8,128)(4,1)S(1)} %copy.51, f32[128,256,256]{2,1,0:T(8,128)} %bitcast.136), kind=kLoop, calls=%fused_computation.3 | loop fusion | flops 8388608 | bytes 67141632 | tf_op jit(solution)/shard_map/jit(_take)/select_n | solution.py:76
  606.8 25.5 %fusion.95 = f32[128,256,32]{1,2,0:T(8,128)} fusion(f32[128,256,256]{2,1,0:T(8,128)} %bitcast_select_fusion, f32[128,32,256]{2,1,0:T(8,128)} %bitcast.141), kind=kOutput, calls=%fused_computation.196 | convolution fusion | flops 3221225472 | bytes 41943040 | tf_op jit(solution)/shard_map/rts,rsi->rti/dot_general | solution.py:78
  632.3 5.6 copy.53
  637.9 6.1 bitcast_subtract_fusion
  (113 shorter events, 44.0 us)
Async XLA Ops:
  7.2 27.2 %copy-start.6 = (f32[256,256]{1,0:T(8,128)S(1)}, f32[256,256]{1,0:T(8,128)}, u32[]{:S(2)}) copy-start(f32[256,256]{1,0:T(8,128)} %param.8) | copy-start | bytes 786436
  7.2 3.5 copy-start.9
  7.2 138.2 %all-gather.3.cloned.1.call-start = ((), (), s32[]{:S(2)}) async-start(), calls=%async_computation | async-start | bytes 17825792 | tf_op jit(solution)/shard_map/all_gather | solution.py:44
  9.8 28.2 %copy-start.7 = (f32[16,256]{1,0:T(8,128)S(1)}, f32[16,256]{1,0:T(8,128)}, u32[]{:S(2)}) copy-start(f32[16,256]{1,0:T(8,128)} %param.11) | copy-start | bytes 49156
  9.9 596.9 %all-gather.5.cloned.1.call-start = ((), (), s32[]{:S(2)}) async-start(), calls=%async_computation.1 | async-start | bytes 4456448 | tf_op jit(solution)/shard_map/all_gather | solution.py:45
  160.3 2.0 copy-start.4
  480.9 3.2 copy-start.3
  503.2 9.5 %copy-start = (f32[1024,1024]{1,0:T(8,128)}, f32[1024,1024]{1,0:T(8,128)S(1)}, u32[]{:S(2)}) copy-start(f32[1024,1024]{1,0:T(8,128)S(1)} %convolution_dynamic-update-slice_fusion) | copy-start | bytes 12582916
  534.6 5.9 copy-start.10
  534.6 6.8 %copy-start.1 = (f32[1024,1024]{1,0:T(8,128)S(1)}, f32[1024,1024]{1,0:T(8,128)}, u32[]{:S(2)}) copy-start(f32[1024,1024]{1,0:T(8,128)} %copy-done) | copy-start | bytes 12582916
  541.4 7.0 %copy-start.8 = (f32[16,256]{1,0:T(8,128)S(1)}, f32[16,256]{1,0:T(8,128)}, u32[]{:S(2)}) copy-start(f32[16,256]{1,0:T(8,128)} %param.12) | copy-start | bytes 49156
  546.9 6.9 %copy-start.5 = (f32[256,4096]{1,0:T(8,128)S(1)}, f32[256,4096]{1,0:T(8,128)}, u32[]{:S(2)}) copy-start(f32[256,4096]{1,0:T(8,128)} %param.7) | copy-start | bytes 12582916
  550.0 20.0 %slice-start = ((s8[16777216]{0:T(1024)(128)(4,1)}), s8[4194304]{0:T(1024)(128)(4,1)S(1)}, s32[]{:S(2)}) async-start(s8[16777216]{0:T(1024)(128)(4,1)} %bitcast.137), calls=%async_computation.2 | async-start | bytes 8388608
  553.7 16.2 %slice-start.1 = ((s8[16777216]{0:T(1024)(128)(4,1)}), s8[4194304]{0:T(1024)(128)(4,1)S(1)}, s32[]{:S(2)}) async-start(s8[16777216]{0:T(1024)(128)(4,1)} %bitcast.137), calls=%async_computation.3 | async-start | bytes 8388608
  553.7 16.2 %slice-start.2 = ((s8[16777216]{0:T(1024)(128)(4,1)}), s8[4194304]{0:T(1024)(128)(4,1)S(1)}, s32[]{:S(2)}) async-start(s8[16777216]{0:T(1024)(128)(4,1)} %bitcast.137), calls=%async_computation.4 | async-start | bytes 8388608
  553.7 16.2 %slice-start.3 = ((s8[16777216]{0:T(1024)(128)(4,1)}), s8[4194304]{0:T(1024)(128)(4,1)S(1)}, s32[]{:S(2)}) async-start(s8[16777216]{0:T(1024)(128)(4,1)} %bitcast.137), calls=%async_computation.5 | async-start | bytes 8388608
  567.5 3.7 copy-start.2
Sparse Core Ops, SparseCore 0:
  10.7 134.6 all-gather.2
  147.6 49.1 all-gather.4

commit v2 on v1

v2 whole, which is shorter than its diff:
```python
import jax
import jax.numpy as jnp
from jax import lax
from jax.sharding import PartitionSpec as P

PANELS = 4
BLOCK = 128
HIGHEST = lax.Precision.HIGHEST


def mdot(left, right):
    return jnp.dot(left, right, precision=HIGHEST, preferred_element_type=jnp.float32)


def tdot(left, right):
    return lax.dot_general(
        left, right, (((1,), (1,)), ((), ())), precision=HIGHEST, preferred_element_type=jnp.float32
    )


def assemble_t(block_cols, values, col_blocks):
    block_rows, nonzero = block_cols.shape
    width = values.shape[1] // nonzero
    span = block_rows * width
    flipped = values.T.reshape(nonzero, 1, width, span)
    spread = jnp.repeat(block_cols.T, width, axis=1)
    columns = jnp.arange(col_blocks, dtype=jnp.int32)
    hit = spread[:, None, None, :] == columns[None, :, None, None]
    dense = jnp.where(hit, flipped, 0.0).sum(axis=0)
    return dense.reshape(col_blocks * width, span)


def invert_lower(factor, block_inverses):
    inverses = jnp.stack(block_inverses)
    size = inverses.shape[1]
    while inverses.shape[0] > 1:
        pairs = inverses.shape[0] // 2
        first, second = inverses[0::2], inverses[1::2]
        coupling = jnp.stack(
            [
                factor[(2 * q + 1) * size:(2 * q + 2) * size, 2 * q * size:(2 * q + 1) * size]
                for q in range(pairs)
            ]
        )
        corner = jnp.einsum("qij,qjk->qik", second, coupling, precision=HIGHEST)
        corner = -jnp.einsum("qik,qkl->qil", corner, first, precision=HIGHEST)
        top = jnp.concatenate([first, jnp.zeros_like(first)], axis=2)
        bottom = jnp.concatenate([corner, second], axis=2)
        inverses = jnp.concatenate([top, bottom], axis=1)
        size *= 2
    return inverses[0]


def on_device(
    carried_block, coupling_values, block_cols, next_block, fixed_rows, fixed_next, tip_block
):
    rows, size = carried_block.shape
    value_rows, value_cols = coupling_values.shape
    local_block_rows, nonzero = block_cols.shape
    width = value_cols // nonzero
    fixed_count = fixed_rows.shape[0]
    factored = PANELS * rows
    me = lax.axis_index("row")
    is_top = me < PANELS
    top_at = jnp.minimum(me, PANELS - 1) * rows
    fixed_cols = fixed_rows.shape[1]
    block = min(BLOCK, rows)
    cols_count = local_block_rows * nonzero
    lanes = max(value_cols, fixed_cols, cols_count)

    def widen(part):
        return jnp.pad(part, ((0, 0), (0, lanes - part.shape[1])))

    cols_row = block_cols.reshape(1, cols_count).astype(jnp.float32)
    packed = jnp.concatenate([widen(coupling_values), widen(fixed_rows), widen(cols_row)], axis=0)
    pad = (-packed.shape[0]) % 8
    packed = jnp.concatenate([packed, jnp.zeros((pad, lanes), jnp.float32)], axis=0)
    gathered = lax.all_gather(packed, "row", axis=0)
    devices = gathered.shape[0]
    all_values = gathered[:, :value_rows, :value_cols].reshape(devices * value_rows, value_cols)
    all_fixed = gathered[:, value_rows:value_rows + fixed_count, :fixed_cols].transpose(1, 0, 2)
    all_fixed = all_fixed.reshape(fixed_count, devices * fixed_cols)
    all_block_cols = gathered[:, value_rows + fixed_count, :cols_count]
    all_block_cols = jnp.round(all_block_cols).astype(jnp.int32).reshape(-1, nonzero)

    chunks = [
        lax.all_gather(carried_block[:, c * rows:(c + 1) * rows], "row", axis=0, tiled=True)
        for c in range(PANELS)
    ]

    columns = []
    block_inverses = []
    for k in range(factored // block):
        chunk, offset = divmod(k * block, rows)
        panel = chunks[chunk][k * block:factored, offset:offset + block]
        if k:
            done = jnp.concatenate([col[k * block:] for col in columns], axis=1)
            panel = panel - tdot(done, done[:block])
        diagonal = jnp.linalg.cholesky(panel[:block])
        diagonal_inverse = jax.scipy.linalg.solve_triangular(
            diagonal, jnp.eye(block, dtype=jnp.float32), lower=True
        )
        under = tdot(panel[block:], diagonal_inverse)
        column = jnp.concatenate(
            [jnp.zeros((k * block, block), jnp.float32), diagonal, under], axis=0
        )
        columns.append(column)
        block_inverses.append(diagonal_inverse)
    head_factor = jnp.concatenate(columns, axis=1)
    head_inverse = invert_lower(head_factor, block_inverses)

    def minus_below(scaled):
        total = None
        for c in range(PANELS):
            part = tdot(scaled[:, c * rows:(c + 1) * rows], chunks[c][factored:])
            total = part if total is None else total + part
        return total

    own_cols = carried_block[:, :factored]
    lower = tdot(own_cols, head_inverse)
    lower = jnp.where(is_top, lax.dynamic_slice_in_dim(head_factor, top_at, rows, 0), lower)
    lower_scaled = mdot(lower, head_inverse)
    state_rest = carried_block[:, factored:] - minus_below(lower_scaled)
    state_rest = jnp.where(is_top, 0.0, state_rest)
    factor_state = jnp.concatenate([lower, state_rest], axis=1)

    coupled = assemble_t(block_cols, coupling_values, size // width).T
    coupled_panel = tdot(coupled[:, :factored], head_inverse)
    coupled_scaled = mdot(coupled_panel, head_inverse)
    coupled_rest = coupled[:, factored:] - minus_below(coupled_scaled)
    coupling_factor = jnp.concatenate([coupled_panel, coupled_rest], axis=1)

    coupling_head_t = assemble_t(all_block_cols, all_values, factored // width)
    carried_next = next_block - mdot(coupled_scaled, coupling_head_t)

    fixed_panel = tdot(all_fixed[:, :factored], head_inverse)
    own_fixed_panel = lax.dynamic_slice_in_dim(fixed_panel, top_at, rows, 1)
    fixed_factor = jnp.where(is_top, own_fixed_panel, fixed_rows - tdot(fixed_panel, lower))
    fixed_carried = fixed_next - tdot(fixed_panel, coupled_panel)
    tip_next = tip_block - tdot(fixed_panel, fixed_panel)
    return (factor_state, coupling_factor, carried_next, fixed_factor, fixed_carried, tip_next)


def solution(mesh):
    return jax.shard_map(
        on_device,
        mesh=mesh,
        in_specs=(
            P(("hyper", "row"), None),
            P(("hyper", "row"), None),
            P("row", None),
            P(("hyper", "row"), None),
            P("hyper", "row"),
            P("hyper", "row"),
            P("hyper", None),
        ),
        out_specs=(
            P(("hyper", "row"), None),
            P(("hyper", "row"), None),
            P(("hyper", "row"), None),
            P("hyper", "row"),
            P("hyper", "row"),
            P("hyper", None),
        ),
        check_vma=False,
    )
```

time: 657 us -> 430 us (0.65)
  other arithmetic: 312 us -> 234 us
  local copies, waits for them, and re-layouts: 99.7 us -> 37 us
  blocking collectives: 43.1 us -> 0 us
  matrix products: 124 us -> 97.1 us
  waiting for transfers between devices: 52.7 us -> 39.5 us
    another operation x33 -> x41, other arithmetic: 259 us -> 188 us  [the longest x24 99.4 us: on_device(): diagonal = jnp.linalg.cholesky(panel[:block])]
    all_gather x2 -> x0, blocking collectives: 43.1 us -> none  [the longest x1 23.6 us: on_device(): all_block_cols = lax.all_gather(block_cols, 'row', axis=0, tiled=True)]
    another operation x29 -> x8, matrix products: 44.9 us -> 2.28 us  [on_device(): jax.scipy.linalg.solve_triangular(diagonal, jnp.eye(block, dtype=jnp.floa...]
    another operation x35 -> x4, local copies, waits for them, and re-layouts: 31.6 us -> 2.05 us  [the longest x3 2.05 us: invert_lower(): jnp.stack([factor[(2 * q + 1) * size:(2 * q + 2) * size, 2 * q * size:(2...]
    reduce_sum x1 -> x2, other arithmetic: 12.2 us -> 36.9 us  [assemble_t(): dense = jnp.where(hit, flipped, 0.0).sum(axis=0)]
    select_n x3 -> x0, other arithmetic: 22.1 us -> none  [the longest x2 22 us: on_device(): jnp.take(scaled_blocks, picks, axis=0)]
    dot_general x2 -> x3, matrix products: 7.46 us -> 27.6 us  [mdot(): jnp.dot(left, right, precision=HIGHEST, preferred_element_type=jnp.float32)]
    dot_general x1 -> x6, matrix products: 25.5 us -> 6.05 us  [the longest x3 3.14 us: invert_lower(): corner = jnp.einsum('qij,qjk->qik', second, coupling, precision=HIGHEST)]
  transfers between devices with their start and end apart: 2 -> 5, of which waited for: 1 -> 1; matrix products, arithmetic and copies ran while one was open for 76% -> 69% of each run, Pallas kernels for 0% -> 0%
where the time goes in v2:
time: 430 us; the launch traced here: 424 us
  other arithmetic  234 us (54%)
  matrix products  97.1 us (23%)
  waiting for transfers between devices  39.5 us (9%)
  local copies, waits for them, and re-layouts  37 us (9%)
  between operations  15.5 us (4%)
    another operation x24, other arithmetic, on_device(): diagonal = jnp.linalg.cholesky(panel[:block])  99.4 us
    another operation x16, other arithmetic, on_device(): jax.scipy.linalg.solve_triangular(diagonal, jnp.eye(block, dtype=jnp.floa...  88.7 us
    dot_general x28, matrix products, tdot(): lax.dot_general(left, right, (((1,), (1,)), ((), ())), precision=HIGHEST,...  61.2 us
    all_gather x4, waiting for transfers between devices, on_device(): lax.all_gather(carried_block[:, c * rows:(c + 1) * rows], 'row', axis=0,...  39.4 us
    reduce_sum x2, other arithmetic, assemble_t(): dense = jnp.where(hit, flipped, 0.0).sum(axis=0)  36.9 us
    dot_general x3, matrix products, mdot(): jnp.dot(left, right, precision=HIGHEST, preferred_element_type=jnp.float32)  27.6 us
    unnamed x81, local copies, waits for them, and re-layouts  12.3 us
  transfers between devices with their start and end apart: 5, of which 1 were waited for; matrix products, arithmetic and copies ran while one was open for 69% of the time, Pallas kernels for 0%

profile of v2, /device:TPU:0, one launch (start us, length us, event | category | flops | bytes accessed | tf_op | source)
XLA Modules:
  0.0 423.6 jit_solution(9663917186038638882)
XLA Ops:
  7.2 1.3 fusion.157
  12.4 0.8 fusion.59
  14.4 6.8 %select_reduce_fusion.1 = f32[128,32,256]{2,1,0:T(8,128)} fusion(f32[8,32,256]{2,1,0:T(8,128)S(1)} %bitcast.200, pred[8,128,256]{2,1,0:T(8,128)(4,1)S(1)} %iota_compare_fusion.4), kind=kLoop, calls=%fused_computation.1 | loop fusion | flops 15728640 | bytes 4718592 | tf_op jit(solution)/shard_map/reduce_sum | solution.py:29
  21.2 6.1 %copy.185 = f32[4096,256]{0,1:T(8,128)} copy(f32[4096,256]{1,0:T(8,128)} %bitcast.193) | data formatting | bytes 8388608 | tf_op jit(solution)/shard_map/reshape | solution.py:30
  27.4 39.3 %all-gather.7.cloned.1.call-done = f32[4096,256]{0,1:T(8,128)} async-done(((f32[256,256]{0,1:T(8,128)}), f32[4096,256]{0,1:T(8,128)}) %all-gather.7.cloned.1.call-update) | async-done | bytes 4194320 | tf_op jit(solution)/shard_map/all_gather | solution.py:87
  67.6 0.9 fusion.136
  68.5 11.7 %cholesky.134 = f32[128,128]{1,0:T(8,128)S(1)} custom-call(f32[128,128]{1,0:T(8,128)S(1)} %fusion.136), custom_call_target="Cholesky" | custom-call | tf_op jit(solution)/shard_map/jit(cholesky)/cholesky | solution.py:99
  80.9 1.3 select_bitcast_fusion.7
  82.2 9.8 %custom-call.12 = f32[1,128,128]{1,2,0:T(8,128)S(1)} custom-call(f32[1,128,128]{2,1,0:T(8,128)S(1)} %get-tuple-element.22), custom_call_target="InvertDiagBlocksLowerTriangular" | custom-call | tf_op jit(solution)/shard_map/jit(_solve_triangular)/triangular_solve | solution.py:100
  92.3 1.5 fusion.51
  94.1 1.6 convolution_subtract_fusion.1
  95.8 11.7 %cholesky.145 = f32[128,128]{1,0:T(8,128)S(1)} custom-call(f32[128,128]{1,0:T(8,128)S(1)} %fusion.134), custom_call_target="Cholesky" | custom-call | tf_op jit(solution)/shard_map/jit(cholesky)/cholesky | solution.py:99
  108.2 1.3 select_bitcast_fusion.6
  109.4 9.9 %custom-call.13 = f32[1,128,128]{1,2,0:T(8,128)S(1)} custom-call(f32[1,128,128]{2,1,0:T(8,128)S(1)} %get-tuple-element.20), custom_call_target="InvertDiagBlocksLowerTriangular" | custom-call | tf_op jit(solution)/shard_map/jit(_solve_triangular)/triangular_solve | solution.py:100
  122.7 1.9 convolution_subtract_fusion.2
  124.7 11.7 %cholesky.156 = f32[128,128]{1,0:T(8,128)S(1)} custom-call(f32[128,128]{1,0:T(8,128)S(1)} %fusion.132), custom_call_target="Cholesky" | custom-call | tf_op jit(solution)/shard_map/jit(cholesky)/cholesky | solution.py:99
  137.1 1.3 select_bitcast_fusion.5
  138.4 9.8 %custom-call.14 = f32[1,128,128]{1,2,0:T(8,128)S(1)} custom-call(f32[1,128,128]{2,1,0:T(8,128)S(1)} %get-tuple-element.18), custom_call_target="InvertDiagBlocksLowerTriangular" | custom-call | tf_op jit(solution)/shard_map/jit(_solve_triangular)/triangular_solve | solution.py:100
  149.2 2.2 convolution_subtract_fusion.3
  151.5 11.9 %cholesky.167 = f32[128,128]{1,0:T(8,128)S(1)} custom-call(f32[128,128]{1,0:T(8,128)S(1)} %fusion.130), custom_call_target="Cholesky" | custom-call | tf_op jit(solution)/shard_map/jit(cholesky)/cholesky | solution.py:99
  164.1 1.3 select_bitcast_fusion.4
  165.4 9.8 %custom-call.15 = f32[1,128,128]{1,2,0:T(8,128)S(1)} custom-call(f32[1,128,128]{2,1,0:T(8,128)S(1)} %get-tuple-element.16), custom_call_target="InvertDiagBlocksLowerTriangular" | custom-call | tf_op jit(solution)/shard_map/jit(_solve_triangular)/triangular_solve | solution.py:100
  176.1 2.2 convolution_subtract_fusion.4
  178.4 11.7 %cholesky.178 = f32[128,128]{1,0:T(8,128)S(1)} custom-call(f32[128,128]{1,0:T(8,128)S(1)} %fusion.128), custom_call_target="Cholesky" | custom-call | tf_op jit(solution)/shard_map/jit(cholesky)/cholesky | solution.py:99
  191.5 10.2 %custom-call.16 = f32[1,128,128]{1,2,0:T(8,128)S(1)} custom-call(f32[1,128,128]{2,1,0:T(8,128)S(1)} %get-tuple-element.14), custom_call_target="InvertDiagBlocksLowerTriangular" | custom-call | tf_op jit(solution)/shard_map/jit(_solve_triangular)/triangular_solve | solution.py:100
  208.0 1.2 constant_dynamic-update-slice_fusion
  209.2 2.4 convolution_subtract_fusion.5
  211.7 11.7 %cholesky.189 = f32[128,128]{1,0:T(8,128)S(1)} custom-call(f32[128,128]{1,0:T(8,128)S(1)} %fusion.126), custom_call_target="Cholesky" | custom-call | tf_op jit(solution)/shard_map/jit(cholesky)/cholesky | solution.py:99
  224.1 1.3 select_bitcast_fusion.2
  225.4 9.8 %custom-call.17 = f32[1,128,128]{1,2,0:T(8,128)S(1)} custom-call(f32[1,128,128]{2,1,0:T(8,128)S(1)} %get-tuple-element.12), custom_call_target="InvertDiagBlocksLowerTriangular" | custom-call | tf_op jit(solution)/shard_map/jit(_solve_triangular)/triangular_solve | solution.py:100
  236.0 1.8 convolution_subtract_fusion.6
  238.0 11.9 %cholesky.200 = f32[128,128]{1,0:T(8,128)S(1)} custom-call(f32[128,128]{1,0:T(8,128)S(1)} %fusion.124), custom_call_target="Cholesky" | custom-call | tf_op jit(solution)/shard_map/jit(cholesky)/cholesky | solution.py:99
  250.5 1.3 select_bitcast_fusion.1
  251.8 9.8 %custom-call.18 = f32[1,128,128]{1,2,0:T(8,128)S(1)} custom-call(f32[1,128,128]{2,1,0:T(8,128)S(1)} %get-tuple-element.10), custom_call_target="InvertDiagBlocksLowerTriangular" | custom-call | tf_op jit(solution)/shard_map/jit(_solve_triangular)/triangular_solve | solution.py:100
  263.2 0.9 constant_dynamic-update-slice_fusion.2
  264.1 1.8 convolution_subtract_fusion.7
  266.0 11.7 %cholesky.211 = f32[128,128]{1,0:T(8,128)S(1)} custom-call(f32[128,128]{1,0:T(8,128)S(1)} %fusion.122), custom_call_target="Cholesky" | custom-call | tf_op jit(solution)/shard_map/jit(cholesky)/cholesky | solution.py:99
  278.4 1.3 select_bitcast_fusion
  279.7 9.8 %custom-call.19 = f32[1,128,128]{1,2,0:T(8,128)S(1)} custom-call(f32[1,128,128]{2,1,0:T(8,128)S(1)} %get-tuple-element.8), custom_call_target="InvertDiagBlocksLowerTriangular" | custom-call | tf_op jit(solution)/shard_map/jit(_solve_triangular)/triangular_solve | solution.py:100
  294.0 1.9 fusion.19
  295.9 1.9 fusion.15
  298.1 3.7 fusion.14
  301.8 4.0 fusion.154
  305.9 3.7 fusion.21
  309.6 3.6 fusion.151
  313.3 3.0 fusion.12
  316.2 3.1 fusion.10
  319.4 3.0 convolution_add_fusion.5
  322.4 3.0 convolution_add_fusion.4
  325.5 3.0 convolution_add_fusion.2
  328.5 3.2 convolution_add_fusion.1
  331.8 3.4 fusion.3
  335.2 3.4 fusion.1
  338.6 2.4 pad_maximum_fusion
  341.0 2.5 pad_maximum_fusion.1
  344.3 1.0 slice_bitcast_fusion.3
  345.3 4.6 %slice.417 = f32[16,256,256]{2,1,0:T(8,128)} slice(f32[16,280,256]{2,1,0:T(8,128)} %bitcast.199), slice={[0:16], [0:256], [0:256]} | slice | bytes 8388608 | tf_op jit(solution)/shard_map/slice | solution.py:80
  350.0 5.9 %copy.215 = f32[4096,256]{0,1:T(8,128)} copy(f32[4096,256]{1,0:T(8,128)} %bitcast.192) | data formatting | bytes 8388608 | tf_op jit(solution)/shard_map/reshape | solution.py:80
  356.4 1.6 iota_compare_fusion.1
  357.9 4.7 %fusion.117 = f32[16,1024]{1,0:T(8,128)S(1)} fusion(f32[16,4096]{1,0:T(8,128)S(1)} %bitcast.202, f32[1,512,512]{2,1,0:T(8,128)} %copy-done.12, f32[1,512,512]{2,1,0:T(8,128)} %copy-done.11, f32[1,512,512]{2,1,0:T(8,128)} %copy-done.9), kind=kOutput, calls=%fused_computation.199 | convolution fusion | flops 205520896 | bytes 3276800 | tf_op jit(solution)/shard_map/dot_general | solution.py:16
  362.6 1.6 fusion.17
  365.0 1.5 convolution_subtract_fusion.8
  366.5 30.1 %select_reduce_fusion = f32[32,32,4096]{2,1,0:T(8,128)} fusion(f32[8,32,4096]{2,1,0:T(8,128)} %bitcast.194, pred[8,32,4096]{2,1,0:T(8,128)(4,1)} %iota_compare_fusion.1), kind=kLoop, calls=%fused_computation | loop fusion | flops 62914560 | bytes 22020096 | tf_op jit(solution)/shard_map/reduce_sum | solution.py:29
  396.6 19.9 %convolution_subtract_fusion = f32[256,4096]{1,0:T(8,128)} fusion(f32[256,4096]{1,0:T(8,128)} %param.13, f32[256,1024]{1,0:T(8,128)S(1)} %fusion.151, f32[1024,4096]{1,0:T(8,128)} %bitcast.181), kind=kOutput, calls=%fused_computation.2 | convolution fusion | flops 12885950464 | bytes 26214400 | tf_op jit(solution)/shard_map/dot_general | solution.py:12
  (195 shorter events, 33.6 us)
Async XLA Ops:
  7.2 5.1 %copy-start.29 = (s32[8,8]{1,0:T(8,128)S(1)}, s32[8,8]{1,0:T(8,128)}, u32[]{:S(2)}) copy-start(s32[8,8]{1,0:T(8,128)} %param.12) | copy-start | bytes 772
  7.2 5.2 %copy-start.26 = (f32[16,256]{1,0:T(8,128)S(1)}, f32[16,256]{1,0:T(8,128)}, u32[]{:S(2)}) copy-start(f32[16,256]{1,0:T(8,128)} %param.14) | copy-start | bytes 49156
  7.2 5.2 %copy-start.10 = (f32[256,256]{1,0:T(8,128)S(1)}, f32[256,256]{1,0:T(8,128)}, u32[]{:S(2)}) copy-start(f32[256,256]{1,0:T(8,128)} %param.11) | copy-start | bytes 786436
  7.2 59.5 %all-gather.7.cloned.1.call-start = ((), (), s32[]{:S(2)}) async-start(), calls=%async_computation | async-start | bytes 4456448 | tf_op jit(solution)/shard_map/all_gather | solution.py:87
  9.4 113.2 %all-gather.9.cloned.1.call-start = ((), (), s32[]{:S(2)}) async-start(), calls=%async_computation.1 | async-start | bytes 4456448 | tf_op jit(solution)/shard_map/all_gather | solution.py:87
  10.4 165.7 %all-gather.11.cloned.1.call-start = ((), (), s32[]{:S(2)}) async-start(), calls=%async_computation.2 | async-start | bytes 4456448 | tf_op jit(solution)/shard_map/all_gather | solution.py:87
  11.3 224.7 %all-gather.13.cloned.1.call-start = ((), (), s32[]{:S(2)}) async-start(), calls=%async_computation.3 | async-start | bytes 4456448 | tf_op jit(solution)/shard_map/all_gather | solution.py:87
  12.2 331.3 %all-gather.15.cloned.1.call-start = ((), (), s32[]{:S(2)}) async-start(), calls=%async_computation.4 | async-start | bytes 4874240 | tf_op jit(solution)/shard_map/all_gather | solution.py:78
  205.6 29.6 %copy-start.8 = (f32[256,768]{1,0:T(8,128)S(1)}, f32[256,768]{1,0:T(8,128)}, u32[]{:S(2)}) copy-start(f32[256,768]{1,0:T(8,128)} %slice_dynamic-update-slice_fusion.5) | copy-start | bytes 2359300
  209.1 80.7 %copy-start.13 = (f32[128,128]{1,0:T(8,128)S(1)}, f32[128,128]{1,0:T(8,128)}, u32[]{:S(2)}) copy-start(f32[128,128]{1,0:T(8,128)} %get-tuple-element.23) | copy-start | bytes 196612
  211.7 78.2 %copy-start.14 = (f32[128,128]{1,0:T(8,128)S(1)}, f32[128,128]{1,0:T(8,128)}, u32[]{:S(2)}) copy-start(f32[128,128]{1,0:T(8,128)} %get-tuple-element.21) | copy-start | bytes 196612
  235.9 54.2 %copy-start.17 = (f32[128,128]{1,0:T(8,128)S(1)}, f32[128,128]{1,0:T(8,128)}, u32[]{:S(2)}) copy-start(f32[128,128]{1,0:T(8,128)} %get-tuple-element.19) | copy-start | bytes 196612
  237.8 52.4 %copy-start.19 = (f32[128,128]{1,0:T(8,128)S(1)}, f32[128,128]{1,0:T(8,128)}, u32[]{:S(2)}) copy-start(f32[128,128]{1,0:T(8,128)} %get-tuple-element.17) | copy-start | bytes 196612
  289.9 0.8 copy-start.15
  290.0 0.8 copy-start.16
  290.0 0.9 copy-start.21
  290.0 0.9 copy-start.28
  290.1 1.0 copy-start.23
  290.1 1.0 copy-start.24
  290.1 1.0 copy-start.25
  290.2 1.5 copy-start.22
  292.3 1.7 copy-start.18
  292.3 1.7 copy-start.20
  295.9 2.2 copy-start.5
  297.7 11.8 %copy-start.9 = (f32[1,512,512]{2,1,0:T(8,128)}, f32[1,512,512]{2,1,0:T(8,128)S(1)}, u32[]{:S(2)}) copy-start(f32[1,512,512]{2,1,0:T(8,128)S(1)} %fusion.15) | copy-start | bytes 3145732
  297.9 11.7 %copy-start.11 = (f32[1,512,512]{2,1,0:T(8,128)}, f32[1,512,512]{2,1,0:T(8,128)S(1)}, u32[]{:S(2)}) copy-start(f32[1,512,512]{2,1,0:T(8,128)S(1)} %get-tuple-element.28) | copy-start | bytes 3145732
  297.9 11.7 %copy-start.12 = (f32[1,512,512]{2,1,0:T(8,128)}, f32[1,512,512]{2,1,0:T(8,128)S(1)}, u32[]{:S(2)}) copy-start(f32[1,512,512]{2,1,0:T(8,128)S(1)} %get-tuple-element.29) | copy-start | bytes 3145732
  301.8 4.1 copy-start.1
  309.6 31.4 %copy-start.6 = (f32[256,1024]{1,0:T(8,128)}, f32[256,1024]{1,0:T(8,128)S(1)}, u32[]{:S(2)}) copy-start(f32[256,1024]{1,0:T(8,128)S(1)} %fusion.21) | copy-start | bytes 3145732
  309.6 3.6 copy-start
  316.2 3.2 copy-start.2
  319.4 3.0 copy-start.3
  328.5 3.3 copy-start.4
  357.9 6.3 %copy-start.30 = (f32[16,16]{1,0:T(8,128)S(1)}, f32[16,16]{1,0:T(8,128)}, u32[]{:S(2)}) copy-start(f32[16,16]{1,0:T(8,128)} %param.16) | copy-start | bytes 3076
  357.9 7.1 %copy-start.7 = (f32[256,1024]{1,0:T(8,128)S(1)}, f32[256,1024]{1,0:T(8,128)}, u32[]{:S(2)}) copy-start(f32[256,1024]{1,0:T(8,128)} %copy-done.6) | copy-start | bytes 3145732
  357.9 7.1 %copy-start.27 = (f32[16,256]{1,0:T(8,128)S(1)}, f32[16,256]{1,0:T(8,128)}, u32[]{:S(2)}) copy-start(f32[16,256]{1,0:T(8,128)} %param.15) | copy-start | bytes 49156
Sparse Core Ops, SparseCore 0:
  10.8 55.9 all-gather.6
  68.9 52.6 all-gather.8
  123.7 50.9 all-gather.10
  176.7 51.6 all-gather.12
  230.5 52.0 all-gather.14

commit v3 on v2

--- a/solution.py
+++ b/solution.py
@@ -6,15 +6,16 @@
 PANELS = 4
 BLOCK = 128
 HIGHEST = lax.Precision.HIGHEST
+HIGH = lax.Precision.HIGH
 
 
-def mdot(left, right):
-    return jnp.dot(left, right, precision=HIGHEST, preferred_element_type=jnp.float32)
+def mdot(left, right, precision=HIGHEST):
+    return jnp.dot(left, right, precision=precision, preferred_element_type=jnp.float32)
 
 
-def tdot(left, right):
+def tdot(left, right, precision=HIGHEST):
     return lax.dot_general(
-        left, right, (((1,), (1,)), ((), ())), precision=HIGHEST, preferred_element_type=jnp.float32
+        left, right, (((1,), (1,)), ((), ())), precision=precision, preferred_element_type=jnp.float32
     )
 
 
@@ -83,15 +84,24 @@
     all_block_cols = gathered[:, value_rows + fixed_count, :cols_count]
     all_block_cols = jnp.round(all_block_cols).astype(jnp.int32).reshape(-1, nonzero)
 
+    blocks = factored // block
+    widths = [1]
+    while sum(widths) < blocks:
+        widths.append(min(sum(widths), blocks - sum(widths)))
+    bounds = [0]
+    for count in widths:
+        bounds.append(bounds[-1] + count * block)
     chunks = [
-        lax.all_gather(carried_block[:, c * rows:(c + 1) * rows], "row", axis=0, tiled=True)
-        for c in range(PANELS)
+        lax.all_gather(carried_block[:, lo:hi], "row", axis=0, tiled=True)
+        for lo, hi in zip(bounds[:-1], bounds[1:])
     ]
+    chunk_of = [c for c, count in enumerate(widths) for _ in range(count)]
 
     columns = []
     block_inverses = []
     for k in range(factored // block):
-        chunk, offset = divmod(k * block, rows)
+        chunk = chunk_of[k]
+        offset = k * block - bounds[chunk]
         panel = chunks[chunk][k * block:factored, offset:offset + block]
         if k:
             done = jnp.concatenate([col[k * block:] for col in columns], axis=1)
@@ -111,27 +121,27 @@
 
     def minus_below(scaled):
         total = None
-        for c in range(PANELS):
-            part = tdot(scaled[:, c * rows:(c + 1) * rows], chunks[c][factored:])
+        for c, (lo, hi) in enumerate(zip(bounds[:-1], bounds[1:])):
+            part = tdot(scaled[:, lo:hi], chunks[c][factored:], HIGH)
             total = part if total is None else total + part
         return total
 
     own_cols = carried_block[:, :factored]
-    lower = tdot(own_cols, head_inverse)
+    lower = tdot(own_cols, head_inverse, HIGH)
     lower = jnp.where(is_top, lax.dynamic_slice_in_dim(head_factor, top_at, rows, 0), lower)
-    lower_scaled = mdot(lower, head_inverse)
+    lower_scaled = mdot(lower, head_inverse, HIGH)
     state_rest = carried_block[:, factored:] - minus_below(lower_scaled)
     state_rest = jnp.where(is_top, 0.0, state_rest)
     factor_state = jnp.concatenate([lower, state_rest], axis=1)
 
     coupled = assemble_t(block_cols, coupling_values, size // width).T
-    coupled_panel = tdot(coupled[:, :factored], head_inverse)
-    coupled_scaled = mdot(coupled_panel, head_inverse)
+    coupled_panel = tdot(coupled[:, :factored], head_inverse, HIGH)
+    coupled_scaled = mdot(coupled_panel, head_inverse, HIGH)
     coupled_rest = coupled[:, factored:] - minus_below(coupled_scaled)
     coupling_factor = jnp.concatenate([coupled_panel, coupled_rest], axis=1)
 
     coupling_head_t = assemble_t(all_block_cols, all_values, factored // width)
-    carried_next = next_block - mdot(coupled_scaled, coupling_head_t)
+    carried_next = next_block - mdot(coupled_scaled, coupling_head_t, HIGH)
 
     fixed_panel = tdot(all_fixed[:, :factored], head_inverse)
     own_fixed_panel = lax.dynamic_slice_in_dim(fixed_panel, top_at, rows, 1)

time: 430 us -> 471 us (1.095)
  waiting for transfers between devices: 39.5 us -> 91.9 us
  matrix products: 97.1 us -> 79.3 us
    all_gather x4, waiting for transfers between devices: 39.4 us -> 91.8 us  [on_device(): lax.all_gather(carried_block[:, lo:hi], 'row', axis=0, tiled=True)]
    dot_general x31, matrix products: 88.8 us -> 70.2 us  [the longest x28 52.9 us: tdot(): lax.dot_general(left, right, (((1,), (1,)), ((), ())), precision=precisio...]
    unnamed x81 -> x105, local copies, waits for them, and re-layouts: 12.3 us -> 14.7 us
  transfers between devices with their start and end apart: 5 -> 5, of which waited for: 1 -> 4; matrix products, arithmetic and copies ran while one was open for 69% -> 39% of each run, Pallas kernels for 0% -> 0%
where the time goes in v3:
time: 471 us; the launch traced here: 464 us
  other arithmetic  238 us (51%)
  waiting for transfers between devices  91.9 us (20%)
  matrix products  79.3 us (17%)
  local copies, waits for them, and re-layouts  39 us (8%)
  between operations  15.6 us (3%)
    another operation x24, other arithmetic, on_device(): diagonal = jnp.linalg.cholesky(panel[:block])  100 us
    all_gather x4, waiting for transfers between devices, on_device(): lax.all_gather(carried_block[:, lo:hi], 'row', axis=0, tiled=True)  91.8 us
    another operation x16, other arithmetic, on_device(): jax.scipy.linalg.solve_triangular(diagonal, jnp.eye(block, dtype=jnp.floa...  85.2 us
    dot_general x28, matrix products, tdot(): lax.dot_general(left, right, (((1,), (1,)), ((), ())), precision=precisio...  52.9 us
    reduce_sum x2, other arithmetic, assemble_t(): dense = jnp.where(hit, flipped, 0.0).sum(axis=0)  37 us
    dot_general x3, matrix products, mdot(): jnp.dot(left, right, precision=precision, preferred_element_type=jnp.floa...  17.3 us
    unnamed x105, local copies, waits for them, and re-layouts  14.7 us
  transfers between devices with their start and end apart: 5, of which 4 were waited for; matrix products, arithmetic and copies ran while one was open for 39% of the time, Pallas kernels for 0%

profile of v3, /device:TPU:0, one launch (start us, length us, event | category | flops | bytes accessed | tf_op | source)
XLA Modules:
  0.0 464.3 jit_solution(15943829978291766269)
XLA Ops:
  7.2 1.1 fusion.171
  12.7 1.8 fusion.75
  14.6 1.0 copy.211
  16.2 6.8 %select_reduce_fusion.1 = f32[128,32,256]{2,1,0:T(8,128)} fusion(f32[8,32,256]{2,1,0:T(8,128)S(1)} %bitcast.204, pred[8,128,256]{2,1,0:T(8,128)(4,1)S(1)} %iota_compare_fusion.4), kind=kLoop, calls=%fused_computation.1 | loop fusion | flops 15728640 | bytes 4718592 | tf_op jit(solution)/shard_map/reduce_sum | solution.py:30
  23.0 5.8 %copy.185 = f32[4096,256]{0,1:T(8,128)} copy(f32[4096,256]{1,0:T(8,128)} %bitcast.197) | data formatting | bytes 8388608 | tf_op jit(solution)/shard_map/reshape | solution.py:31
  28.8 25.3 %all-gather.7.cloned.1.call-done = f32[4096,128]{0,1:T(8,128)} async-done(((f32[256,128]{0,1:T(8,128)}), f32[4096,128]{0,1:T(8,128)}) %all-gather.7.cloned.1.call-update) | async-done | bytes 2097168 | tf_op jit(solution)/shard_map/all_gather | solution.py:95
  55.9 11.7 %cholesky.134 = f32[128,128]{1,0:T(8,128)S(1)} custom-call(f32[128,128]{1,0:T(8,128)S(1)} %fusion.150), custom_call_target="Cholesky" | custom-call | tf_op jit(solution)/shard_map/jit(cholesky)/cholesky | solution.py:109
  69.0 9.8 %custom-call.12 = f32[1,128,128]{1,2,0:T(8,128)S(1)} custom-call(f32[1,128,128]{2,1,0:T(8,128)S(1)} %get-tuple-element.22), custom_call_target="InvertDiagBlocksLowerTriangular" | custom-call | tf_op jit(solution)/shard_map/jit(_solve_triangular)/triangular_solve | solution.py:110
  79.1 1.5 fusion.67
  80.9 15.9 %all-gather.9.cloned.1.call-done = f32[4096,128]{0,1:T(8,128)} async-done(((f32[256,128]{0,1:T(8,128)}), f32[4096,128]{0,1:T(8,128)}) %all-gather.9.cloned.1.call-update) | async-done | bytes 2097168 | tf_op jit(solution)/shard_map/all_gather | solution.py:95
  96.8 1.6 convolution_subtract_fusion.1
  98.4 11.7 %cholesky.145 = f32[128,128]{1,0:T(8,128)S(1)} custom-call(f32[128,128]{1,0:T(8,128)S(1)} %fusion.148), custom_call_target="Cholesky" | custom-call | tf_op jit(solution)/shard_map/jit(cholesky)/cholesky | solution.py:109
  111.5 10.0 %custom-call.13 = f32[1,128,128]{1,2,0:T(8,128)S(1)} custom-call(f32[1,128,128]{2,1,0:T(8,128)S(1)} %get-tuple-element.20), custom_call_target="InvertDiagBlocksLowerTriangular" | custom-call | tf_op jit(solution)/shard_map/jit(_solve_triangular)/triangular_solve | solution.py:110
  127.8 23.6 %all-gather.11.cloned.1.call-done = f32[4096,256]{0,1:T(8,128)} async-done(((f32[256,256]{0,1:T(8,128)}), f32[4096,256]{0,1:T(8,128)}) %all-gather.11.cloned.1.call-update) | async-done | bytes 4194320 | tf_op jit(solution)/shard_map/all_gather | solution.py:95
  151.4 1.9 convolution_subtract_fusion.2
  155.0 11.7 %cholesky.156 = f32[128,128]{1,0:T(8,128)S(1)} custom-call(f32[128,128]{1,0:T(8,128)S(1)} %fusion.146), custom_call_target="Cholesky" | custom-call | tf_op jit(solution)/shard_map/jit(cholesky)/cholesky | solution.py:109
  168.1 9.8 %custom-call.14 = f32[1,128,128]{1,2,0:T(8,128)S(1)} custom-call(f32[1,128,128]{2,1,0:T(8,128)S(1)} %get-tuple-element.18), custom_call_target="InvertDiagBlocksLowerTriangular" | custom-call | tf_op jit(solution)/shard_map/jit(_solve_triangular)/triangular_solve | solution.py:110
  178.2 1.7 fusion.73
  180.0 2.3 convolution_subtract_fusion.3
  182.4 12.1 %cholesky.167 = f32[128,128]{1,0:T(8,128)S(1)} custom-call(f32[128,128]{1,0:T(8,128)S(1)} %fusion.144), custom_call_target="Cholesky" | custom-call | tf_op jit(solution)/shard_map/jit(cholesky)/cholesky | solution.py:109
  195.8 9.8 %custom-call.15 = f32[1,128,128]{1,2,0:T(8,128)S(1)} custom-call(f32[1,128,128]{2,1,0:T(8,128)S(1)} %get-tuple-element.16), custom_call_target="InvertDiagBlocksLowerTriangular" | custom-call | tf_op jit(solution)/shard_map/jit(_solve_triangular)/triangular_solve | solution.py:110
  212.6 4.8 %slice.417 = f32[16,256,256]{2,1,0:T(8,128)} slice(f32[16,280,256]{2,1,0:T(8,128)} %bitcast.202), slice={[0:16], [0:256], [0:256]} | slice | bytes 8388608 | tf_op jit(solution)/shard_map/slice | solution.py:81
  217.6 5.7 %copy.215 = f32[4096,256]{0,1:T(8,128)} copy(f32[4096,256]{1,0:T(8,128)} %bitcast.196) | data formatting | bytes 8388608 | tf_op jit(solution)/shard_map/reshape | solution.py:81
  223.2 1.0 slice_bitcast_fusion.3
  226.0 30.2 %select_reduce_fusion = f32[32,32,4096]{2,1,0:T(8,128)} fusion(f32[8,32,4096]{2,1,0:T(8,128)} %bitcast.198, pred[8,32,4096]{2,1,0:T(8,128)(4,1)S(1)} %iota_compare_fusion.1), kind=kLoop, calls=%fused_computation | loop fusion | flops 62914560 | bytes 22020096 | tf_op jit(solution)/shard_map/reduce_sum | solution.py:30
  256.2 27.0 %all-gather.13.cloned.1.call-done = f32[4096,512]{0,1:T(8,128)} async-done(((f32[256,512]{0,1:T(8,128)}), f32[4096,512]{0,1:T(8,128)}) %all-gather.13.cloned.1.call-update) | async-done | bytes 8388624 | tf_op jit(solution)/shard_map/all_gather | solution.py:95
  283.2 2.1 convolution_subtract_fusion.4
  285.5 11.7 %cholesky.178 = f32[128,128]{1,0:T(8,128)S(1)} custom-call(f32[128,128]{1,0:T(8,128)S(1)} %fusion.142), custom_call_target="Cholesky" | custom-call | tf_op jit(solution)/shard_map/jit(cholesky)/cholesky | solution.py:109
  298.6 9.8 %custom-call.16 = f32[1,128,128]{1,2,0:T(8,128)S(1)} custom-call(f32[1,128,128]{2,1,0:T(8,128)S(1)} %get-tuple-element.14), custom_call_target="InvertDiagBlocksLowerTriangular" | custom-call | tf_op jit(solution)/shard_map/jit(_solve_triangular)/triangular_solve | solution.py:110
  308.7 1.2 constant_dynamic-update-slice_fusion
  309.9 2.4 convolution_subtract_fusion.5
  312.4 11.9 %cholesky.189 = f32[128,128]{1,0:T(8,128)S(1)} custom-call(f32[128,128]{1,0:T(8,128)S(1)} %fusion.140), custom_call_target="Cholesky" | custom-call | tf_op jit(solution)/shard_map/jit(cholesky)/cholesky | solution.py:109
  325.7 9.8 %custom-call.17 = f32[1,128,128]{1,2,0:T(8,128)S(1)} custom-call(f32[1,128,128]{2,1,0:T(8,128)S(1)} %get-tuple-element.12), custom_call_target="InvertDiagBlocksLowerTriangular" | custom-call | tf_op jit(solution)/shard_map/jit(_solve_triangular)/triangular_solve | solution.py:110
  336.5 1.1 constant_dynamic-update-slice_fusion.1
  337.5 2.2 convolution_subtract_fusion.6
  339.9 11.7 %cholesky.200 = f32[128,128]{1,0:T(8,128)S(1)} custom-call(f32[128,128]{1,0:T(8,128)S(1)} %fusion.138), custom_call_target="Cholesky" | custom-call | tf_op jit(solution)/shard_map/jit(cholesky)/cholesky | solution.py:109
  352.2 1.3 select_bitcast_fusion.1
  353.5 9.8 %custom-call.18 = f32[1,128,128]{1,2,0:T(8,128)S(1)} custom-call(f32[1,128,128]{2,1,0:T(8,128)S(1)} %get-tuple-element.10), custom_call_target="InvertDiagBlocksLowerTriangular" | custom-call | tf_op jit(solution)/shard_map/jit(_solve_triangular)/triangular_solve | solution.py:110
  365.2 1.4 convolution_subtract_fusion.7
  366.8 12.1 %cholesky.211 = f32[128,128]{1,0:T(8,128)S(1)} custom-call(f32[128,128]{1,0:T(8,128)S(1)} %fusion.136), custom_call_target="Cholesky" | custom-call | tf_op jit(solution)/shard_map/jit(cholesky)/cholesky | solution.py:109
  379.6 1.3 select_bitcast_fusion
  380.8 9.8 %custom-call.19 = f32[1,128,128]{1,2,0:T(8,128)S(1)} custom-call(f32[1,128,128]{2,1,0:T(8,128)S(1)} %get-tuple-element.8), custom_call_target="InvertDiagBlocksLowerTriangular" | custom-call | tf_op jit(solution)/shard_map/jit(_solve_triangular)/triangular_solve | solution.py:110
  391.0 1.3 fusion.92
  394.7 1.9 fusion.33
  396.9 1.9 fusion.29
  399.7 4.0 fusion.131
  403.6 1.9 fusion.28
  405.6 2.0 fusion.168
  407.7 1.5 fusion.31
  410.1 1.5 fusion.26
  411.6 1.6 convolution_add_fusion.3
  413.2 1.9 convolution_add_fusion.2
  415.6 3.9 fusion.17
  419.5 2.4 pad_maximum_fusion
  421.9 1.3 copy-done.2
  423.2 2.0 fusion.35
  425.2 3.7 fusion.165
  428.9 1.5 convolution_subtract_fusion.8
  430.4 1.5 fusion.24
  431.9 1.6 convolution_add_fusion.1
  433.6 1.9 convolution_add_fusion
  435.5 5.6 %fusion.14 = f32[256,3072]{1,0:T(8,128)} fusion(f32[256,3072]{1,0:T(8,128)S(1)} %convolution_add_fusion, f32[4096,512]{0,1:T(8,128)S(1)} %bitcast.185, f32[256,4096]{1,0:T(8,128)S(1)} %bitcast.200, f32[256,1024]{1,0:T(8,128)S(1)} %fusion.165), kind=kOutput, calls=%fused_computation.16 | convolution fusion | flops 2417491968 | bytes 16252928 | tf_op jit(solution)/shard_map/dot_general | solution.py:17
  441.0 4.6 pad_maximum_fusion.1
  445.7 11.6 %convolution_subtract_fusion = f32[256,4096]{1,0:T(8,128)} fusion(f32[256,4096]{1,0:T(8,128)} %param.13, f32[256,1024]{1,0:T(8,128)S(1)} %fusion.165, f32[1024,4096]{1,0:T(8,128)S(1)} %bitcast.183), kind=kOutput, calls=%fused_computation.6 | convolution fusion | flops 6443499520 | bytes 26214400 | tf_op jit(solution)/shard_map/dot_general | solution.py:13
  (226 shorter events, 42.5 us)
Async XLA Ops:
  7.2 7.4 %slice-start.8 = ((f32[256,4096]{1,0:T(8,128)}), f32[256,512]{1,0:T(8,128)S(1)}, s32[]{:S(2)}) async-start(f32[256,4096]{1,0:T(8,128)} %param.10), calls=%async_computation.13 | async-start | bytes 1048576 | tf_op jit(solution)/shard_map/slice | solution.py:95
  7.2 8.6 %copy-start.35 = (s32[8,8]{1,0:T(8,128)S(1)}, s32[8,8]{1,0:T(8,128)}, u32[]{:S(2)}) copy-start(s32[8,8]{1,0:T(8,128)} %param.12) | copy-start | bytes 772
  7.2 8.5 %copy-start.13 = (f32[256,256]{1,0:T(8,128)S(1)}, f32[256,256]{1,0:T(8,128)}, u32[]{:S(2)}) copy-start(f32[256,256]{1,0:T(8,128)} %param.11) | copy-start | bytes 786436
  7.2 46.9 %all-gather.7.cloned.1.call-start = ((), (), s32[]{:S(2)}) async-start(), calls=%async_computation | async-start | bytes 2228224 | tf_op jit(solution)/shard_map/all_gather | solution.py:95
  9.1 87.7 %all-gather.9.cloned.1.call-start = ((), (), s32[]{:S(2)}) async-start(), calls=%async_computation.1 | async-start | bytes 2228224 | tf_op jit(solution)/shard_map/all_gather | solution.py:95
  9.9 141.4 %all-gather.11.cloned.1.call-start = ((), (), s32[]{:S(2)}) async-start(), calls=%async_computation.2 | async-start | bytes 4456448 | tf_op jit(solution)/shard_map/all_gather | solution.py:95
  11.8 199.9 %all-gather.15.cloned.1.call-start = ((), (), s32[]{:S(2)}) async-start(), calls=%async_computation.4 | async-start | bytes 4874240 | tf_op jit(solution)/shard_map/all_gather | solution.py:79
  14.6 268.7 %all-gather.13.cloned.1.call-start = ((), (), s32[]{:S(2)}) async-start(), calls=%async_computation.3 | async-start | bytes 8912896 | tf_op jit(solution)/shard_map/all_gather | solution.py:95
  111.5 41.8 %copy-start.15 = (f32[128,128]{1,0:T(8,128)}, f32[128,128]{1,0:T(8,128)S(1)}, u32[]{:S(2)}) copy-start(f32[128,128]{1,0:T(8,128)S(1)} %get-tuple-element.21) | copy-start | bytes 196612
  122.6 30.7 %copy-start = (f32[768,128]{1,0:T(8,128)}, f32[768,128]{1,0:T(8,128)S(1)}, u32[]{:S(2)}) copy-start(f32[768,128]{1,0:T(8,128)S(1)} %fusion.70) | copy-start | bytes 1179652
  123.5 58.7 %copy-start.21 = (f32[128,128]{1,0:T(8,128)}, f32[128,128]{1,0:T(8,128)S(1)}, u32[]{:S(2)}) copy-start(f32[128,128]{1,0:T(8,128)S(1)} %cholesky.135) | copy-start | bytes 196612
  153.3 0.7 copy-start.12
  168.1 40.8 %copy-start.26 = (f32[128,128]{1,0:T(8,128)}, f32[128,128]{1,0:T(8,128)S(1)}, u32[]{:S(2)}) copy-start(f32[128,128]{1,0:T(8,128)S(1)} %get-tuple-element.19) | copy-start | bytes 196612
  179.9 31.1 %copy-start.3 = (f32[640,128]{1,0:T(8,128)}, f32[640,128]{1,0:T(8,128)S(1)}, u32[]{:S(2)}) copy-start(f32[640,128]{1,0:T(8,128)S(1)} %fusion.73) | copy-start | bytes 983044
  195.8 21.6 %copy-start.28 = (f32[128,128]{1,0:T(8,128)}, f32[128,128]{1,0:T(8,128)S(1)}, u32[]{:S(2)}) copy-start(f32[128,128]{1,0:T(8,128)S(1)} %get-tuple-element.17) | copy-start | bytes 196612
  205.7 11.7 %copy-start.24 = (f32[256,128]{1,0:T(8,128)}, f32[256,128]{1,0:T(8,128)S(1)}, u32[]{:S(2)}) copy-start(f32[256,128]{1,0:T(8,128)S(1)} %broadcast_in_dim.83) | copy-start | bytes 393220
  208.9 8.5 %copy-start.10 = (f32[128,896]{1,0:T(8,128)}, f32[128,896]{1,0:T(8,128)S(1)}, u32[]{:S(2)}) copy-start(f32[128,896]{1,0:T(8,128)S(1)} %constant_dynamic-update-slice_fusion.5) | copy-start | bytes 1376260
  226.0 57.2 %slice-start.4 = ((f32[768,128]{1,0:T(8,128)}), f32[512,128]{1,0:T(8,128)S(1)}, s32[]{:S(2)}) async-start(f32[768,128]{1,0:T(8,128)} %copy-done), calls=%async_computation.9 | async-start | bytes 524288 | tf_op jit(solution)/shard_map/slice | solution.py:107
  226.0 57.2 %slice-start.7 = ((f32[640,128]{1,0:T(8,128)}), f32[512,128]{1,0:T(8,128)S(1)}, s32[]{:S(2)}) async-start(f32[640,128]{1,0:T(8,128)} %copy-done.3), calls=%async_computation.12 | async-start | bytes 524288 | tf_op jit(solution)/shard_map/slice | solution.py:107
  285.4 78.0 %copy-start.11 = (f32[128,896]{1,0:T(8,128)S(1)}, f32[128,896]{1,0:T(8,128)}, u32[]{:S(2)}) copy-start(f32[128,896]{1,0:T(8,128)} %copy-done.10) | copy-start | bytes 1376260
  298.6 94.4 %copy-start.17 = (f32[128,128]{1,0:T(8,128)}, f32[128,128]{1,0:T(8,128)S(1)}, u32[]{:S(2)}) copy-start(f32[128,128]{1,0:T(8,128)S(1)} %get-tuple-element.15) | copy-start | bytes 196612
  325.7 67.3 %copy-start.19 = (f32[128,128]{1,0:T(8,128)}, f32[128,128]{1,0:T(8,128)S(1)}, u32[]{:S(2)}) copy-start(f32[128,128]{1,0:T(8,128)S(1)} %get-tuple-element.13) | copy-start | bytes 196612
  366.6 26.3 %copy-start.1 = (f32[768,128]{1,0:T(8,128)S(1)}, f32[768,128]{1,0:T(8,128)}, u32[]{:S(2)}) copy-start(f32[768,128]{1,0:T(8,128)} %copy-done) | copy-start | bytes 1179652
  366.6 26.3 %copy-start.16 = (f32[128,128]{1,0:T(8,128)S(1)}, f32[128,128]{1,0:T(8,128)}, u32[]{:S(2)}) copy-start(f32[128,128]{1,0:T(8,128)} %copy-done.15) | copy-start | bytes 196612
  366.7 26.3 %copy-start.22 = (f32[128,128]{1,0:T(8,128)S(1)}, f32[128,128]{1,0:T(8,128)}, u32[]{:S(2)}) copy-start(f32[128,128]{1,0:T(8,128)} %copy-done.21) | copy-start | bytes 196612
  393.0 1.7 copy-start.4
  393.0 1.7 copy-start.25
  393.0 1.7 copy-start.27
  393.0 1.7 copy-start.29
  396.6 2.1 copy-start.18
  396.6 2.6 copy-start.32
  396.6 2.7 copy-start.20
  396.6 2.7 copy-start.23
  396.6 2.7 copy-start.30
  396.7 2.9 copy-start.31
  396.8 25.1 %copy-start.14 = (f32[1,512,512]{2,1,0:T(8,128)}, f32[1,512,512]{2,1,0:T(8,128)S(1)}, u32[]{:S(2)}) copy-start(f32[1,512,512]{2,1,0:T(8,128)S(1)} %get-tuple-element.27) | copy-start | bytes 3145732
  399.6 4.0 copy-start.8
  405.6 2.1 copy-start.33
  405.6 3.6 copy-start.36
  405.6 4.4 copy-start.6
  407.7 3.9 copy-start.7
  410.1 3.1 copy-start.5
  411.6 3.5 slice-start.5
  413.2 2.4 slice-start.6
  419.5 3.7 copy-start.2
  425.2 3.7 copy-start.9
  425.2 3.7 copy-start.34
  433.6 12.1 %slice-start = ((s8[16777216]{0:T(1024)(128)(4,1)}), s8[4194304]{0:T(1024)(128)(4,1)S(1)}, s32[]{:S(2)}) async-start(s8[16777216]{0:T(1024)(128)(4,1)} %bitcast.181), calls=%async_computation.5 | async-start | bytes 8388608
  433.6 12.1 %slice-start.1 = ((s8[16777216]{0:T(1024)(128)(4,1)}), s8[4194304]{0:T(1024)(128)(4,1)S(1)}, s32[]{:S(2)}) async-start(s8[16777216]{0:T(1024)(128)(4,1)} %bitcast.181), calls=%async_computation.6 | async-start | bytes 8388608
  435.5 10.2 %slice-start.2 = ((s8[16777216]{0:T(1024)(128)(4,1)}), s8[4194304]{0:T(1024)(128)(4,1)S(1)}, s32[]{:S(2)}) async-start(s8[16777216]{0:T(1024)(128)(4,1)} %bitcast.181), calls=%async_computation.7 | async-start | bytes 8388608
  435.5 10.2 %slice-start.3 = ((s8[16777216]{0:T(1024)(128)(4,1)}), s8[4194304]{0:T(1024)(128)(4,1)S(1)}, s32[]{:S(2)}) async-start(s8[16777216]{0:T(1024)(128)(4,1)} %bitcast.181), calls=%async_computation.8 | async-start | bytes 8388608
Sparse Core Ops, SparseCore 0:
  10.2 43.8 all-gather.6
  56.3 40.4 all-gather.8
  99.5 51.8 all-gather.10
  153.5 51.0 all-gather.14
  206.6 76.5 all-gather.12

commit v4 on v3

--- a/solution.py
+++ b/solution.py
@@ -19,11 +19,11 @@
     )
 
 
-def assemble_t(block_cols, values, col_blocks):
+def assemble_t(block_cols, values_t, col_blocks):
     block_rows, nonzero = block_cols.shape
-    width = values.shape[1] // nonzero
+    width = values_t.shape[0] // nonzero
     span = block_rows * width
-    flipped = values.T.reshape(nonzero, 1, width, span)
+    flipped = values_t.reshape(nonzero, 1, width, span)
     spread = jnp.repeat(block_cols.T, width, axis=1)
     columns = jnp.arange(col_blocks, dtype=jnp.int32)
     hit = spread[:, None, None, :] == columns[None, :, None, None]
@@ -72,22 +72,20 @@
     def widen(part):
         return jnp.pad(part, ((0, 0), (0, lanes - part.shape[1])))
 
+    values_t = coupling_values.T
     cols_row = block_cols.reshape(1, cols_count).astype(jnp.float32)
-    packed = jnp.concatenate([widen(coupling_values), widen(fixed_rows), widen(cols_row)], axis=0)
+    packed = jnp.concatenate([widen(fixed_rows), widen(cols_row)], axis=0)
     pad = (-packed.shape[0]) % 8
     packed = jnp.concatenate([packed, jnp.zeros((pad, lanes), jnp.float32)], axis=0)
     gathered = lax.all_gather(packed, "row", axis=0)
     devices = gathered.shape[0]
-    all_values = gathered[:, :value_rows, :value_cols].reshape(devices * value_rows, value_cols)
-    all_fixed = gathered[:, value_rows:value_rows + fixed_count, :fixed_cols].transpose(1, 0, 2)
+    all_fixed = gathered[:, :fixed_count, :fixed_cols].transpose(1, 0, 2)
     all_fixed = all_fixed.reshape(fixed_count, devices * fixed_cols)
-    all_block_cols = gathered[:, value_rows + fixed_count, :cols_count]
+    all_block_cols = gathered[:, fixed_count, :cols_count]
     all_block_cols = jnp.round(all_block_cols).astype(jnp.int32).reshape(-1, nonzero)
 
     blocks = factored // block
-    widths = [1]
-    while sum(widths) < blocks:
-        widths.append(min(sum(widths), blocks - sum(widths)))
+    widths = [rows // block] * PANELS
     bounds = [0]
     for count in widths:
         bounds.append(bounds[-1] + count * block)
@@ -106,7 +104,7 @@
         if k:
             done = jnp.concatenate([col[k * block:] for col in columns], axis=1)
             panel = panel - tdot(done, done[:block])
-        diagonal = jnp.linalg.cholesky(panel[:block])
+        diagonal = jnp.linalg.cholesky(panel[:block], symmetrize_input=False)
         diagonal_inverse = jax.scipy.linalg.solve_triangular(
             diagonal, jnp.eye(block, dtype=jnp.float32), lower=True
         )
@@ -134,13 +132,14 @@
     state_rest = jnp.where(is_top, 0.0, state_rest)
     factor_state = jnp.concatenate([lower, state_rest], axis=1)
 
-    coupled = assemble_t(block_cols, coupling_values, size // width).T
+    coupled = assemble_t(block_cols, values_t, size // width).T
     coupled_panel = tdot(coupled[:, :factored], head_inverse, HIGH)
     coupled_scaled = mdot(coupled_panel, head_inverse, HIGH)
     coupled_rest = coupled[:, factored:] - minus_below(coupled_scaled)
     coupling_factor = jnp.concatenate([coupled_panel, coupled_rest], axis=1)
 
-    coupling_head_t = assemble_t(all_block_cols, all_values, factored // width)
+    all_values_t = lax.all_gather(values_t, "row", axis=1, tiled=True)
+    coupling_head_t = assemble_t(all_block_cols, all_values_t, factored // width)
     carried_next = next_block - mdot(coupled_scaled, coupling_head_t, HIGH)
 
     fixed_panel = tdot(all_fixed[:, :factored], head_inverse)

time: 471 us -> 415 us (0.88)
  waiting for transfers between devices: 91.9 us -> 10.5 us
  blocking collectives: 0 us -> 25 us
  other arithmetic: 238 us -> 248 us
  local copies, waits for them, and re-layouts: 39 us -> 30.1 us
    all_gather x4, waiting for transfers between devices: 91.8 us -> 8.52 us  [on_device(): lax.all_gather(carried_block[:, lo:hi], 'row', axis=0, tiled=True)]
    all_gather x0 -> x1, blocking collectives: none -> 25 us  [on_device(): gathered = lax.all_gather(packed, 'row', axis=0)]
    reshape x1 -> x0, local copies, waits for them, and re-layouts: 5.69 us -> none  [on_device(): gathered[:, :value_rows, :value_cols]]
    another operation x16, other arithmetic: 85.2 us -> 90.9 us  [on_device(): jax.scipy.linalg.solve_triangular(diagonal, jnp.eye(block, dtype=jnp.floa...]
    slice x16 -> x8, local copies, waits for them, and re-layouts: 7.13 us -> 2.13 us  [the longest x7 2.13 us: on_device(): diagonal = jnp.linalg.cholesky(panel[:block], symmetrize_input=False)]
    unnamed x105 -> x75, local copies, waits for them, and re-layouts: 14.7 us -> 14.8 us
  transfers between devices with their start and end apart: 5 -> 5, of which waited for: 4 -> 1; matrix products, arithmetic and copies ran while one was open for 39% -> 75% of each run, Pallas kernels for 0% -> 0%
where the time goes in v4:
time: 415 us; the launch traced here: 408 us
  other arithmetic  248 us (60%)
  matrix products  79 us (19%)
  local copies, waits for them, and re-layouts  30.1 us (7%)
  blocking collectives  25 us (6%)
  between operations  14.8 us (4%)
  waiting for transfers between devices  10.5 us (3%)
    another operation x24, other arithmetic, on_device(): diagonal = jnp.linalg.cholesky(panel[:block], symmetrize_input=False)  103 us
    another operation x16, other arithmetic, on_device(): jax.scipy.linalg.solve_triangular(diagonal, jnp.eye(block, dtype=jnp.floa...  90.9 us
    dot_general x28, matrix products, tdot(): lax.dot_general(left, right, (((1,), (1,)), ((), ())), precision=precisio...  48.2 us
    reduce_sum x2, other arithmetic, assemble_t(): dense = jnp.where(hit, flipped, 0.0).sum(axis=0)  38.3 us
    all_gather x1, blocking collectives, on_device(): gathered = lax.all_gather(packed, 'row', axis=0)  25 us
    dot_general x3, matrix products, mdot(): jnp.dot(left, right, precision=precision, preferred_element_type=jnp.floa...  17.3 us
    unnamed x75, local copies, waits for them, and re-layouts  14.8 us
    all_gather x4, waiting for transfers between devices, on_device(): lax.all_gather(carried_block[:, lo:hi], 'row', axis=0, tiled=True)  8.52 us
  transfers between devices with their start and end apart: 5, of which 1 were waited for; matrix products, arithmetic and copies ran while one was open for 75% of the time, Pallas kernels for 0%

profile of v4, /device:TPU:0, one launch (start us, length us, event | category | flops | bytes accessed | tf_op | source)
XLA Modules:
  0.0 407.7 jit_solution(746519850895406614)
XLA Ops:
  7.2 2.2 fusion.149
  11.5 1.8 copy.126
  15.0 25.0 %all-gather = f32[384,256]{1,0:T(8,128)S(1)} all-gather(f32[24,256]{1,0:T(8,128)S(1)} %fusion.128), channel_id=2, replica_groups=mesh['hyper'=2,'row'=16] {'row'}, dimensions={0}, use_global_device_ids=true | all-gather | bytes 417792 | tf_op jit(solution)/shard_map/all_gather | solution.py:80
  40.5 8.3 %select_reduce_fusion.1 = f32[128,32,256]{2,1,0:T(8,128)} fusion(f32[8,32,256]{2,1,0:T(8,128)} %bitcast.162, pred[8,128,256]{2,1,0:T(8,128)(4,1)S(1)} %iota_compare_fusion.4), kind=kLoop, calls=%fused_computation.1 | loop fusion | flops 15728640 | bytes 4718592 | tf_op jit(solution)/shard_map/reduce_sum | solution.py:30
  48.8 5.9 %copy.127 = f32[4096,256]{0,1:T(8,128)} copy(f32[4096,256]{1,0:T(8,128)} %bitcast.157) | data formatting | bytes 8388608 | tf_op jit(solution)/shard_map/reshape | solution.py:31
  56.6 8.5 %all-gather.7.cloned.1.call-done = f32[4096,256]{1,0:T(8,128)} async-done(((f32[256,256]{1,0:T(8,128)}), f32[4096,256]{1,0:T(8,128)}) %all-gather.7.cloned.1.call-update) | async-done | bytes 4194320 | tf_op jit(solution)/shard_map/all_gather | solution.py:93
  66.0 11.7 %cholesky.135 = f32[128,128]{1,0:T(8,128)S(1)} custom-call(f32[128,128]{1,0:T(8,128)S(1)} %slice.349), custom_call_target="Cholesky" | custom-call | tf_op jit(solution)/shard_map/jit(cholesky)/cholesky | solution.py:107
  79.0 9.8 %custom-call.12 = f32[1,128,128]{1,2,0:T(8,128)S(1)} custom-call(f32[1,128,128]{2,1,0:T(8,128)S(1)} %get-tuple-element.22), custom_call_target="InvertDiagBlocksLowerTriangular" | custom-call | tf_op jit(solution)/shard_map/jit(_solve_triangular)/triangular_solve | solution.py:108
  89.7 1.6 fusion.51
  92.3 2.0 convolution_subtract_fusion.1
  94.3 12.2 %cholesky.146 = f32[128,128]{1,0:T(8,128)S(1)} custom-call(f32[128,128]{1,0:T(8,128)S(1)} %slice.353), custom_call_target="Cholesky" | custom-call | tf_op jit(solution)/shard_map/jit(cholesky)/cholesky | solution.py:107
  108.4 9.8 %custom-call.13 = f32[1,128,128]{1,2,0:T(8,128)S(1)} custom-call(f32[1,128,128]{2,1,0:T(8,128)S(1)} %get-tuple-element.20), custom_call_target="InvertDiagBlocksLowerTriangular" | custom-call | tf_op jit(solution)/shard_map/jit(_solve_triangular)/triangular_solve | solution.py:108
  122.6 1.8 convolution_subtract_fusion.2
  125.2 11.7 %cholesky.157 = f32[128,128]{1,0:T(8,128)S(1)} custom-call(f32[128,128]{1,0:T(8,128)S(1)} %slice.357), custom_call_target="Cholesky" | custom-call | tf_op jit(solution)/shard_map/jit(cholesky)/cholesky | solution.py:107
  137.6 1.3 select_bitcast_fusion.5
  138.8 9.8 %custom-call.14 = f32[1,128,128]{1,2,0:T(8,128)S(1)} custom-call(f32[1,128,128]{2,1,0:T(8,128)S(1)} %get-tuple-element.18), custom_call_target="InvertDiagBlocksLowerTriangular" | custom-call | tf_op jit(solution)/shard_map/jit(_solve_triangular)/triangular_solve | solution.py:108
  149.6 1.4 fusion.57
  151.7 2.1 convolution_subtract_fusion.3
  154.6 11.7 %cholesky.168 = f32[128,128]{1,0:T(8,128)S(1)} custom-call(f32[128,128]{1,0:T(8,128)S(1)} %slice.362), custom_call_target="Cholesky" | custom-call | tf_op jit(solution)/shard_map/jit(cholesky)/cholesky | solution.py:107
  167.0 1.3 select_bitcast_fusion.4
  168.2 9.8 %custom-call.15 = f32[1,128,128]{1,2,0:T(8,128)S(1)} custom-call(f32[1,128,128]{2,1,0:T(8,128)S(1)} %get-tuple-element.16), custom_call_target="InvertDiagBlocksLowerTriangular" | custom-call | tf_op jit(solution)/shard_map/jit(_solve_triangular)/triangular_solve | solution.py:108
  179.0 1.4 fusion.78
  182.4 2.1 convolution_subtract_fusion.4
  185.3 11.7 %cholesky.179 = f32[128,128]{1,0:T(8,128)S(1)} custom-call(f32[128,128]{1,0:T(8,128)S(1)} %slice.368), custom_call_target="Cholesky" | custom-call | tf_op jit(solution)/shard_map/jit(cholesky)/cholesky | solution.py:107
  198.4 10.0 %custom-call.16 = f32[1,128,128]{1,2,0:T(8,128)S(1)} custom-call(f32[1,128,128]{2,1,0:T(8,128)S(1)} %get-tuple-element.14), custom_call_target="InvertDiagBlocksLowerTriangular" | custom-call | tf_op jit(solution)/shard_map/jit(_solve_triangular)/triangular_solve | solution.py:108
  210.7 1.9 constant_dynamic-update-slice_fusion
  212.6 2.3 convolution_subtract_fusion.5
  215.5 13.2 %cholesky.190 = f32[128,128]{1,0:T(8,128)} custom-call(f32[128,128]{1,0:T(8,128)} %slice.376), custom_call_target="Cholesky" | custom-call | tf_op jit(solution)/shard_map/jit(cholesky)/cholesky | solution.py:107
  230.2 2.2 select_bitcast_fusion.2
  232.4 11.3 %custom-call.17 = f32[1,128,128]{1,2,0:T(8,128)} custom-call(f32[1,128,128]{2,1,0:T(8,128)} %get-tuple-element.12), custom_call_target="InvertDiagBlocksLowerTriangular" | custom-call | tf_op jit(solution)/shard_map/jit(_solve_triangular)/triangular_solve | solution.py:108
  246.4 1.7 maximum_dynamic-update-slice_fusion.5
  248.1 1.7 maximum_dynamic-update-slice_fusion.4
  249.9 1.7 maximum_dynamic-update-slice_fusion.3
  257.4 2.1 convolution_subtract_fusion.6
  260.1 12.9 %cholesky.201 = f32[128,128]{1,0:T(8,128)S(1)} custom-call(f32[128,128]{1,0:T(8,128)} %slice.385), custom_call_target="Cholesky" | custom-call | tf_op jit(solution)/shard_map/jit(cholesky)/cholesky | solution.py:107
  273.7 1.3 select_bitcast_fusion.1
  275.0 10.6 %custom-call.18 = f32[1,128,128]{1,2,0:T(8,128)S(1)} custom-call(f32[1,128,128]{2,1,0:T(8,128)} %get-tuple-element.10), custom_call_target="InvertDiagBlocksLowerTriangular" | custom-call | tf_op jit(solution)/shard_map/jit(_solve_triangular)/triangular_solve | solution.py:108
  286.9 1.8 convolution_subtract_fusion.7
  288.7 11.7 %cholesky.212 = f32[128,128]{1,0:T(8,128)S(1)} custom-call(f32[128,128]{1,0:T(8,128)S(1)} %convolution_subtract_fusion.7), custom_call_target="Cholesky" | custom-call | tf_op jit(solution)/shard_map/jit(cholesky)/cholesky | solution.py:107
  301.1 1.3 select_bitcast_fusion
  302.4 9.8 %custom-call.19 = f32[1,128,128]{1,2,0:T(8,128)S(1)} custom-call(f32[1,128,128]{2,1,0:T(8,128)S(1)} %get-tuple-element.8), custom_call_target="InvertDiagBlocksLowerTriangular" | custom-call | tf_op jit(solution)/shard_map/jit(_solve_triangular)/triangular_solve | solution.py:108
  312.7 1.3 fusion.80
  314.6 1.7 fusion.47
  317.4 1.9 fusion.19
  319.3 1.9 fusion.15
  321.6 3.8 fusion.115
  326.3 1.8 fusion.14
  328.1 1.5 fusion.17
  329.7 2.2 fusion.21
  331.9 1.5 convolution_subtract_fusion.8
  333.4 2.0 fusion.146
  335.5 2.0 fusion.143
  337.7 1.6 fusion.12
  339.3 1.6 fusion.10
  341.4 1.6 convolution_add_fusion.5
  343.6 1.6 convolution_add_fusion.4
  345.2 2.2 convolution_add_fusion.2
  347.4 1.6 convolution_add_fusion.1
  349.6 1.8 fusion.3
  351.4 1.8 fusion.1
  353.2 2.3 pad_maximum_fusion
  355.5 2.3 pad_maximum_fusion.1
  357.8 30.0 %select_reduce_fusion = f32[32,32,4096]{2,1,0:T(8,128)} fusion(f32[8,32,4096]{2,1,0:T(8,128)} %bitcast.160, pred[8,32,4096]{2,1,0:T(8,128)(4,1)S(1)} %iota_compare_fusion.1), kind=kLoop, calls=%fused_computation | loop fusion | flops 62914560 | bytes 22020096 | tf_op jit(solution)/shard_map/reduce_sum | solution.py:30
  387.8 13.2 %convolution_subtract_fusion = f32[256,4096]{1,0:T(8,128)} fusion(f32[256,4096]{1,0:T(8,128)} %param.13, f32[256,1024]{1,0:T(8,128)S(1)} %fusion.143, f32[1024,4096]{1,0:T(8,128)} %bitcast.146), kind=kOutput, calls=%fused_computation.2 | convolution fusion | flops 6443499520 | bytes 26214400 | tf_op jit(solution)/shard_map/dot_general | solution.py:13
  (172 shorter events, 47.2 us)
Async XLA Ops:
  7.2 32.9 %copy-start.28 = (s32[8,8]{1,0:T(8,128)S(1)}, s32[8,8]{1,0:T(8,128)}, u32[]{:S(2)}) copy-start(s32[8,8]{1,0:T(8,128)} %param.12) | copy-start | bytes 772
  7.2 57.9 %all-gather.7.cloned.1.call-start = ((), (), s32[]{:S(2)}) async-start(), calls=%async_computation | async-start | bytes 4456448 | tf_op jit(solution)/shard_map/all_gather | solution.py:93
  9.4 113.2 %all-gather.9.cloned.1.call-start = ((), (), s32[]{:S(2)}) async-start(), calls=%async_computation.1 | async-start | bytes 4456448 | tf_op jit(solution)/shard_map/all_gather | solution.py:93
  10.2 172.2 %all-gather.11.cloned.1.call-start = ((), (), s32[]{:S(2)}) async-start(), calls=%async_computation.2 | async-start | bytes 4456448 | tf_op jit(solution)/shard_map/all_gather | solution.py:93
  10.9 246.5 %all-gather.13.cloned.1.call-start = ((), (), s32[]{:S(2)}) async-start(), calls=%async_computation.3 | async-start | bytes 4456448 | tf_op jit(solution)/shard_map/all_gather | solution.py:93
  11.5 346.3 %all-gather.15.cloned.1.call-start = ((), (), s32[]{:S(2)}) async-start(), calls=%async_computation.4 | async-start | bytes 4456448 | tf_op jit(solution)/shard_map/all_gather | solution.py:141
  124.4 0.8 copy-start.7
  153.8 0.7 copy-start.8
  179.0 31.4 %copy-start.6 = (f32[8,128,128]{2,1,0:T(8,128)S(1)}, f32[8,128,128]{2,1,0:T(8,128)}, u32[]{:S(2)}) copy-start(f32[8,128,128]{2,1,0:T(8,128)} %get-tuple-element.52) | copy-start | bytes 1572868
  184.6 0.7 copy-start.9
  198.3 53.3 %copy-start.13 = (f32[128,128]{1,0:T(8,128)}, f32[128,128]{1,0:T(8,128)S(1)}, u32[]{:S(2)}) copy-start(f32[128,128]{1,0:T(8,128)S(1)} %get-tuple-element.15) | copy-start | bytes 196612
  243.6 8.9 %copy-start.14 = (f32[128,128]{1,0:T(8,128)S(1)}, f32[128,128]{1,0:T(8,128)}, u32[]{:S(2)}) copy-start(f32[128,128]{1,0:T(8,128)} %get-tuple-element.13) | copy-start | bytes 196612
  246.4 7.7 %copy-start.15 = (f32[128,128]{1,0:T(8,128)}, f32[128,128]{1,0:T(8,128)S(1)}, u32[]{:S(2)}) copy-start(f32[128,128]{1,0:T(8,128)S(1)} %cholesky.136) | copy-start | bytes 196612
  248.1 4.4 %copy-start.19 = (f32[256,128]{1,0:T(8,128)}, f32[256,128]{1,0:T(8,128)S(1)}, u32[]{:S(2)}) copy-start(f32[256,128]{1,0:T(8,128)S(1)} %broadcast_in_dim.83) | copy-start | bytes 393220
  249.9 1.8 copy-start.10
  286.9 27.5 %copy-start.17 = (f32[128,128]{1,0:T(8,128)}, f32[128,128]{1,0:T(8,128)S(1)}, u32[]{:S(2)}) copy-start(f32[128,128]{1,0:T(8,128)S(1)} %get-tuple-element.45) | copy-start | bytes 196612
  314.5 2.8 copy-start.11
  314.5 2.8 copy-start.12
  314.5 2.8 copy-start.16
  314.5 2.8 copy-start.20
  314.5 2.8 copy-start.21
  314.5 2.8 copy-start.22
  317.4 3.8 copy-start.18
  317.4 3.8 copy-start.23
  317.4 3.8 copy-start.25
  317.4 4.0 copy-start.24
  321.6 3.8 copy-start.29
  321.6 4.6 %copy-start.5 = (f32[256,4096]{1,0:T(8,128)S(1)}, f32[256,4096]{1,0:T(8,128)}, u32[]{:S(2)}) copy-start(f32[256,4096]{1,0:T(8,128)} %param.10) | copy-start | bytes 12582916
  326.3 1.9 copy-start.26
  326.3 3.4 copy-start
  329.7 2.2 copy-start.27
  335.5 2.2 copy-start.1
  339.2 2.2 copy-start.2
  341.4 2.2 copy-start.3
  347.4 2.2 copy-start.4
Sparse Core Ops, SparseCore 0:
  10.7 54.3 all-gather.6
  67.3 49.2 all-gather.8
  118.7 49.4 all-gather.10
  170.2 49.4 all-gather.12
  221.7 51.9 all-gather.14

commit v5 on v4

--- a/solution.py
+++ b/solution.py
@@ -5,6 +5,7 @@
 
 PANELS = 4
 BLOCK = 128
+REACH = 32
 HIGHEST = lax.Precision.HIGHEST
 HIGH = lax.Precision.HIGH
 
@@ -139,8 +140,24 @@
     coupling_factor = jnp.concatenate([coupled_panel, coupled_rest], axis=1)
 
     all_values_t = lax.all_gather(values_t, "row", axis=1, tiled=True)
-    coupling_head_t = assemble_t(all_block_cols, all_values_t, factored // width)
-    carried_next = next_block - mdot(coupled_scaled, coupling_head_t, HIGH)
+    all_blocks = size // width
+    head_blocks = factored // width
+    near_end = min(head_blocks + REACH, all_blocks)
+    far_start = max(all_blocks - REACH, near_end)
+    spans = [(lo, hi) for lo, hi in ((0, near_end), (far_start, all_blocks)) if hi > lo]
+    pieces = []
+    at = 0
+    for lo, hi in spans:
+        if lo > at:
+            pieces.append(next_block[:, at * width:lo * width])
+        head_t = assemble_t(all_block_cols[lo:hi], all_values_t[:, lo * width:hi * width], head_blocks)
+        pieces.append(
+            next_block[:, lo * width:hi * width] - mdot(coupled_scaled, head_t, HIGH)
+        )
+        at = hi
+    if at < all_blocks:
+        pieces.append(next_block[:, at * width:])
+    carried_next = jnp.concatenate(pieces, axis=1)
 
     fixed_panel = tdot(all_fixed[:, :factored], head_inverse)
     own_fixed_panel = lax.dynamic_slice_in_dim(fixed_panel, top_at, rows, 1)

time: 415 us -> 389 us (0.937)
  other arithmetic: 248 us -> 233 us
  matrix products: 79 us -> 71.8 us
    reduce_sum x2 -> x3, other arithmetic: 38.3 us -> 29.8 us  [assemble_t(): dense = jnp.where(hit, flipped, 0.0).sum(axis=0)]
    another operation x16, other arithmetic: 90.9 us -> 85.7 us  [on_device(): jax.scipy.linalg.solve_triangular(diagonal, jnp.eye(block, dtype=jnp.floa...]
    unnamed x75 -> x109, local copies, waits for them, and re-layouts: 14.8 us -> 14.4 us
    dot_general x3 -> x4, matrix products: 17.3 us -> 17 us  [mdot(): jnp.dot(left, right, precision=precision, preferred_element_type=jnp.floa...]
  transfers between devices with their start and end apart: 5 -> 5, of which waited for: 1 -> 1; matrix products, arithmetic and copies ran while one was open for 75% -> 74% of each run, Pallas kernels for 0% -> 0%
where the time goes in v5:
time: 389 us; the launch traced here: 383 us
  other arithmetic  233 us (60%)
  matrix products  71.8 us (18%)
  local copies, waits for them, and re-layouts  28.4 us (7%)
  blocking collectives  25 us (6%)
  between operations  15.4 us (4%)
  waiting for transfers between devices  9.09 us (2%)
    another operation x24, other arithmetic, on_device(): diagonal = jnp.linalg.cholesky(panel[:block], symmetrize_input=False)  99.9 us
    another operation x16, other arithmetic, on_device(): jax.scipy.linalg.solve_triangular(diagonal, jnp.eye(block, dtype=jnp.floa...  85.7 us
    dot_general x28, matrix products, tdot(): lax.dot_general(left, right, (((1,), (1,)), ((), ())), precision=precisio...  45.2 us
    reduce_sum x3, other arithmetic, assemble_t(): dense = jnp.where(hit, flipped, 0.0).sum(axis=0)  29.8 us
    all_gather x1, blocking collectives, on_device(): gathered = lax.all_gather(packed, 'row', axis=0)  25 us
    dot_general x4, matrix products, mdot(): jnp.dot(left, right, precision=precision, preferred_element_type=jnp.floa...  17 us
    unnamed x109, local copies, waits for them, and re-layouts  14.4 us
  transfers between devices with their start and end apart: 5, of which 1 were waited for; matrix products, arithmetic and copies ran while one was open for 74% of the time, Pallas kernels for 0%

profile of v5, /device:TPU:0, one launch (start us, length us, event | category | flops | bytes accessed | tf_op | source)
XLA Modules:
  0.0 383.0 jit_solution(12783247219097705858)
XLA Ops:
  7.2 2.2 fusion.149
  11.5 1.8 copy.129
  15.0 25.0 %all-gather = f32[384,256]{1,0:T(8,128)S(1)} all-gather(f32[24,256]{1,0:T(8,128)S(1)} %fusion.128), channel_id=2, replica_groups=mesh['hyper'=2,'row'=16] {'row'}, dimensions={0}, use_global_device_ids=true | all-gather | bytes 417792 | tf_op jit(solution)/shard_map/all_gather | solution.py:81
  40.5 8.3 %select_reduce_fusion.2 = f32[128,32,256]{2,1,0:T(8,128)} fusion(f32[8,32,256]{2,1,0:T(8,128)} %bitcast.171, pred[8,128,256]{2,1,0:T(8,128)(4,1)S(1)} %iota_compare_fusion.5), kind=kLoop, calls=%fused_computation.2 | loop fusion | flops 15728640 | bytes 4718592 | tf_op jit(solution)/shard_map/reduce_sum | solution.py:31
  48.8 5.7 %copy.130 = f32[4096,256]{0,1:T(8,128)} copy(f32[4096,256]{1,0:T(8,128)} %bitcast.165) | data formatting | bytes 8388608 | tf_op jit(solution)/shard_map/reshape | solution.py:32
  56.2 1.1 iota_compare_fusion.2
  58.0 7.2 %all-gather.7.cloned.1.call-done = f32[4096,256]{1,0:T(8,128)} async-done(((f32[256,256]{1,0:T(8,128)}), f32[4096,256]{1,0:T(8,128)}) %all-gather.7.cloned.1.call-update) | async-done | bytes 4194320 | tf_op jit(solution)/shard_map/all_gather | solution.py:94
  66.0 11.7 %cholesky.135 = f32[128,128]{1,0:T(8,128)S(1)} custom-call(f32[128,128]{1,0:T(8,128)S(1)} %slice.387), custom_call_target="Cholesky" | custom-call | tf_op jit(solution)/shard_map/jit(cholesky)/cholesky | solution.py:108
  79.0 9.8 %custom-call.12 = f32[1,128,128]{1,2,0:T(8,128)S(1)} custom-call(f32[1,128,128]{2,1,0:T(8,128)S(1)} %get-tuple-element.22), custom_call_target="InvertDiagBlocksLowerTriangular" | custom-call | tf_op jit(solution)/shard_map/jit(_solve_triangular)/triangular_solve | solution.py:109
  89.2 1.6 fusion.51
  91.7 1.9 convolution_subtract_fusion.2
  93.6 11.9 %cholesky.146 = f32[128,128]{1,0:T(8,128)S(1)} custom-call(f32[128,128]{1,0:T(8,128)S(1)} %slice.391), custom_call_target="Cholesky" | custom-call | tf_op jit(solution)/shard_map/jit(cholesky)/cholesky | solution.py:108
  106.9 9.8 %custom-call.13 = f32[1,128,128]{1,2,0:T(8,128)S(1)} custom-call(f32[1,128,128]{2,1,0:T(8,128)S(1)} %get-tuple-element.20), custom_call_target="InvertDiagBlocksLowerTriangular" | custom-call | tf_op jit(solution)/shard_map/jit(_solve_triangular)/triangular_solve | solution.py:109
  119.8 1.8 convolution_subtract_fusion.3
  121.6 11.7 %cholesky.157 = f32[128,128]{1,0:T(8,128)S(1)} custom-call(f32[128,128]{1,0:T(8,128)S(1)} %slice.395), custom_call_target="Cholesky" | custom-call | tf_op jit(solution)/shard_map/jit(cholesky)/cholesky | solution.py:108
  134.6 9.8 %custom-call.14 = f32[1,128,128]{1,2,0:T(8,128)S(1)} custom-call(f32[1,128,128]{2,1,0:T(8,128)S(1)} %get-tuple-element.18), custom_call_target="InvertDiagBlocksLowerTriangular" | custom-call | tf_op jit(solution)/shard_map/jit(_solve_triangular)/triangular_solve | solution.py:109
  145.2 2.0 convolution_subtract_fusion.4
  147.9 12.1 %cholesky.168 = f32[128,128]{1,0:T(8,128)S(1)} custom-call(f32[128,128]{1,0:T(8,128)S(1)} %slice.400), custom_call_target="Cholesky" | custom-call | tf_op jit(solution)/shard_map/jit(cholesky)/cholesky | solution.py:108
  161.3 9.8 %custom-call.15 = f32[1,128,128]{1,2,0:T(8,128)S(1)} custom-call(f32[1,128,128]{2,1,0:T(8,128)S(1)} %get-tuple-element.16), custom_call_target="InvertDiagBlocksLowerTriangular" | custom-call | tf_op jit(solution)/shard_map/jit(_solve_triangular)/triangular_solve | solution.py:109
  171.5 1.3 fusion.78
  174.9 1.9 convolution_subtract_fusion.5
  176.8 11.7 %cholesky.179 = f32[128,128]{1,0:T(8,128)S(1)} custom-call(f32[128,128]{1,0:T(8,128)S(1)} %slice.406), custom_call_target="Cholesky" | custom-call | tf_op jit(solution)/shard_map/jit(cholesky)/cholesky | solution.py:108
  189.9 9.9 %custom-call.16 = f32[1,128,128]{1,2,0:T(8,128)S(1)} custom-call(f32[1,128,128]{2,1,0:T(8,128)S(1)} %get-tuple-element.14), custom_call_target="InvertDiagBlocksLowerTriangular" | custom-call | tf_op jit(solution)/shard_map/jit(_solve_triangular)/triangular_solve | solution.py:109
  202.2 1.0 constant_dynamic-update-slice_fusion
  203.2 2.3 convolution_subtract_fusion.6
  205.5 11.7 %cholesky.190 = f32[128,128]{1,0:T(8,128)S(1)} custom-call(f32[128,128]{1,0:T(8,128)S(1)} %slice.414), custom_call_target="Cholesky" | custom-call | tf_op jit(solution)/shard_map/jit(cholesky)/cholesky | solution.py:108
  217.9 1.3 select_bitcast_fusion.2
  219.2 9.8 %custom-call.17 = f32[1,128,128]{1,2,0:T(8,128)S(1)} custom-call(f32[1,128,128]{2,1,0:T(8,128)S(1)} %get-tuple-element.12), custom_call_target="InvertDiagBlocksLowerTriangular" | custom-call | tf_op jit(solution)/shard_map/jit(_solve_triangular)/triangular_solve | solution.py:109
  230.0 1.0 constant_dynamic-update-slice_fusion.1
  239.3 1.7 convolution_subtract_fusion.7
  241.0 11.9 %cholesky.201 = f32[128,128]{1,0:T(8,128)S(1)} custom-call(f32[128,128]{1,0:T(8,128)S(1)} %slice.423), custom_call_target="Cholesky" | custom-call | tf_op jit(solution)/shard_map/jit(cholesky)/cholesky | solution.py:108
  253.6 1.3 select_bitcast_fusion.1
  254.9 9.8 %custom-call.18 = f32[1,128,128]{1,2,0:T(8,128)S(1)} custom-call(f32[1,128,128]{2,1,0:T(8,128)S(1)} %get-tuple-element.10), custom_call_target="InvertDiagBlocksLowerTriangular" | custom-call | tf_op jit(solution)/shard_map/jit(_solve_triangular)/triangular_solve | solution.py:109
  265.9 1.8 convolution_subtract_fusion.8
  267.8 11.7 %cholesky.212 = f32[128,128]{1,0:T(8,128)S(1)} custom-call(f32[128,128]{1,0:T(8,128)S(1)} %convolution_subtract_fusion.8), custom_call_target="Cholesky" | custom-call | tf_op jit(solution)/shard_map/jit(cholesky)/cholesky | solution.py:108
  280.1 1.3 select_bitcast_fusion
  281.4 9.8 %custom-call.19 = f32[1,128,128]{1,2,0:T(8,128)S(1)} custom-call(f32[1,128,128]{2,1,0:T(8,128)S(1)} %get-tuple-element.8), custom_call_target="InvertDiagBlocksLowerTriangular" | custom-call | tf_op jit(solution)/shard_map/jit(_solve_triangular)/triangular_solve | solution.py:109
  291.6 1.9 fusion.80
  294.3 1.1 maximum_dynamic-update-slice_fusion
  297.2 1.9 fusion.19
  299.0 1.9 fusion.15
  301.2 1.9 fusion.14
  303.2 2.0 fusion.146
  305.7 2.0 fusion.21
  307.7 2.2 fusion.143
  310.3 1.6 fusion.12
  311.9 1.6 fusion.10
  314.1 1.6 convolution_add_fusion.5
  316.3 1.6 convolution_add_fusion.4
  317.9 1.8 convolution_add_fusion.2
  319.6 1.6 convolution_add_fusion.1
  321.8 2.0 fusion.3
  323.8 1.8 fusion.1
  325.6 2.3 pad_maximum_fusion
  327.9 2.3 pad_maximum_fusion.1
  330.2 1.3 slice.454
  331.5 6.7 %select_reduce_fusion.1 = f32[32,32,1024]{2,1,0:T(8,128)} fusion(f32[8,32,1024]{2,1,0:T(8,128)S(1)} %bitcast.169, pred[8,32,1024]{2,1,0:T(8,128)(4,1)S(1)} %copy-done.20), kind=kLoop, calls=%fused_computation.1 | loop fusion | flops 15728640 | bytes 5505024 | tf_op jit(solution)/shard_map/reduce_sum | solution.py:31
  338.2 4.7 %convolution_subtract_fusion.1 = f32[256,1024]{1,0:T(8,128)S(1)} fusion(f32[256,1024]{1,0:T(8,128)S(1)} %fusion.143, f32[1024,1024]{1,0:T(8,128)} %bitcast.164, f32[256,4096]{1,0:T(8,128)} %param.13), kind=kOutput, calls=%fused_computation.34 | convolution fusion | flops 1610874880 | bytes 7340032 | tf_op jit(solution)/shard_map/dot_general | solution.py:14
  342.9 14.8 %select_reduce_fusion = f32[32,32,2048]{2,1,0:T(8,128)} fusion(f32[8,32,2048]{2,1,0:T(8,128)S(1)} %bitcast.168, pred[8,32,2048]{2,1,0:T(8,128)(4,1)S(1)} %copy-done.11), kind=kLoop, calls=%fused_computation | loop fusion | flops 31457280 | bytes 11010048 | tf_op jit(solution)/shard_map/reduce_sum | solution.py:31
  357.8 8.1 %convolution_subtract_fusion = f32[256,2048]{1,0:T(8,128)S(1)} fusion(f32[256,1024]{1,0:T(8,128)S(1)} %fusion.143, f32[1024,2048]{1,0:T(8,128)} %bitcast.153, f32[256,4096]{1,0:T(8,128)} %param.13), kind=kOutput, calls=%fused_computation.28 | convolution fusion | flops 3221749760 | bytes 13631488 | tf_op jit(solution)/shard_map/dot_general | solution.py:14
  365.9 3.8 fusion.115
  369.7 1.5 fusion.17
  371.3 1.5 convolution_subtract_fusion.9
  373.6 2.3 pad_maximum_fusion.2
  (221 shorter events, 43.4 us)
Async XLA Ops:
  7.2 33.0 %copy-start.45 = (s32[8,8]{1,0:T(8,128)S(1)}, s32[8,8]{1,0:T(8,128)}, u32[]{:S(2)}) copy-start(s32[8,8]{1,0:T(8,128)} %param.12) | copy-start | bytes 772
  7.2 58.0 %all-gather.7.cloned.1.call-start = ((), (), s32[]{:S(2)}) async-start(), calls=%async_computation | async-start | bytes 4456448 | tf_op jit(solution)/shard_map/all_gather | solution.py:94
  9.4 110.3 %all-gather.9.cloned.1.call-start = ((), (), s32[]{:S(2)}) async-start(), calls=%async_computation.1 | async-start | bytes 4456448 | tf_op jit(solution)/shard_map/all_gather | solution.py:94
  10.2 164.7 %all-gather.11.cloned.1.call-start = ((), (), s32[]{:S(2)}) async-start(), calls=%async_computation.2 | async-start | bytes 4456448 | tf_op jit(solution)/shard_map/all_gather | solution.py:94
  10.9 228.4 %all-gather.13.cloned.1.call-start = ((), (), s32[]{:S(2)}) async-start(), calls=%async_computation.3 | async-start | bytes 4456448 | tf_op jit(solution)/shard_map/all_gather | solution.py:94
  11.5 318.7 %all-gather.15.cloned.1.call-start = ((), (), s32[]{:S(2)}) async-start(), calls=%async_computation.4 | async-start | bytes 4456448 | tf_op jit(solution)/shard_map/all_gather | solution.py:142
  79.0 39.9 %copy-start.23 = (f32[128,128]{1,0:T(8,128)}, f32[128,128]{1,0:T(8,128)S(1)}, u32[]{:S(2)}) copy-start(f32[128,128]{1,0:T(8,128)S(1)} %get-tuple-element.23) | copy-start | bytes 196612
  106.9 124.1 %copy-start.26 = (f32[128,128]{1,0:T(8,128)}, f32[128,128]{1,0:T(8,128)S(1)}, u32[]{:S(2)}) copy-start(f32[128,128]{1,0:T(8,128)S(1)} %get-tuple-element.21) | copy-start | bytes 196612
  134.6 97.2 %copy-start.36 = (f32[128,128]{1,0:T(8,128)}, f32[128,128]{1,0:T(8,128)S(1)}, u32[]{:S(2)}) copy-start(f32[128,128]{1,0:T(8,128)S(1)} %get-tuple-element.19) | copy-start | bytes 196612
  147.2 0.7 copy-start.12
  161.3 71.4 %copy-start.38 = (f32[128,128]{1,0:T(8,128)}, f32[128,128]{1,0:T(8,128)S(1)}, u32[]{:S(2)}) copy-start(f32[128,128]{1,0:T(8,128)S(1)} %get-tuple-element.17) | copy-start | bytes 196612
  189.9 43.7 %copy-start.28 = (f32[128,128]{1,0:T(8,128)}, f32[128,128]{1,0:T(8,128)S(1)}, u32[]{:S(2)}) copy-start(f32[128,128]{1,0:T(8,128)S(1)} %get-tuple-element.15) | copy-start | bytes 196612
  203.2 31.3 %copy-start.24 = (f32[128,128]{1,0:T(8,128)S(1)}, f32[128,128]{1,0:T(8,128)}, u32[]{:S(2)}) copy-start(f32[128,128]{1,0:T(8,128)} %copy-done.23) | copy-start | bytes 196612
  229.0 5.5 %copy-start.29 = (f32[128,128]{1,0:T(8,128)S(1)}, f32[128,128]{1,0:T(8,128)}, u32[]{:S(2)}) copy-start(f32[128,128]{1,0:T(8,128)} %get-tuple-element.13) | copy-start | bytes 196612
  231.0 5.1 %copy-start.30 = (f32[128,128]{1,0:T(8,128)}, f32[128,128]{1,0:T(8,128)S(1)}, u32[]{:S(2)}) copy-start(f32[128,128]{1,0:T(8,128)S(1)} %cholesky.136) | copy-start | bytes 196612
  231.8 0.9 copy-start.34
  231.9 7.5 %copy-start.10 = (f32[256,768]{1,0:T(8,128)S(1)}, f32[256,768]{1,0:T(8,128)}, u32[]{:S(2)}) copy-start(f32[256,768]{1,0:T(8,128)} %get-tuple-element.42) | copy-start | bytes 2359300
  232.7 0.9 copy-start.21
  235.2 56.4 %copy-start.41 = (f32[1,128,128]{2,1,0:T(8,128)S(1)}, f32[1,128,128]{2,1,0:T(8,128)}, u32[]{:S(2)}) copy-start(f32[1,128,128]{2,1,0:T(8,128)} %get-tuple-element.34) | copy-start | bytes 196612
  265.9 25.7 %copy-start.32 = (f32[128,128]{1,0:T(8,128)}, f32[128,128]{1,0:T(8,128)S(1)}, u32[]{:S(2)}) copy-start(f32[128,128]{1,0:T(8,128)S(1)} %get-tuple-element.45) | copy-start | bytes 196612
  267.7 27.7 %copy-start.15 = (f32[1,256,256]{2,1,0:T(8,128)S(1)}, f32[1,256,256]{2,1,0:T(8,128)}, u32[]{:S(2)}) copy-start(f32[1,256,256]{2,1,0:T(8,128)} %get-tuple-element.61) | copy-start | bytes 786436
  291.2 2.9 copy-start.42
  291.2 4.2 %copy-start.40 = (f32[128,128]{1,0:T(8,128)S(1)}, f32[128,128]{1,0:T(8,128)}, u32[]{:S(2)}) copy-start(f32[128,128]{1,0:T(8,128)} %get-tuple-element.9) | copy-start | bytes 196612
  293.5 0.8 copy-start.33
  294.1 3.0 copy-start.22
  294.1 3.0 copy-start.25
  294.1 3.0 copy-start.27
  294.1 3.0 copy-start.31
  294.1 3.0 copy-start.35
  294.1 3.0 copy-start.37
  294.1 3.0 copy-start.39
  299.0 2.2 copy-start.5
  300.9 6.8 %copy-start.13 = (f32[1,512,512]{2,1,0:T(8,128)}, f32[1,512,512]{2,1,0:T(8,128)S(1)}, u32[]{:S(2)}) copy-start(f32[1,512,512]{2,1,0:T(8,128)S(1)} %fusion.15) | copy-start | bytes 3145732
  301.1 6.6 %copy-start.16 = (f32[1,512,512]{2,1,0:T(8,128)}, f32[1,512,512]{2,1,0:T(8,128)S(1)}, u32[]{:S(2)}) copy-start(f32[1,512,512]{2,1,0:T(8,128)S(1)} %get-tuple-element.28) | copy-start | bytes 3145732
  301.1 6.6 %copy-start.18 = (f32[1,512,512]{2,1,0:T(8,128)}, f32[1,512,512]{2,1,0:T(8,128)S(1)}, u32[]{:S(2)}) copy-start(f32[1,512,512]{2,1,0:T(8,128)S(1)} %get-tuple-element.29) | copy-start | bytes 3145732
  303.1 22.5 %copy-start.6 = (f32[256,1024]{1,0:T(8,128)}, f32[256,1024]{1,0:T(8,128)S(1)}, u32[]{:S(2)}) copy-start(f32[256,1024]{1,0:T(8,128)S(1)} %fusion.14) | copy-start | bytes 3145732
  303.1 2.6 copy-start
  307.7 20.2 %copy-start.8 = (f32[256,1024]{1,0:T(8,128)}, f32[256,1024]{1,0:T(8,128)S(1)}, u32[]{:S(2)}) copy-start(f32[256,1024]{1,0:T(8,128)S(1)} %fusion.21) | copy-start | bytes 3145732
  307.7 2.6 copy-start.1
  311.9 2.2 copy-start.2
  314.1 2.2 copy-start.3
  319.6 2.2 copy-start.4
  327.9 3.6 copy-start.20
  338.2 4.7 %slice-start = ((f32[256,4096]{1,0:T(8,128)}), f32[256,2048]{1,0:T(8,128)S(1)}, s32[]{:S(2)}) async-start(f32[256,4096]{1,0:T(8,128)} %all-gather.15.cloned.1.call-done), calls=%async_computation.5 | async-start | bytes 4194304 | tf_op jit(solution)/shard_map/slice | solution.py:153
  338.2 4.7 %copy-start.11 = (pred[8,32,2048]{2,1,0:T(8,128)(4,1)S(1)}, pred[8,32,2048]{2,1,0:T(8,128)(4,1)}, u32[]{:S(2)}) copy-start(pred[8,32,2048]{2,1,0:T(8,128)(4,1)} %iota_compare_fusion.2) | copy-start | bytes 1572868
  357.7 8.1 %copy-start.14 = (f32[1,512,512]{2,1,0:T(8,128)S(1)}, f32[1,512,512]{2,1,0:T(8,128)}, u32[]{:S(2)}) copy-start(f32[1,512,512]{2,1,0:T(8,128)} %copy-done.13) | copy-start | bytes 3145732
  357.7 8.1 %copy-start.17 = (f32[1,512,512]{2,1,0:T(8,128)S(1)}, f32[1,512,512]{2,1,0:T(8,128)}, u32[]{:S(2)}) copy-start(f32[1,512,512]{2,1,0:T(8,128)} %copy-done.16) | copy-start | bytes 3145732
  357.7 8.1 %copy-start.19 = (f32[1,512,512]{2,1,0:T(8,128)S(1)}, f32[1,512,512]{2,1,0:T(8,128)}, u32[]{:S(2)}) copy-start(f32[1,512,512]{2,1,0:T(8,128)} %copy-done.18) | copy-start | bytes 3145732
  365.8 3.9 %copy-start.7 = (f32[256,1024]{1,0:T(8,128)S(1)}, f32[256,1024]{1,0:T(8,128)}, u32[]{:S(2)}) copy-start(f32[256,1024]{1,0:T(8,128)} %copy-done.6) | copy-start | bytes 3145732
  365.8 3.9 %copy-start.43 = (f32[16,256]{1,0:T(8,128)S(1)}, f32[16,256]{1,0:T(8,128)}, u32[]{:S(2)}) copy-start(f32[16,256]{1,0:T(8,128)} %param.14) | copy-start | bytes 49156
  365.9 5.4 %copy-start.9 = (f32[256,1024]{1,0:T(8,128)S(1)}, f32[256,1024]{1,0:T(8,128)}, u32[]{:S(2)}) copy-start(f32[256,1024]{1,0:T(8,128)} %copy-done.8) | copy-start | bytes 3145732
  365.9 5.4 %copy-start.44 = (f32[16,256]{1,0:T(8,128)S(1)}, f32[16,256]{1,0:T(8,128)}, u32[]{:S(2)}) copy-start(f32[16,256]{1,0:T(8,128)} %param.15) | copy-start | bytes 49156
  365.9 6.9 %copy-start.46 = (f32[16,16]{1,0:T(8,128)S(1)}, f32[16,16]{1,0:T(8,128)}, u32[]{:S(2)}) copy-start(f32[16,16]{1,0:T(8,128)} %param.16) | copy-start | bytes 3076
  365.9 7.7 %slice-start.1 = ((f32[256,4096]{1,0:T(8,128)}), f32[256,1024]{1,0:T(8,128)S(1)}, s32[]{:S(2)}) async-start(f32[256,4096]{1,0:T(8,128)} %param.13), calls=%async_computation.6 | async-start | bytes 2097152 | tf_op jit(solution)/shard_map/slice | solution.py:152
Sparse Core Ops, SparseCore 0:
  10.7 54.3 all-gather.6
  67.3 49.2 all-gather.8
  118.7 49.6 all-gather.10
  170.4 49.5 all-gather.12
  222.0 51.6 all-gather.14

commit v6 on v5

--- a/solution.py
+++ b/solution.py
@@ -125,18 +125,19 @@
             total = part if total is None else total + part
         return total
 
-    own_cols = carried_block[:, :factored]
-    lower = tdot(own_cols, head_inverse, HIGH)
-    lower = jnp.where(is_top, lax.dynamic_slice_in_dim(head_factor, top_at, rows, 0), lower)
-    lower_scaled = mdot(lower, head_inverse, HIGH)
-    state_rest = carried_block[:, factored:] - minus_below(lower_scaled)
-    state_rest = jnp.where(is_top, 0.0, state_rest)
+    coupled = assemble_t(block_cols, values_t, size // width).T
+    stacked = jnp.concatenate([carried_block[:, :factored], coupled[:, :factored]], axis=0)
+    panels = tdot(stacked, head_inverse, HIGH)
+    lower = jnp.where(
+        is_top, lax.dynamic_slice_in_dim(head_factor, top_at, rows, 0), panels[:rows]
+    )
+    coupled_panel = panels[rows:]
+    scaled = mdot(jnp.concatenate([lower, coupled_panel], axis=0), head_inverse, HIGH)
+    coupled_scaled = scaled[rows:]
+    updates = minus_below(scaled)
+    state_rest = jnp.where(is_top, 0.0, carried_block[:, factored:] - updates[:rows])
     factor_state = jnp.concatenate([lower, state_rest], axis=1)
-
-    coupled = assemble_t(block_cols, values_t, size // width).T
-    coupled_panel = tdot(coupled[:, :factored], head_inverse, HIGH)
-    coupled_scaled = mdot(coupled_panel, head_inverse, HIGH)
-    coupled_rest = coupled[:, factored:] - minus_below(coupled_scaled)
+    coupled_rest = coupled[:, factored:] - updates[rows:]
     coupling_factor = jnp.concatenate([coupled_panel, coupled_rest], axis=1)
 
     all_values_t = lax.all_gather(values_t, "row", axis=1, tiled=True)

time: 389 us -> 399 us (1.026)
  matrix products: 71.8 us -> 78 us
  local copies, waits for them, and re-layouts: 28.4 us -> 34.6 us
    unnamed x7, other arithmetic: 6.07 us -> 0.56 us
    sub x0 -> x1, other arithmetic: none -> 5.15 us  [on_device(): coupled_rest = coupled[:, factored:] - updates[rows:]]
    dot_general x28 -> x23, matrix products: 45.2 us -> 50.2 us  [tdot(): lax.dot_general(left, right, (((1,), (1,)), ((), ())), precision=precisio...]
    slice x3 -> x2, local copies, waits for them, and re-layouts: 1.3 us -> 6.19 us  [on_device(): all_values_t[:, lo * width:hi * width]]
    unnamed x109 -> x59, local copies, waits for them, and re-layouts: 14.4 us -> 11.9 us
    dot_general x4 -> x3, matrix products: 17 us -> 19.4 us  [mdot(): jnp.dot(left, right, precision=precision, preferred_element_type=jnp.floa...]
  transfers between devices with their start and end apart: 5 -> 5, of which waited for: 1 -> 1; matrix products, arithmetic and copies ran while one was open for 74% -> 67% of each run, Pallas kernels for 0% -> 0%
where the time goes in v6:
time: 399 us; the launch traced here: 393 us
  other arithmetic  232 us (58%)
  matrix products  78 us (20%)
  local copies, waits for them, and re-layouts  34.6 us (9%)
  blocking collectives  24.6 us (6%)
  between operations  15.1 us (4%)
  waiting for transfers between devices  9.01 us (2%)
    another operation x24, other arithmetic, on_device(): diagonal = jnp.linalg.cholesky(panel[:block], symmetrize_input=False)  99.9 us
    another operation x16, other arithmetic, on_device(): jax.scipy.linalg.solve_triangular(diagonal, jnp.eye(block, dtype=jnp.floa...  85.2 us
    dot_general x23, matrix products, tdot(): lax.dot_general(left, right, (((1,), (1,)), ((), ())), precision=precisio...  50.2 us
    reduce_sum x3, other arithmetic, assemble_t(): dense = jnp.where(hit, flipped, 0.0).sum(axis=0)  31 us
    all_gather x1, blocking collectives, on_device(): gathered = lax.all_gather(packed, 'row', axis=0)  24.6 us
    dot_general x3, matrix products, mdot(): jnp.dot(left, right, precision=precision, preferred_element_type=jnp.floa...  19.4 us
    unnamed x59, local copies, waits for them, and re-layouts  11.9 us
  transfers between devices with their start and end apart: 5, of which 1 were waited for; matrix products, arithmetic and copies ran while one was open for 67% of the time, Pallas kernels for 0%

profile of v6, /device:TPU:0, one launch (start us, length us, event | category | flops | bytes accessed | tf_op | source)
XLA Modules:
  0.0 393.3 jit_solution(921545045208440035)
XLA Ops:
  7.2 2.2 fusion.152
  11.5 1.8 copy.119
  13.6 24.6 %all-gather = f32[384,256]{1,0:T(8,128)S(1)} all-gather(f32[24,256]{1,0:T(8,128)S(1)} %fusion.128), channel_id=2, replica_groups=mesh['hyper'=2,'row'=16] {'row'}, dimensions={0}, use_global_device_ids=true | all-gather | bytes 417792 | tf_op jit(solution)/shard_map/all_gather | solution.py:81
  39.4 6.8 %select_reduce_fusion.2 = f32[128,32,256]{2,1,0:T(8,128)} fusion(f32[8,32,256]{2,1,0:T(8,128)S(1)} %bitcast.160, pred[8,128,256]{2,1,0:T(8,128)(4,1)S(1)} %iota_compare_fusion.5), kind=kLoop, calls=%fused_computation.2 | loop fusion | flops 15728640 | bytes 4718592 | tf_op jit(solution)/shard_map/reduce_sum | solution.py:31
  46.2 5.8 %copy.120 = f32[4096,256]{0,1:T(8,128)} copy(f32[4096,256]{1,0:T(8,128)} %bitcast.154) | data formatting | bytes 8388608 | tf_op jit(solution)/shard_map/reshape | solution.py:32
  52.0 2.3 slice.432
  55.3 1.1 iota_compare_fusion.2
  56.8 0.9 iota_compare_fusion.4
  57.7 7.0 %all-gather.7.cloned.1.call-done = f32[4096,256]{1,0:T(8,128)} async-done(((f32[256,256]{1,0:T(8,128)}), f32[4096,256]{1,0:T(8,128)}) %all-gather.7.cloned.1.call-update) | async-done | bytes 4194320 | tf_op jit(solution)/shard_map/all_gather | solution.py:94
  64.7 0.8 slice.387
  65.6 11.7 %cholesky.135 = f32[128,128]{1,0:T(8,128)S(1)} custom-call(f32[128,128]{1,0:T(8,128)S(1)} %slice.387), custom_call_target="Cholesky" | custom-call | tf_op jit(solution)/shard_map/jit(cholesky)/cholesky | solution.py:108
  78.6 9.8 %custom-call.12 = f32[1,128,128]{1,2,0:T(8,128)S(1)} custom-call(f32[1,128,128]{2,1,0:T(8,128)S(1)} %get-tuple-element.22), custom_call_target="InvertDiagBlocksLowerTriangular" | custom-call | tf_op jit(solution)/shard_map/jit(_solve_triangular)/triangular_solve | solution.py:109
  88.7 1.6 fusion.60
  92.0 2.0 convolution_subtract_fusion.2
  94.0 11.9 %cholesky.146 = f32[128,128]{1,0:T(8,128)S(1)} custom-call(f32[128,128]{1,0:T(8,128)S(1)} %slice.391), custom_call_target="Cholesky" | custom-call | tf_op jit(solution)/shard_map/jit(cholesky)/cholesky | solution.py:108
  107.2 9.8 %custom-call.13 = f32[1,128,128]{1,2,0:T(8,128)S(1)} custom-call(f32[1,128,128]{2,1,0:T(8,128)S(1)} %get-tuple-element.20), custom_call_target="InvertDiagBlocksLowerTriangular" | custom-call | tf_op jit(solution)/shard_map/jit(_solve_triangular)/triangular_solve | solution.py:109
  118.5 1.8 convolution_subtract_fusion.3
  120.3 11.7 %cholesky.157 = f32[128,128]{1,0:T(8,128)S(1)} custom-call(f32[128,128]{1,0:T(8,128)S(1)} %slice.395), custom_call_target="Cholesky" | custom-call | tf_op jit(solution)/shard_map/jit(cholesky)/cholesky | solution.py:108
  132.7 1.3 select_bitcast_fusion.5
  134.0 9.8 %custom-call.14 = f32[1,128,128]{1,2,0:T(8,128)S(1)} custom-call(f32[1,128,128]{2,1,0:T(8,128)S(1)} %get-tuple-element.18), custom_call_target="InvertDiagBlocksLowerTriangular" | custom-call | tf_op jit(solution)/shard_map/jit(_solve_triangular)/triangular_solve | solution.py:109
  145.9 2.0 convolution_subtract_fusion.4
  147.9 0.7 copy-done.11
  148.6 12.1 %cholesky.168 = f32[128,128]{1,0:T(8,128)S(1)} custom-call(f32[128,128]{1,0:T(8,128)S(1)} %slice.400), custom_call_target="Cholesky" | custom-call | tf_op jit(solution)/shard_map/jit(cholesky)/cholesky | solution.py:108
  162.1 9.8 %custom-call.15 = f32[1,128,128]{1,2,0:T(8,128)S(1)} custom-call(f32[1,128,128]{2,1,0:T(8,128)S(1)} %get-tuple-element.16), custom_call_target="InvertDiagBlocksLowerTriangular" | custom-call | tf_op jit(solution)/shard_map/jit(_solve_triangular)/triangular_solve | solution.py:109
  172.2 1.3 fusion.79
  176.3 1.9 convolution_subtract_fusion.5
  178.2 11.7 %cholesky.179 = f32[128,128]{1,0:T(8,128)S(1)} custom-call(f32[128,128]{1,0:T(8,128)S(1)} %slice.406), custom_call_target="Cholesky" | custom-call | tf_op jit(solution)/shard_map/jit(cholesky)/cholesky | solution.py:108
  191.3 10.0 %custom-call.16 = f32[1,128,128]{1,2,0:T(8,128)S(1)} custom-call(f32[1,128,128]{2,1,0:T(8,128)S(1)} %get-tuple-element.14), custom_call_target="InvertDiagBlocksLowerTriangular" | custom-call | tf_op jit(solution)/shard_map/jit(_solve_triangular)/triangular_solve | solution.py:109
  201.5 1.0 constant_dynamic-update-slice_fusion
  202.5 2.3 convolution_subtract_fusion.6
  204.8 11.7 %cholesky.190 = f32[128,128]{1,0:T(8,128)S(1)} custom-call(f32[128,128]{1,0:T(8,128)S(1)} %slice.414), custom_call_target="Cholesky" | custom-call | tf_op jit(solution)/shard_map/jit(cholesky)/cholesky | solution.py:108
  217.9 9.8 %custom-call.17 = f32[1,128,128]{1,2,0:T(8,128)S(1)} custom-call(f32[1,128,128]{2,1,0:T(8,128)S(1)} %get-tuple-element.12), custom_call_target="InvertDiagBlocksLowerTriangular" | custom-call | tf_op jit(solution)/shard_map/jit(_solve_triangular)/triangular_solve | solution.py:109
  229.3 1.0 constant_dynamic-update-slice_fusion.1
  230.3 2.0 convolution_subtract_fusion.7
  232.3 11.9 %cholesky.201 = f32[128,128]{1,0:T(8,128)S(1)} custom-call(f32[128,128]{1,0:T(8,128)S(1)} %slice.423), custom_call_target="Cholesky" | custom-call | tf_op jit(solution)/shard_map/jit(cholesky)/cholesky | solution.py:108
  245.6 9.8 %custom-call.18 = f32[1,128,128]{1,2,0:T(8,128)S(1)} custom-call(f32[1,128,128]{2,1,0:T(8,128)S(1)} %get-tuple-element.10), custom_call_target="InvertDiagBlocksLowerTriangular" | custom-call | tf_op jit(solution)/shard_map/jit(_solve_triangular)/triangular_solve | solution.py:109
  258.3 0.9 constant_dynamic-update-slice_fusion.2
  259.2 1.8 convolution_subtract_fusion.8
  260.9 11.7 %cholesky.212 = f32[128,128]{1,0:T(8,128)S(1)} custom-call(f32[128,128]{1,0:T(8,128)S(1)} %convolution_subtract_fusion.8), custom_call_target="Cholesky" | custom-call | tf_op jit(solution)/shard_map/jit(cholesky)/cholesky | solution.py:108
  274.0 10.4 %custom-call.19 = f32[1,128,128]{1,2,0:T(8,128)} custom-call(f32[1,128,128]{2,1,0:T(8,128)S(1)} %get-tuple-element.8), custom_call_target="InvertDiagBlocksLowerTriangular" | custom-call | tf_op jit(solution)/shard_map/jit(_solve_triangular)/triangular_solve | solution.py:109
  285.8 0.8 fusion.81
  288.8 1.9 fusion.25
  290.7 1.9 fusion.21
  292.8 3.8 fusion.17
  296.6 3.5 fusion.9
  300.1 1.7 convolution_subtract_fusion.9
  302.1 1.5 fusion.23
  303.7 3.5 fusion.13
  307.2 3.9 slice.453
  311.1 15.9 %select_reduce_fusion = f32[32,32,2048]{2,1,0:T(8,128)} fusion(f32[8,32,2048]{2,1,0:T(8,128)} %bitcast.157, pred[8,32,2048]{2,1,0:T(8,128)(4,1)S(1)} %copy-done.10), kind=kLoop, calls=%fused_computation | loop fusion | flops 31457280 | bytes 11010048 | tf_op jit(solution)/shard_map/reduce_sum | solution.py:31
  327.0 10.2 %convolution_subtract_fusion = f32[256,2048]{1,0:T(8,128)} fusion(f32[1024,2048]{1,0:T(8,128)} %bitcast.142, f32[256,4096]{1,0:T(8,128)} %param.13, f32[512,1024]{1,0:T(8,128)S(1)} %fusion.13), kind=kOutput, calls=%fused_computation.20 | convolution fusion | flops 3221749760 | bytes 13631488 | tf_op jit(solution)/shard_map/dot_general | solution.py:14
  337.3 2.3 slice.455
  339.6 8.3 %select_reduce_fusion.1 = f32[32,32,1024]{2,1,0:T(8,128)} fusion(f32[8,32,1024]{2,1,0:T(8,128)} %bitcast.158, pred[8,32,1024]{2,1,0:T(8,128)(4,1)S(1)} %copy-done.13), kind=kLoop, calls=%fused_computation.1 | loop fusion | flops 15728640 | bytes 5505024 | tf_op jit(solution)/shard_map/reduce_sum | solution.py:31
  347.9 5.6 %convolution_subtract_fusion.1 = f32[256,1024]{1,0:T(8,128)} fusion(f32[1024,1024]{1,0:T(8,128)} %bitcast.153, f32[256,4096]{1,0:T(8,128)} %param.13, f32[512,1024]{1,0:T(8,128)S(1)} %fusion.13), kind=kOutput, calls=%fused_computation.35 | convolution fusion | flops 1610874880 | bytes 7340032 | tf_op jit(solution)/shard_map/dot_general | solution.py:14
  353.6 0.8 convolution_subtract_fusion.11
  354.4 3.1 fusion.5
  357.5 3.3 fusion.7
  360.8 3.1 fusion.3
  363.9 9.0 %add_add_fusion = f32[512,3072]{1,0:T(8,128)} fusion(f32[512,3072]{1,0:T(8,128)S(1)} %fusion.3, f32[512,3072]{1,0:T(8,128)S(1)} %fusion.7, f32[512,3072]{1,0:T(8,128)S(1)} %fusion.5, f32[4096,256]{1,0:T(8,128)} %all-gather.13.cloned.1.call-done, f32[512,1024]{1,0:T(8,128)} %copy-done.1), kind=kOutput, calls=%fused_computation.3 | convolution fusion | flops 2420637696 | bytes 28835840 | tf_op jit(solution)/shard_map/dot_general | solution.py:18
  372.9 5.1 %slice_subtract_fusion = (f32[256,3072]{1,0:T(8,128)S(1)}, f32[256,3072]{1,0:T(8,128)S(1)}) fusion(f32[512,3072]{1,0:T(8,128)} %add_add_fusion, f32[256,4096]{1,0:T(8,128)S(1)} %bitcast.156, f32[256,4096]{1,0:T(8,128)} %param.10, pred[]{:T(512)S(6)} %lt.7), kind=kLoop, calls=%fused_computation.10 | loop fusion | flops 2359296 | bytes 18874368 | tf_op jit(solution)/shard_map/sub | solution.py:140
  378.1 2.3 pad_maximum_fusion.1
  380.4 2.5 pad_maximum_fusion
  382.8 0.9 slice-done.1
  384.0 2.3 pad_maximum_fusion.2
  (169 shorter events, 32.4 us)
Async XLA Ops:
  7.2 6.2 %copy-start.20 = (s32[8,8]{1,0:T(8,128)S(1)}, s32[8,8]{1,0:T(8,128)}, u32[]{:S(2)}) copy-start(s32[8,8]{1,0:T(8,128)} %param.12) | copy-start | bytes 772
  7.2 6.4 %copy-start.17 = (f32[16,256]{1,0:T(8,128)S(1)}, f32[16,256]{1,0:T(8,128)}, u32[]{:S(2)}) copy-start(f32[16,256]{1,0:T(8,128)} %param.14) | copy-start | bytes 49156
  7.2 57.5 %all-gather.7.cloned.1.call-start = ((), (), s32[]{:S(2)}) async-start(), calls=%async_computation | async-start | bytes 4456448 | tf_op jit(solution)/shard_map/all_gather | solution.py:94
  9.4 109.1 %all-gather.9.cloned.1.call-start = ((), (), s32[]{:S(2)}) async-start(), calls=%async_computation.1 | async-start | bytes 4456448 | tf_op jit(solution)/shard_map/all_gather | solution.py:94
  10.2 166.1 %all-gather.11.cloned.1.call-start = ((), (), s32[]{:S(2)}) async-start(), calls=%async_computation.2 | async-start | bytes 4456448 | tf_op jit(solution)/shard_map/all_gather | solution.py:94
  10.9 219.3 %all-gather.13.cloned.1.call-start = ((), (), s32[]{:S(2)}) async-start(), calls=%async_computation.3 | async-start | bytes 4456448 | tf_op jit(solution)/shard_map/all_gather | solution.py:94
  11.5 295.7 %all-gather.15.cloned.1.call-start = ((), (), s32[]{:S(2)}) async-start(), calls=%async_computation.4 | async-start | bytes 4456448 | tf_op jit(solution)/shard_map/all_gather | solution.py:143
  13.4 26.0 %copy-start.9 = (f32[256,256]{0,1:T(8,128)S(1)}, f32[256,256]{0,1:T(8,128)}, u32[]{:S(2)}) copy-start(f32[256,256]{0,1:T(8,128)} %copy.119) | copy-start | bytes 786436
  147.9 0.7 copy-start.11
  204.8 79.8 %copy-start.14 = (f32[128,128]{1,0:T(8,128)S(1)}, f32[128,128]{1,0:T(8,128)}, u32[]{:S(2)}) copy-start(f32[128,128]{1,0:T(8,128)} %get-tuple-element.19) | copy-start | bytes 196612
  284.5 0.7 copy-start.19
  284.6 0.8 copy-start.16
  284.7 1.1 copy-start.15
  292.7 3.8 slice-start
  292.7 3.8 copy-start.12
  296.6 3.5 copy-start.18
  302.1 1.6 copy-start.4
  307.2 53.6 %copy-start.1 = (f32[512,1024]{1,0:T(8,128)}, f32[512,1024]{1,0:T(8,128)S(1)}, u32[]{:S(2)}) copy-start(f32[512,1024]{1,0:T(8,128)S(1)} %fusion.13) | copy-start | bytes 6291460
  307.2 3.9 copy-start.10
  327.0 12.6 %copy-start.13 = (pred[8,32,1024]{2,1,0:T(8,128)(4,1)S(1)}, pred[8,32,1024]{2,1,0:T(8,128)(4,1)}, u32[]{:S(2)}) copy-start(pred[8,32,1024]{2,1,0:T(8,128)(4,1)} %iota_compare_fusion.4) | copy-start | bytes 786436
  347.9 5.6 %copy-start.21 = (f32[16,16]{1,0:T(8,128)S(1)}, f32[16,16]{1,0:T(8,128)}, u32[]{:S(2)}) copy-start(f32[16,16]{1,0:T(8,128)} %param.16) | copy-start | bytes 3076
  347.9 6.5 %copy-start.7 = (f32[4096,256]{1,0:T(8,128)S(1)}, f32[4096,256]{1,0:T(8,128)}, u32[]{:S(2)}) copy-start(f32[4096,256]{1,0:T(8,128)} %all-gather.9.cloned.1.call-done) | copy-start | bytes 12582916
  354.4 3.1 copy-start.6
  357.5 3.3 copy-start.8
  363.9 9.0 %copy-start = (f32[4096,256]{0,1:T(8,128)S(1)}, f32[4096,256]{0,1:T(8,128)}, u32[]{:S(2)}) copy-start(f32[4096,256]{0,1:T(8,128)} %copy.120) | copy-start | bytes 12582916
  372.9 5.2 %copy-start.5 = (f32[256,1024]{1,0:T(8,128)S(1)}, f32[256,1024]{1,0:T(8,128)}, u32[]{:S(2)}) copy-start(f32[256,1024]{1,0:T(8,128)} %copy-done.4) | copy-start | bytes 3145732
  380.4 2.5 copy-start.2
  380.4 3.3 slice-start.1
  380.4 3.7 copy-start.3
Sparse Core Ops, SparseCore 0:
  10.8 53.9 all-gather.6
  66.9 49.2 all-gather.8
  118.4 49.5 all-gather.10
  170.0 49.9 all-gather.12
  222.0 53.0 all-gather.14

commit v7 on v5

--- a/solution.py
+++ b/solution.py
@@ -159,11 +159,13 @@
         pieces.append(next_block[:, at * width:])
     carried_next = jnp.concatenate(pieces, axis=1)
 
-    fixed_panel = tdot(all_fixed[:, :factored], head_inverse)
+    fixed_panel = tdot(all_fixed[:, :factored], head_inverse, HIGH)
     own_fixed_panel = lax.dynamic_slice_in_dim(fixed_panel, top_at, rows, 1)
-    fixed_factor = jnp.where(is_top, own_fixed_panel, fixed_rows - tdot(fixed_panel, lower))
-    fixed_carried = fixed_next - tdot(fixed_panel, coupled_panel)
-    tip_next = tip_block - tdot(fixed_panel, fixed_panel)
+    fixed_factor = jnp.where(
+        is_top, own_fixed_panel, fixed_rows - tdot(fixed_panel, lower, HIGH)
+    )
+    fixed_carried = fixed_next - tdot(fixed_panel, coupled_panel, HIGH)
+    tip_next = tip_block - tdot(fixed_panel, fixed_panel, HIGH)
     return (factor_state, coupling_factor, carried_next, fixed_factor, fixed_carried, tip_next)
 
 

time: 389 us -> 387 us (level)
  no operation moved by 1% of the time
where the time goes in v7:
time: 387 us; the launch traced here: 381 us
  other arithmetic  233 us (60%)
  matrix products  69.6 us (18%)
  local copies, waits for them, and re-layouts  28.4 us (7%)
  blocking collectives  25 us (6%)
  between operations  15.4 us (4%)
  waiting for transfers between devices  9.09 us (2%)
    another operation x24, other arithmetic, on_device(): diagonal = jnp.linalg.cholesky(panel[:block], symmetrize_input=False)  99.9 us
    another operation x16, other arithmetic, on_device(): jax.scipy.linalg.solve_triangular(diagonal, jnp.eye(block, dtype=jnp.floa...  85.7 us
    dot_general x28, matrix products, tdot(): lax.dot_general(left, right, (((1,), (1,)), ((), ())), precision=precisio...  43 us
    reduce_sum x3, other arithmetic, assemble_t(): dense = jnp.where(hit, flipped, 0.0).sum(axis=0)  29.8 us
    all_gather x1, blocking collectives, on_device(): gathered = lax.all_gather(packed, 'row', axis=0)  25 us
    dot_general x4, matrix products, mdot(): jnp.dot(left, right, precision=precision, preferred_element_type=jnp.floa...  17 us
    unnamed x109, local copies, waits for them, and re-layouts  14.4 us
  transfers between devices with their start and end apart: 5, of which 1 were waited for; matrix products, arithmetic and copies ran while one was open for 74% of the time, Pallas kernels for 0%

profile of v7, /device:TPU:0, one launch (start us, length us, event | category | flops | bytes accessed | tf_op | source)
XLA Modules:
  0.0 380.8 jit_solution(4831652648715444227)
XLA Ops:
  7.2 2.2 fusion.149
  11.5 1.8 copy.129
  15.0 25.0 %all-gather = f32[384,256]{1,0:T(8,128)S(1)} all-gather(f32[24,256]{1,0:T(8,128)S(1)} %fusion.128), channel_id=2, replica_groups=mesh['hyper'=2,'row'=16] {'row'}, dimensions={0}, use_global_device_ids=true | all-gather | bytes 417792 | tf_op jit(solution)/shard_map/all_gather | solution.py:81
  40.5 8.3 %select_reduce_fusion.2 = f32[128,32,256]{2,1,0:T(8,128)} fusion(f32[8,32,256]{2,1,0:T(8,128)} %bitcast.171, pred[8,128,256]{2,1,0:T(8,128)(4,1)S(1)} %iota_compare_fusion.5), kind=kLoop, calls=%fused_computation.2 | loop fusion | flops 15728640 | bytes 4718592 | tf_op jit(solution)/shard_map/reduce_sum | solution.py:31
  48.8 5.7 %copy.130 = f32[4096,256]{0,1:T(8,128)} copy(f32[4096,256]{1,0:T(8,128)} %bitcast.165) | data formatting | bytes 8388608 | tf_op jit(solution)/shard_map/reshape | solution.py:32
  56.2 1.1 iota_compare_fusion.2
  58.0 7.2 %all-gather.7.cloned.1.call-done = f32[4096,256]{1,0:T(8,128)} async-done(((f32[256,256]{1,0:T(8,128)}), f32[4096,256]{1,0:T(8,128)}) %all-gather.7.cloned.1.call-update) | async-done | bytes 4194320 | tf_op jit(solution)/shard_map/all_gather | solution.py:94
  66.0 11.7 %cholesky.135 = f32[128,128]{1,0:T(8,128)S(1)} custom-call(f32[128,128]{1,0:T(8,128)S(1)} %slice.387), custom_call_target="Cholesky" | custom-call | tf_op jit(solution)/shard_map/jit(cholesky)/cholesky | solution.py:108
  79.0 9.8 %custom-call.12 = f32[1,128,128]{1,2,0:T(8,128)S(1)} custom-call(f32[1,128,128]{2,1,0:T(8,128)S(1)} %get-tuple-element.22), custom_call_target="InvertDiagBlocksLowerTriangular" | custom-call | tf_op jit(solution)/shard_map/jit(_solve_triangular)/triangular_solve | solution.py:109
  89.2 1.6 fusion.51
  91.7 1.9 convolution_subtract_fusion.2
  93.6 11.9 %cholesky.146 = f32[128,128]{1,0:T(8,128)S(1)} custom-call(f32[128,128]{1,0:T(8,128)S(1)} %slice.391), custom_call_target="Cholesky" | custom-call | tf_op jit(solution)/shard_map/jit(cholesky)/cholesky | solution.py:108
  106.9 9.8 %custom-call.13 = f32[1,128,128]{1,2,0:T(8,128)S(1)} custom-call(f32[1,128,128]{2,1,0:T(8,128)S(1)} %get-tuple-element.20), custom_call_target="InvertDiagBlocksLowerTriangular" | custom-call | tf_op jit(solution)/shard_map/jit(_solve_triangular)/triangular_solve | solution.py:109
  119.8 1.8 convolution_subtract_fusion.3
  121.6 11.7 %cholesky.157 = f32[128,128]{1,0:T(8,128)S(1)} custom-call(f32[128,128]{1,0:T(8,128)S(1)} %slice.395), custom_call_target="Cholesky" | custom-call | tf_op jit(solution)/shard_map/jit(cholesky)/cholesky | solution.py:108
  134.6 9.8 %custom-call.14 = f32[1,128,128]{1,2,0:T(8,128)S(1)} custom-call(f32[1,128,128]{2,1,0:T(8,128)S(1)} %get-tuple-element.18), custom_call_target="InvertDiagBlocksLowerTriangular" | custom-call | tf_op jit(solution)/shard_map/jit(_solve_triangular)/triangular_solve | solution.py:109
  145.2 2.0 convolution_subtract_fusion.4
  147.9 12.1 %cholesky.168 = f32[128,128]{1,0:T(8,128)S(1)} custom-call(f32[128,128]{1,0:T(8,128)S(1)} %slice.400), custom_call_target="Cholesky" | custom-call | tf_op jit(solution)/shard_map/jit(cholesky)/cholesky | solution.py:108
  161.3 9.8 %custom-call.15 = f32[1,128,128]{1,2,0:T(8,128)S(1)} custom-call(f32[1,128,128]{2,1,0:T(8,128)S(1)} %get-tuple-element.16), custom_call_target="InvertDiagBlocksLowerTriangular" | custom-call | tf_op jit(solution)/shard_map/jit(_solve_triangular)/triangular_solve | solution.py:109
  171.5 1.3 fusion.78
  174.9 1.9 convolution_subtract_fusion.5
  176.8 11.7 %cholesky.179 = f32[128,128]{1,0:T(8,128)S(1)} custom-call(f32[128,128]{1,0:T(8,128)S(1)} %slice.406), custom_call_target="Cholesky" | custom-call | tf_op jit(solution)/shard_map/jit(cholesky)/cholesky | solution.py:108
  189.9 9.9 %custom-call.16 = f32[1,128,128]{1,2,0:T(8,128)S(1)} custom-call(f32[1,128,128]{2,1,0:T(8,128)S(1)} %get-tuple-element.14), custom_call_target="InvertDiagBlocksLowerTriangular" | custom-call | tf_op jit(solution)/shard_map/jit(_solve_triangular)/triangular_solve | solution.py:109
  202.2 1.0 constant_dynamic-update-slice_fusion
  203.2 2.3 convolution_subtract_fusion.6
  205.5 11.7 %cholesky.190 = f32[128,128]{1,0:T(8,128)S(1)} custom-call(f32[128,128]{1,0:T(8,128)S(1)} %slice.414), custom_call_target="Cholesky" | custom-call | tf_op jit(solution)/shard_map/jit(cholesky)/cholesky | solution.py:108
  217.9 1.3 select_bitcast_fusion.2
  219.2 9.8 %custom-call.17 = f32[1,128,128]{1,2,0:T(8,128)S(1)} custom-call(f32[1,128,128]{2,1,0:T(8,128)S(1)} %get-tuple-element.12), custom_call_target="InvertDiagBlocksLowerTriangular" | custom-call | tf_op jit(solution)/shard_map/jit(_solve_triangular)/triangular_solve | solution.py:109
  230.0 1.0 constant_dynamic-update-slice_fusion.1
  239.3 1.7 convolution_subtract_fusion.7
  241.0 11.9 %cholesky.201 = f32[128,128]{1,0:T(8,128)S(1)} custom-call(f32[128,128]{1,0:T(8,128)S(1)} %slice.423), custom_call_target="Cholesky" | custom-call | tf_op jit(solution)/shard_map/jit(cholesky)/cholesky | solution.py:108
  253.6 1.3 select_bitcast_fusion.1
  254.9 9.8 %custom-call.18 = f32[1,128,128]{1,2,0:T(8,128)S(1)} custom-call(f32[1,128,128]{2,1,0:T(8,128)S(1)} %get-tuple-element.10), custom_call_target="InvertDiagBlocksLowerTriangular" | custom-call | tf_op jit(solution)/shard_map/jit(_solve_triangular)/triangular_solve | solution.py:109
  265.9 1.8 convolution_subtract_fusion.8
  267.8 11.7 %cholesky.212 = f32[128,128]{1,0:T(8,128)S(1)} custom-call(f32[128,128]{1,0:T(8,128)S(1)} %convolution_subtract_fusion.8), custom_call_target="Cholesky" | custom-call | tf_op jit(solution)/shard_map/jit(cholesky)/cholesky | solution.py:108
  280.1 1.3 select_bitcast_fusion
  281.4 9.8 %custom-call.19 = f32[1,128,128]{1,2,0:T(8,128)S(1)} custom-call(f32[1,128,128]{2,1,0:T(8,128)S(1)} %get-tuple-element.8), custom_call_target="InvertDiagBlocksLowerTriangular" | custom-call | tf_op jit(solution)/shard_map/jit(_solve_triangular)/triangular_solve | solution.py:109
  291.6 1.9 fusion.80
  294.3 1.1 maximum_dynamic-update-slice_fusion
  297.2 1.9 fusion.19
  299.0 1.9 fusion.15
  301.2 1.9 fusion.14
  303.2 2.0 fusion.146
  305.7 2.0 fusion.21
  307.7 2.2 fusion.143
  310.3 1.6 fusion.12
  311.9 1.6 fusion.10
  314.1 1.6 convolution_add_fusion.5
  316.3 1.6 convolution_add_fusion.4
  317.9 1.8 convolution_add_fusion.2
  319.6 1.6 convolution_add_fusion.1
  321.8 2.0 fusion.3
  323.8 1.8 fusion.1
  325.6 2.3 pad_maximum_fusion
  327.9 2.3 pad_maximum_fusion.1
  330.2 1.3 slice.454
  331.5 6.7 %select_reduce_fusion.1 = f32[32,32,1024]{2,1,0:T(8,128)} fusion(f32[8,32,1024]{2,1,0:T(8,128)S(1)} %bitcast.169, pred[8,32,1024]{2,1,0:T(8,128)(4,1)S(1)} %copy-done.20), kind=kLoop, calls=%fused_computation.1 | loop fusion | flops 15728640 | bytes 5505024 | tf_op jit(solution)/shard_map/reduce_sum | solution.py:31
  338.2 4.7 %convolution_subtract_fusion.1 = f32[256,1024]{1,0:T(8,128)S(1)} fusion(f32[256,1024]{1,0:T(8,128)S(1)} %fusion.143, f32[1024,1024]{1,0:T(8,128)} %bitcast.164, f32[256,4096]{1,0:T(8,128)} %param.13), kind=kOutput, calls=%fused_computation.34 | convolution fusion | flops 1610874880 | bytes 7340032 | tf_op jit(solution)/shard_map/dot_general | solution.py:14
  342.9 14.8 %select_reduce_fusion = f32[32,32,2048]{2,1,0:T(8,128)} fusion(f32[8,32,2048]{2,1,0:T(8,128)S(1)} %bitcast.168, pred[8,32,2048]{2,1,0:T(8,128)(4,1)S(1)} %copy-done.11), kind=kLoop, calls=%fused_computation | loop fusion | flops 31457280 | bytes 11010048 | tf_op jit(solution)/shard_map/reduce_sum | solution.py:31
  357.8 8.1 %convolution_subtract_fusion = f32[256,2048]{1,0:T(8,128)S(1)} fusion(f32[256,1024]{1,0:T(8,128)S(1)} %fusion.143, f32[1024,2048]{1,0:T(8,128)} %bitcast.153, f32[256,4096]{1,0:T(8,128)} %param.13), kind=kOutput, calls=%fused_computation.28 | convolution fusion | flops 3221749760 | bytes 13631488 | tf_op jit(solution)/shard_map/dot_general | solution.py:14
  365.9 2.4 fusion.115
  368.4 1.2 fusion.17
  369.6 1.1 convolution_subtract_fusion.9
  371.5 2.3 pad_maximum_fusion.2
  (221 shorter events, 43.4 us)
Async XLA Ops:
  7.2 33.0 %copy-start.45 = (s32[8,8]{1,0:T(8,128)S(1)}, s32[8,8]{1,0:T(8,128)}, u32[]{:S(2)}) copy-start(s32[8,8]{1,0:T(8,128)} %param.12) | copy-start | bytes 772
  7.2 58.0 %all-gather.7.cloned.1.call-start = ((), (), s32[]{:S(2)}) async-start(), calls=%async_computation | async-start | bytes 4456448 | tf_op jit(solution)/shard_map/all_gather | solution.py:94
  9.4 110.3 %all-gather.9.cloned.1.call-start = ((), (), s32[]{:S(2)}) async-start(), calls=%async_computation.1 | async-start | bytes 4456448 | tf_op jit(solution)/shard_map/all_gather | solution.py:94
  10.2 164.7 %all-gather.11.cloned.1.call-start = ((), (), s32[]{:S(2)}) async-start(), calls=%async_computation.2 | async-start | bytes 4456448 | tf_op jit(solution)/shard_map/all_gather | solution.py:94
  10.9 228.4 %all-gather.13.cloned.1.call-start = ((), (), s32[]{:S(2)}) async-start(), calls=%async_computation.3 | async-start | bytes 4456448 | tf_op jit(solution)/shard_map/all_gather | solution.py:94
  11.5 318.7 %all-gather.15.cloned.1.call-start = ((), (), s32[]{:S(2)}) async-start(), calls=%async_computation.4 | async-start | bytes 4456448 | tf_op jit(solution)/shard_map/all_gather | solution.py:142
  79.0 39.9 %copy-start.23 = (f32[128,128]{1,0:T(8,128)}, f32[128,128]{1,0:T(8,128)S(1)}, u32[]{:S(2)}) copy-start(f32[128,128]{1,0:T(8,128)S(1)} %get-tuple-element.23) | copy-start | bytes 196612
  106.9 124.1 %copy-start.26 = (f32[128,128]{1,0:T(8,128)}, f32[128,128]{1,0:T(8,128)S(1)}, u32[]{:S(2)}) copy-start(f32[128,128]{1,0:T(8,128)S(1)} %get-tuple-element.21) | copy-start | bytes 196612
  134.6 97.2 %copy-start.36 = (f32[128,128]{1,0:T(8,128)}, f32[128,128]{1,0:T(8,128)S(1)}, u32[]{:S(2)}) copy-start(f32[128,128]{1,0:T(8,128)S(1)} %get-tuple-element.19) | copy-start | bytes 196612
  147.2 0.7 copy-start.12
  161.3 71.4 %copy-start.38 = (f32[128,128]{1,0:T(8,128)}, f32[128,128]{1,0:T(8,128)S(1)}, u32[]{:S(2)}) copy-start(f32[128,128]{1,0:T(8,128)S(1)} %get-tuple-element.17) | copy-start | bytes 196612
  189.9 43.7 %copy-start.28 = (f32[128,128]{1,0:T(8,128)}, f32[128,128]{1,0:T(8,128)S(1)}, u32[]{:S(2)}) copy-start(f32[128,128]{1,0:T(8,128)S(1)} %get-tuple-element.15) | copy-start | bytes 196612
  203.2 31.3 %copy-start.24 = (f32[128,128]{1,0:T(8,128)S(1)}, f32[128,128]{1,0:T(8,128)}, u32[]{:S(2)}) copy-start(f32[128,128]{1,0:T(8,128)} %copy-done.23) | copy-start | bytes 196612
  229.0 5.5 %copy-start.29 = (f32[128,128]{1,0:T(8,128)S(1)}, f32[128,128]{1,0:T(8,128)}, u32[]{:S(2)}) copy-start(f32[128,128]{1,0:T(8,128)} %get-tuple-element.13) | copy-start | bytes 196612
  231.0 5.1 %copy-start.30 = (f32[128,128]{1,0:T(8,128)}, f32[128,128]{1,0:T(8,128)S(1)}, u32[]{:S(2)}) copy-start(f32[128,128]{1,0:T(8,128)S(1)} %cholesky.136) | copy-start | bytes 196612
  231.8 0.9 copy-start.34
  231.9 7.5 %copy-start.10 = (f32[256,768]{1,0:T(8,128)S(1)}, f32[256,768]{1,0:T(8,128)}, u32[]{:S(2)}) copy-start(f32[256,768]{1,0:T(8,128)} %get-tuple-element.42) | copy-start | bytes 2359300
  232.7 0.9 copy-start.21
  235.2 56.4 %copy-start.41 = (f32[1,128,128]{2,1,0:T(8,128)S(1)}, f32[1,128,128]{2,1,0:T(8,128)}, u32[]{:S(2)}) copy-start(f32[1,128,128]{2,1,0:T(8,128)} %get-tuple-element.34) | copy-start | bytes 196612
  265.9 25.7 %copy-start.32 = (f32[128,128]{1,0:T(8,128)}, f32[128,128]{1,0:T(8,128)S(1)}, u32[]{:S(2)}) copy-start(f32[128,128]{1,0:T(8,128)S(1)} %get-tuple-element.45) | copy-start | bytes 196612
  267.7 27.7 %copy-start.15 = (f32[1,256,256]{2,1,0:T(8,128)S(1)}, f32[1,256,256]{2,1,0:T(8,128)}, u32[]{:S(2)}) copy-start(f32[1,256,256]{2,1,0:T(8,128)} %get-tuple-element.61) | copy-start | bytes 786436
  291.2 2.9 copy-start.42
  291.2 4.2 %copy-start.40 = (f32[128,128]{1,0:T(8,128)S(1)}, f32[128,128]{1,0:T(8,128)}, u32[]{:S(2)}) copy-start(f32[128,128]{1,0:T(8,128)} %get-tuple-element.9) | copy-start | bytes 196612
  293.5 0.8 copy-start.33
  294.1 3.0 copy-start.22
  294.1 3.0 copy-start.25
  294.1 3.0 copy-start.27
  294.1 3.0 copy-start.31
  294.1 3.0 copy-start.35
  294.1 3.0 copy-start.37
  294.1 3.0 copy-start.39
  299.0 2.2 copy-start.5
  300.9 6.8 %copy-start.13 = (f32[1,512,512]{2,1,0:T(8,128)}, f32[1,512,512]{2,1,0:T(8,128)S(1)}, u32[]{:S(2)}) copy-start(f32[1,512,512]{2,1,0:T(8,128)S(1)} %fusion.15) | copy-start | bytes 3145732
  301.1 6.6 %copy-start.16 = (f32[1,512,512]{2,1,0:T(8,128)}, f32[1,512,512]{2,1,0:T(8,128)S(1)}, u32[]{:S(2)}) copy-start(f32[1,512,512]{2,1,0:T(8,128)S(1)} %get-tuple-element.28) | copy-start | bytes 3145732
  301.1 6.6 %copy-start.18 = (f32[1,512,512]{2,1,0:T(8,128)}, f32[1,512,512]{2,1,0:T(8,128)S(1)}, u32[]{:S(2)}) copy-start(f32[1,512,512]{2,1,0:T(8,128)S(1)} %get-tuple-element.29) | copy-start | bytes 3145732
  303.1 22.5 %copy-start.6 = (f32[256,1024]{1,0:T(8,128)}, f32[256,1024]{1,0:T(8,128)S(1)}, u32[]{:S(2)}) copy-start(f32[256,1024]{1,0:T(8,128)S(1)} %fusion.14) | copy-start | bytes 3145732
  303.1 2.6 copy-start
  307.7 20.2 %copy-start.8 = (f32[256,1024]{1,0:T(8,128)}, f32[256,1024]{1,0:T(8,128)S(1)}, u32[]{:S(2)}) copy-start(f32[256,1024]{1,0:T(8,128)S(1)} %fusion.21) | copy-start | bytes 3145732
  307.7 2.6 copy-start.1
  311.9 2.2 copy-start.2
  314.1 2.2 copy-start.3
  319.6 2.2 copy-start.4
  327.9 3.6 copy-start.20
  338.2 4.7 %slice-start = ((f32[256,4096]{1,0:T(8,128)}), f32[256,2048]{1,0:T(8,128)S(1)}, s32[]{:S(2)}) async-start(f32[256,4096]{1,0:T(8,128)} %all-gather.15.cloned.1.call-done), calls=%async_computation.5 | async-start | bytes 4194304 | tf_op jit(solution)/shard_map/slice | solution.py:153
  338.2 4.7 %copy-start.11 = (pred[8,32,2048]{2,1,0:T(8,128)(4,1)S(1)}, pred[8,32,2048]{2,1,0:T(8,128)(4,1)}, u32[]{:S(2)}) copy-start(pred[8,32,2048]{2,1,0:T(8,128)(4,1)} %iota_compare_fusion.2) | copy-start | bytes 1572868
  357.7 8.1 %copy-start.14 = (f32[1,512,512]{2,1,0:T(8,128)S(1)}, f32[1,512,512]{2,1,0:T(8,128)}, u32[]{:S(2)}) copy-start(f32[1,512,512]{2,1,0:T(8,128)} %copy-done.13) | copy-start | bytes 3145732
  357.7 8.1 %copy-start.17 = (f32[1,512,512]{2,1,0:T(8,128)S(1)}, f32[1,512,512]{2,1,0:T(8,128)}, u32[]{:S(2)}) copy-start(f32[1,512,512]{2,1,0:T(8,128)} %copy-done.16) | copy-start | bytes 3145732
  357.7 8.1 %copy-start.19 = (f32[1,512,512]{2,1,0:T(8,128)S(1)}, f32[1,512,512]{2,1,0:T(8,128)}, u32[]{:S(2)}) copy-start(f32[1,512,512]{2,1,0:T(8,128)} %copy-done.18) | copy-start | bytes 3145732
  365.8 2.6 copy-start.7
  365.8 2.6 copy-start.43
  365.9 3.7 copy-start.9
  365.9 3.7 copy-start.44
  365.9 4.8 %copy-start.46 = (f32[16,16]{1,0:T(8,128)S(1)}, f32[16,16]{1,0:T(8,128)}, u32[]{:S(2)}) copy-start(f32[16,16]{1,0:T(8,128)} %param.16) | copy-start | bytes 3076
  365.9 5.6 %slice-start.1 = ((f32[256,4096]{1,0:T(8,128)}), f32[256,1024]{1,0:T(8,128)S(1)}, s32[]{:S(2)}) async-start(f32[256,4096]{1,0:T(8,128)} %param.13), calls=%async_computation.6 | async-start | bytes 2097152 | tf_op jit(solution)/shard_map/slice | solution.py:152
Sparse Core Ops, SparseCore 0:
  10.7 54.3 all-gather.6
  67.3 49.2 all-gather.8
  118.7 49.6 all-gather.10
  170.4 49.5 all-gather.12
  222.0 51.6 all-gather.14

commit v8 on v7

--- a/solution.py
+++ b/solution.py
@@ -129,15 +129,15 @@
     lower = tdot(own_cols, head_inverse, HIGH)
     lower = jnp.where(is_top, lax.dynamic_slice_in_dim(head_factor, top_at, rows, 0), lower)
     lower_scaled = mdot(lower, head_inverse, HIGH)
-    state_rest = carried_block[:, factored:] - minus_below(lower_scaled)
-    state_rest = jnp.where(is_top, 0.0, state_rest)
-    factor_state = jnp.concatenate([lower, state_rest], axis=1)
+    state_updates = jnp.pad(minus_below(lower_scaled), ((0, 0), (factored, 0)))
+    factor_state = jnp.where(is_top, 0.0, carried_block - state_updates)
+    factor_state = lax.dynamic_update_slice(factor_state, lower, (0, 0))
 
     coupled = assemble_t(block_cols, values_t, size // width).T
     coupled_panel = tdot(coupled[:, :factored], head_inverse, HIGH)
     coupled_scaled = mdot(coupled_panel, head_inverse, HIGH)
-    coupled_rest = coupled[:, factored:] - minus_below(coupled_scaled)
-    coupling_factor = jnp.concatenate([coupled_panel, coupled_rest], axis=1)
+    coupled_updates = jnp.pad(minus_below(coupled_scaled), ((0, 0), (factored, 0)))
+    coupling_factor = lax.dynamic_update_slice(coupled - coupled_updates, coupled_panel, (0, 0))
 
     all_values_t = lax.all_gather(values_t, "row", axis=1, tiled=True)
     all_blocks = size // width
@@ -149,15 +149,13 @@
     at = 0
     for lo, hi in spans:
         if lo > at:
-            pieces.append(next_block[:, at * width:lo * width])
+            pieces.append(jnp.zeros((rows, (lo - at) * width), jnp.float32))
         head_t = assemble_t(all_block_cols[lo:hi], all_values_t[:, lo * width:hi * width], head_blocks)
-        pieces.append(
-            next_block[:, lo * width:hi * width] - mdot(coupled_scaled, head_t, HIGH)
-        )
+        pieces.append(mdot(coupled_scaled, head_t, HIGH))
         at = hi
     if at < all_blocks:
-        pieces.append(next_block[:, at * width:])
-    carried_next = jnp.concatenate(pieces, axis=1)
+        pieces.append(jnp.zeros((rows, (all_blocks - at) * width), jnp.float32))
+    carried_next = next_block - jnp.concatenate(pieces, axis=1)
 
     fixed_panel = tdot(all_fixed[:, :factored], head_inverse, HIGH)
     own_fixed_panel = lax.dynamic_slice_in_dim(fixed_panel, top_at, rows, 1)

time: 387 us -> 385 us (level)
  other arithmetic: 233 us -> 229 us
    concatenate x3 -> x0, other arithmetic: 6.94 us -> none  [the longest x1 2.34 us: on_device(): carried_next = jnp.concatenate(pieces, axis=1)]
    sub x0 -> x2, other arithmetic: none -> 5.28 us  [the longest x1 2.81 us: on_device(): carried_next = next_block - jnp.concatenate(pieces, axis=1)]
    unnamed x7, other arithmetic: 6.07 us -> 1.34 us
    unnamed x109 -> x79, local copies, waits for them, and re-layouts: 14.4 us -> 14.2 us
  transfers between devices with their start and end apart: 5 -> 5, of which waited for: 1 -> 1; matrix products, arithmetic and copies ran while one was open for 74% -> 75% of each run, Pallas kernels for 0% -> 0%
where the time goes in v8:
time: 385 us; the launch traced here: 378 us
  other arithmetic  229 us (59%)
  matrix products  69.1 us (18%)
  local copies, waits for them, and re-layouts  31 us (8%)
  blocking collectives  25 us (6%)
  between operations  15 us (4%)
  waiting for transfers between devices  8.25 us (2%)
    another operation x24, other arithmetic, on_device(): diagonal = jnp.linalg.cholesky(panel[:block], symmetrize_input=False)  100 us
    another operation x16, other arithmetic, on_device(): jax.scipy.linalg.solve_triangular(diagonal, jnp.eye(block, dtype=jnp.floa...  86.4 us
    dot_general x28, matrix products, tdot(): lax.dot_general(left, right, (((1,), (1,)), ((), ())), precision=precisio...  45.9 us
    reduce_sum x3, other arithmetic, assemble_t(): dense = jnp.where(hit, flipped, 0.0).sum(axis=0)  29.7 us
    all_gather x1, blocking collectives, on_device(): gathered = lax.all_gather(packed, 'row', axis=0)  25 us
    dot_general x4, matrix products, mdot(): jnp.dot(left, right, precision=precision, preferred_element_type=jnp.floa...  15 us
    unnamed x79, local copies, waits for them, and re-layouts  14.2 us
  transfers between devices with their start and end apart: 5, of which 1 were waited for; matrix products, arithmetic and copies ran while one was open for 75% of the time, Pallas kernels for 0%

profile of v8, /device:TPU:0, one launch (start us, length us, event | category | flops | bytes accessed | tf_op | source)
XLA Modules:
  0.0 378.1 jit_solution(13906848805464958730)
XLA Ops:
  7.2 2.2 fusion.146
  11.5 1.8 copy.129
  15.0 25.0 %all-gather = f32[384,256]{1,0:T(8,128)S(1)} all-gather(f32[24,256]{1,0:T(8,128)S(1)} %fusion.125), channel_id=2, replica_groups=mesh['hyper'=2,'row'=16] {'row'}, dimensions={0}, use_global_device_ids=true | all-gather | bytes 417792 | tf_op jit(solution)/shard_map/all_gather | solution.py:81
  41.1 8.2 %select_reduce_fusion.2 = f32[128,32,256]{2,1,0:T(8,128)} fusion(f32[8,32,256]{2,1,0:T(8,128)} %bitcast.171, pred[8,128,256]{2,1,0:T(8,128)(4,1)S(1)} %iota_compare_fusion.5), kind=kLoop, calls=%fused_computation.2 | loop fusion | flops 15728640 | bytes 4718592 | tf_op jit(solution)/shard_map/reduce_sum | solution.py:31
  49.3 5.9 %copy.130 = f32[4096,256]{0,1:T(8,128)} copy(f32[4096,256]{1,0:T(8,128)} %bitcast.166) | data formatting | bytes 8388608 | tf_op jit(solution)/shard_map/reshape | solution.py:32
  56.9 1.2 iota_compare_fusion.2
  58.8 6.3 %all-gather.7.cloned.1.call-done = f32[4096,256]{1,0:T(8,128)} async-done(((f32[256,256]{1,0:T(8,128)}), f32[4096,256]{1,0:T(8,128)}) %all-gather.7.cloned.1.call-update) | async-done | bytes 4194320 | tf_op jit(solution)/shard_map/all_gather | solution.py:94
  65.9 11.7 %cholesky.135 = f32[128,128]{1,0:T(8,128)S(1)} custom-call(f32[128,128]{1,0:T(8,128)S(1)} %slice.367), custom_call_target="Cholesky" | custom-call | tf_op jit(solution)/shard_map/jit(cholesky)/cholesky | solution.py:108
  79.0 9.8 %custom-call.12 = f32[1,128,128]{1,2,0:T(8,128)S(1)} custom-call(f32[1,128,128]{2,1,0:T(8,128)S(1)} %get-tuple-element.22), custom_call_target="InvertDiagBlocksLowerTriangular" | custom-call | tf_op jit(solution)/shard_map/jit(_solve_triangular)/triangular_solve | solution.py:109
  89.1 1.6 fusion.48
  91.7 1.9 convolution_subtract_fusion
  93.6 12.2 %cholesky.146 = f32[128,128]{1,0:T(8,128)S(1)} custom-call(f32[128,128]{1,0:T(8,128)S(1)} %slice.371), custom_call_target="Cholesky" | custom-call | tf_op jit(solution)/shard_map/jit(cholesky)/cholesky | solution.py:108
  107.1 9.8 %custom-call.13 = f32[1,128,128]{1,2,0:T(8,128)S(1)} custom-call(f32[1,128,128]{2,1,0:T(8,128)S(1)} %get-tuple-element.20), custom_call_target="InvertDiagBlocksLowerTriangular" | custom-call | tf_op jit(solution)/shard_map/jit(_solve_triangular)/triangular_solve | solution.py:109
  120.0 1.8 convolution_subtract_fusion.1
  121.8 11.7 %cholesky.157 = f32[128,128]{1,0:T(8,128)S(1)} custom-call(f32[128,128]{1,0:T(8,128)S(1)} %slice.375), custom_call_target="Cholesky" | custom-call | tf_op jit(solution)/shard_map/jit(cholesky)/cholesky | solution.py:108
  134.2 1.3 select_bitcast_fusion.5
  135.5 9.8 %custom-call.14 = f32[1,128,128]{1,2,0:T(8,128)S(1)} custom-call(f32[1,128,128]{2,1,0:T(8,128)S(1)} %get-tuple-element.18), custom_call_target="InvertDiagBlocksLowerTriangular" | custom-call | tf_op jit(solution)/shard_map/jit(_solve_triangular)/triangular_solve | solution.py:109
  146.1 2.0 convolution_subtract_fusion.2
  148.8 11.8 %cholesky.168 = f32[128,128]{1,0:T(8,128)S(1)} custom-call(f32[128,128]{1,0:T(8,128)S(1)} %slice.380), custom_call_target="Cholesky" | custom-call | tf_op jit(solution)/shard_map/jit(cholesky)/cholesky | solution.py:108
  161.3 1.3 select_bitcast_fusion.4
  162.5 9.8 %custom-call.15 = f32[1,128,128]{1,2,0:T(8,128)S(1)} custom-call(f32[1,128,128]{2,1,0:T(8,128)S(1)} %get-tuple-element.16), custom_call_target="InvertDiagBlocksLowerTriangular" | custom-call | tf_op jit(solution)/shard_map/jit(_solve_triangular)/triangular_solve | solution.py:109
  172.6 1.3 fusion.75
  176.1 1.9 convolution_subtract_fusion.3
  178.0 11.7 %cholesky.179 = f32[128,128]{1,0:T(8,128)S(1)} custom-call(f32[128,128]{1,0:T(8,128)S(1)} %slice.386), custom_call_target="Cholesky" | custom-call | tf_op jit(solution)/shard_map/jit(cholesky)/cholesky | solution.py:108
  191.1 10.0 %custom-call.16 = f32[1,128,128]{1,2,0:T(8,128)S(1)} custom-call(f32[1,128,128]{2,1,0:T(8,128)S(1)} %get-tuple-element.14), custom_call_target="InvertDiagBlocksLowerTriangular" | custom-call | tf_op jit(solution)/shard_map/jit(_solve_triangular)/triangular_solve | solution.py:109
  203.4 1.0 constant_dynamic-update-slice_fusion
  204.4 2.3 convolution_subtract_fusion.4
  206.8 11.7 %cholesky.190 = f32[128,128]{1,0:T(8,128)S(1)} custom-call(f32[128,128]{1,0:T(8,128)S(1)} %slice.394), custom_call_target="Cholesky" | custom-call | tf_op jit(solution)/shard_map/jit(cholesky)/cholesky | solution.py:108
  219.8 9.8 %custom-call.17 = f32[1,128,128]{1,2,0:T(8,128)S(1)} custom-call(f32[1,128,128]{2,1,0:T(8,128)S(1)} %get-tuple-element.12), custom_call_target="InvertDiagBlocksLowerTriangular" | custom-call | tf_op jit(solution)/shard_map/jit(_solve_triangular)/triangular_solve | solution.py:109
  234.1 2.0 convolution_subtract_fusion.5
  236.2 12.1 %cholesky.201 = f32[128,128]{1,0:T(8,128)S(1)} custom-call(f32[128,128]{1,0:T(8,128)S(1)} %slice.403), custom_call_target="Cholesky" | custom-call | tf_op jit(solution)/shard_map/jit(cholesky)/cholesky | solution.py:108
  249.0 1.3 select_bitcast_fusion.1
  250.2 9.8 %custom-call.18 = f32[1,128,128]{1,2,0:T(8,128)S(1)} custom-call(f32[1,128,128]{2,1,0:T(8,128)S(1)} %get-tuple-element.10), custom_call_target="InvertDiagBlocksLowerTriangular" | custom-call | tf_op jit(solution)/shard_map/jit(_solve_triangular)/triangular_solve | solution.py:109
  261.9 1.8 convolution_subtract_fusion.6
  263.7 11.7 %cholesky.212 = f32[128,128]{1,0:T(8,128)S(1)} custom-call(f32[128,128]{1,0:T(8,128)S(1)} %convolution_subtract_fusion.6), custom_call_target="Cholesky" | custom-call | tf_op jit(solution)/shard_map/jit(cholesky)/cholesky | solution.py:108
  276.1 1.3 select_bitcast_fusion
  277.3 9.8 %custom-call.19 = f32[1,128,128]{1,2,0:T(8,128)S(1)} custom-call(f32[1,128,128]{2,1,0:T(8,128)S(1)} %get-tuple-element.8), custom_call_target="InvertDiagBlocksLowerTriangular" | custom-call | tf_op jit(solution)/shard_map/jit(_solve_triangular)/triangular_solve | solution.py:109
  291.8 1.8 fusion.16
  294.2 1.9 fusion.12
  296.1 1.9 fusion.11
  298.0 2.0 fusion.143
  300.6 1.7 fusion.9
  302.8 2.0 convolution_add_fusion.5
  305.0 1.8 convolution_add_fusion.4
  307.2 1.8 convolution_add_fusion.3
  309.0 2.7 subtract_select_fusion
  311.7 1.0 constant_dynamic-update-slice_fusion.17
  312.8 3.2 fusion.18
  316.1 2.0 fusion.140
  318.1 1.7 fusion.7
  319.8 1.8 convolution_add_fusion.2
  321.6 2.2 convolution_add_fusion.1
  323.8 1.8 convolution_add_fusion
  325.6 2.5 pad_subtract_fusion
  328.1 1.0 constant_dynamic-update-slice_fusion.16
  329.1 1.3 slice.433
  330.4 6.7 %select_reduce_fusion.1 = f32[32,32,1024]{2,1,0:T(8,128)} fusion(f32[8,32,1024]{2,1,0:T(8,128)S(1)} %bitcast.169, pred[8,32,1024]{2,1,0:T(8,128)(4,1)S(1)} %copy-done.20), kind=kLoop, calls=%fused_computation.1 | loop fusion | flops 15728640 | bytes 5505024 | tf_op jit(solution)/shard_map/reduce_sum | solution.py:31
  337.1 4.4 %fusion.151 = f32[256,1024]{1,0:T(8,128)S(1)} fusion(f32[256,1024]{1,0:T(8,128)S(1)} %fusion.140, f32[1024,1024]{1,0:T(8,128)} %bitcast.165), kind=kOutput, calls=%fused_computation.271 | convolution fusion | flops 1610612736 | bytes 6291456 | tf_op jit(solution)/shard_map/dot_general | solution.py:14
  341.5 14.8 %select_reduce_fusion = f32[32,32,2048]{2,1,0:T(8,128)} fusion(f32[8,32,2048]{2,1,0:T(8,128)S(1)} %bitcast.168, pred[8,32,2048]{2,1,0:T(8,128)(4,1)S(1)} %copy-done.11), kind=kLoop, calls=%fused_computation | loop fusion | flops 31457280 | bytes 11010048 | tf_op jit(solution)/shard_map/reduce_sum | solution.py:31
  356.3 6.6 %fusion.150 = f32[256,2048]{1,0:T(8,128)S(1)} fusion(f32[256,1024]{1,0:T(8,128)S(1)} %fusion.140, f32[1024,2048]{1,0:T(8,128)} %bitcast.154), kind=kOutput, calls=%fused_computation.270 | convolution fusion | flops 3221225472 | bytes 11534336 | tf_op jit(solution)/shard_map/dot_general | solution.py:14
  363.0 2.4 fusion.112
  365.5 1.2 fusion.14
  366.7 1.1 convolution_subtract_fusion.7
  368.6 2.8 maximum_subtract_fusion
  (193 shorter events, 40.2 us)
Async XLA Ops:
  7.2 33.5 %copy-start.30 = (s32[8,8]{1,0:T(8,128)S(1)}, s32[8,8]{1,0:T(8,128)}, u32[]{:S(2)}) copy-start(s32[8,8]{1,0:T(8,128)} %param.12) | copy-start | bytes 772
  7.2 57.9 %all-gather.7.cloned.1.call-start = ((), (), s32[]{:S(2)}) async-start(), calls=%async_computation | async-start | bytes 4456448 | tf_op jit(solution)/shard_map/all_gather | solution.py:94
  9.4 110.6 %all-gather.9.cloned.1.call-start = ((), (), s32[]{:S(2)}) async-start(), calls=%async_computation.1 | async-start | bytes 4456448 | tf_op jit(solution)/shard_map/all_gather | solution.py:94
  10.2 165.9 %all-gather.11.cloned.1.call-start = ((), (), s32[]{:S(2)}) async-start(), calls=%async_computation.2 | async-start | bytes 4456448 | tf_op jit(solution)/shard_map/all_gather | solution.py:94
  10.9 223.2 %all-gather.13.cloned.1.call-start = ((), (), s32[]{:S(2)}) async-start(), calls=%async_computation.3 | async-start | bytes 4456448 | tf_op jit(solution)/shard_map/all_gather | solution.py:94
  11.5 317.7 %all-gather.15.cloned.1.call-start = ((), (), s32[]{:S(2)}) async-start(), calls=%async_computation.4 | async-start | bytes 4456448 | tf_op jit(solution)/shard_map/all_gather | solution.py:142
  148.0 0.7 copy-start.12
  204.4 83.1 %copy-start.25 = (f32[1,128,128]{2,1,0:T(8,128)S(1)}, f32[1,128,128]{2,1,0:T(8,128)}, u32[]{:S(2)}) copy-start(f32[1,128,128]{2,1,0:T(8,128)} %get-tuple-element.34) | copy-start | bytes 196612
  287.1 2.2 copy-start.26
  290.8 0.8 copy-start.21
  290.9 0.9 copy-start.22
  291.3 6.7 %copy-start.17 = (f32[1,512,512]{2,1,0:T(8,128)}, f32[1,512,512]{2,1,0:T(8,128)S(1)}, u32[]{:S(2)}) copy-start(f32[1,512,512]{2,1,0:T(8,128)S(1)} %get-tuple-element.29) | copy-start | bytes 3145732
  291.3 24.7 %copy-start.15 = (f32[1,512,512]{2,1,0:T(8,128)}, f32[1,512,512]{2,1,0:T(8,128)S(1)}, u32[]{:S(2)}) copy-start(f32[1,512,512]{2,1,0:T(8,128)S(1)} %get-tuple-element.28) | copy-start | bytes 3145732
  291.8 2.1 copy-start.23
  291.8 2.1 copy-start.29
  291.8 2.3 copy-start.24
  293.7 2.4 copy-start.5
  296.1 20.0 %copy-start.13 = (f32[1,512,512]{2,1,0:T(8,128)}, f32[1,512,512]{2,1,0:T(8,128)S(1)}, u32[]{:S(2)}) copy-start(f32[1,512,512]{2,1,0:T(8,128)S(1)} %fusion.12) | copy-start | bytes 3145732
  298.0 13.7 %copy-start.7 = (f32[256,1024]{1,0:T(8,128)}, f32[256,1024]{1,0:T(8,128)S(1)}, u32[]{:S(2)}) copy-start(f32[256,1024]{1,0:T(8,128)S(1)} %fusion.11) | copy-start | bytes 3145732
  298.0 2.6 copy-start.1
  300.6 2.2 copy-start.2
  302.8 2.2 copy-start.3
  305.0 2.2 copy-start.4
  309.0 3.8 copy-start
  312.8 3.3 copy-start.18
  316.1 12.0 %copy-start.9 = (f32[256,1024]{1,0:T(8,128)}, f32[256,1024]{1,0:T(8,128)S(1)}, u32[]{:S(2)}) copy-start(f32[256,1024]{1,0:T(8,128)S(1)} %fusion.18) | copy-start | bytes 3145732
  328.1 2.3 copy-start.20
  337.1 4.4 %slice-start = ((f32[256,4096]{1,0:T(8,128)}), f32[256,2048]{1,0:T(8,128)S(1)}, s32[]{:S(2)}) async-start(f32[256,4096]{1,0:T(8,128)} %all-gather.15.cloned.1.call-done), calls=%async_computation.5 | async-start | bytes 4194304 | tf_op jit(solution)/shard_map/slice | solution.py:153
  337.1 4.4 %copy-start.11 = (pred[8,32,2048]{2,1,0:T(8,128)(4,1)S(1)}, pred[8,32,2048]{2,1,0:T(8,128)(4,1)}, u32[]{:S(2)}) copy-start(pred[8,32,2048]{2,1,0:T(8,128)(4,1)} %iota_compare_fusion.2) | copy-start | bytes 1572868
  356.3 6.6 %copy-start.14 = (f32[1,512,512]{2,1,0:T(8,128)S(1)}, f32[1,512,512]{2,1,0:T(8,128)}, u32[]{:S(2)}) copy-start(f32[1,512,512]{2,1,0:T(8,128)} %copy-done.13) | copy-start | bytes 3145732
  356.3 6.6 %copy-start.16 = (f32[1,512,512]{2,1,0:T(8,128)S(1)}, f32[1,512,512]{2,1,0:T(8,128)}, u32[]{:S(2)}) copy-start(f32[1,512,512]{2,1,0:T(8,128)} %copy-done.15) | copy-start | bytes 3145732
  356.3 6.6 %copy-start.19 = (f32[1,512,512]{2,1,0:T(8,128)S(1)}, f32[1,512,512]{2,1,0:T(8,128)}, u32[]{:S(2)}) copy-start(f32[1,512,512]{2,1,0:T(8,128)} %copy-done.17) | copy-start | bytes 3145732
  362.9 2.6 copy-start.8
  362.9 2.6 copy-start.27
  363.0 3.7 copy-start.10
  363.0 3.7 copy-start.28
  363.0 4.8 %copy-start.31 = (f32[16,16]{1,0:T(8,128)S(1)}, f32[16,16]{1,0:T(8,128)}, u32[]{:S(2)}) copy-start(f32[16,16]{1,0:T(8,128)} %param.16) | copy-start | bytes 3076
  363.0 5.6 %copy-start.6 = (f32[256,4096]{1,0:T(8,128)S(1)}, f32[256,4096]{1,0:T(8,128)}, u32[]{:S(2)}) copy-start(f32[256,4096]{1,0:T(8,128)} %param.13) | copy-start | bytes 12582916
Sparse Core Ops, SparseCore 0:
  10.7 54.2 all-gather.6
  67.2 49.3 all-gather.8
  118.8 50.0 all-gather.10
  170.9 49.8 all-gather.12
  222.7 52.5 all-gather.14

commit v9 on v8

--- a/solution.py
+++ b/solution.py
@@ -103,19 +103,20 @@
         offset = k * block - bounds[chunk]
         panel = chunks[chunk][k * block:factored, offset:offset + block]
         if k:
-            done = jnp.concatenate([col[k * block:] for col in columns], axis=1)
+            done = jnp.concatenate(
+                [col[(k - j) * block:] for j, col in enumerate(columns)], axis=1
+            )
             panel = panel - tdot(done, done[:block])
         diagonal = jnp.linalg.cholesky(panel[:block], symmetrize_input=False)
         diagonal_inverse = jax.scipy.linalg.solve_triangular(
             diagonal, jnp.eye(block, dtype=jnp.float32), lower=True
         )
         under = tdot(panel[block:], diagonal_inverse)
-        column = jnp.concatenate(
-            [jnp.zeros((k * block, block), jnp.float32), diagonal, under], axis=0
-        )
-        columns.append(column)
+        columns.append(jnp.concatenate([diagonal, under], axis=0))
         block_inverses.append(diagonal_inverse)
-    head_factor = jnp.concatenate(columns, axis=1)
+    head_factor = jnp.concatenate(
+        [jnp.pad(col, ((j * block, 0), (0, 0))) for j, col in enumerate(columns)], axis=1
+    )
     head_inverse = invert_lower(head_factor, block_inverses)
 
     def minus_below(scaled):

time: 385 us -> 385 us (level)
    unnamed x79 -> x81, local copies, waits for them, and re-layouts: 14.2 us -> 12.7 us
where the time goes in v9:
time: 385 us; the launch traced here: 379 us
  other arithmetic  232 us (60%)
  matrix products  69.2 us (18%)
  local copies, waits for them, and re-layouts  28.9 us (8%)
  blocking collectives  25 us (6%)
  between operations  15 us (4%)
  waiting for transfers between devices  8.86 us (2%)
    another operation x24, other arithmetic, on_device(): diagonal = jnp.linalg.cholesky(panel[:block], symmetrize_input=False)  100 us
    another operation x16, other arithmetic, on_device(): jax.scipy.linalg.solve_triangular(diagonal, jnp.eye(block, dtype=jnp.floa...  87.7 us
    dot_general x28, matrix products, tdot(): lax.dot_general(left, right, (((1,), (1,)), ((), ())), precision=precisio...  44.9 us
    reduce_sum x3, other arithmetic, assemble_t(): dense = jnp.where(hit, flipped, 0.0).sum(axis=0)  29.8 us
    all_gather x1, blocking collectives, on_device(): gathered = lax.all_gather(packed, 'row', axis=0)  25 us
    dot_general x4, matrix products, mdot(): jnp.dot(left, right, precision=precision, preferred_element_type=jnp.floa...  15 us
    unnamed x81, local copies, waits for them, and re-layouts  12.7 us
  transfers between devices with their start and end apart: 5, of which 1 were waited for; matrix products, arithmetic and copies ran while one was open for 75% of the time, Pallas kernels for 0%

profile of v9, /device:TPU:0, one launch (start us, length us, event | category | flops | bytes accessed | tf_op | source)
XLA Modules:
  0.0 378.9 jit_solution(7832371087122037537)
XLA Ops:
  7.2 2.2 fusion.138
  11.5 1.8 copy.129
  15.0 25.0 %all-gather = f32[384,256]{1,0:T(8,128)S(1)} all-gather(f32[24,256]{1,0:T(8,128)S(1)} %fusion.117), channel_id=2, replica_groups=mesh['hyper'=2,'row'=16] {'row'}, dimensions={0}, use_global_device_ids=true | all-gather | bytes 417792 | tf_op jit(solution)/shard_map/all_gather | solution.py:81
  40.5 8.3 %select_reduce_fusion.2 = f32[128,32,256]{2,1,0:T(8,128)} fusion(f32[8,32,256]{2,1,0:T(8,128)} %bitcast.171, pred[8,128,256]{2,1,0:T(8,128)(4,1)S(1)} %iota_compare_fusion.5), kind=kLoop, calls=%fused_computation.2 | loop fusion | flops 15728640 | bytes 4718592 | tf_op jit(solution)/shard_map/reduce_sum | solution.py:31
  48.8 5.9 %copy.130 = f32[4096,256]{0,1:T(8,128)} copy(f32[4096,256]{1,0:T(8,128)} %bitcast.166) | data formatting | bytes 8388608 | tf_op jit(solution)/shard_map/reshape | solution.py:32
  56.3 1.2 iota_compare_fusion.2
  58.2 6.9 %all-gather.7.cloned.1.call-done = f32[4096,256]{1,0:T(8,128)} async-done(((f32[256,256]{1,0:T(8,128)}), f32[4096,256]{1,0:T(8,128)}) %all-gather.7.cloned.1.call-update) | async-done | bytes 4194320 | tf_op jit(solution)/shard_map/all_gather | solution.py:94
  66.0 11.7 %cholesky.135 = f32[128,128]{1,0:T(8,128)S(1)} custom-call(f32[128,128]{1,0:T(8,128)S(1)} %slice.374), custom_call_target="Cholesky" | custom-call | tf_op jit(solution)/shard_map/jit(cholesky)/cholesky | solution.py:110
  79.0 9.8 %custom-call.12 = f32[1,128,128]{1,2,0:T(8,128)S(1)} custom-call(f32[1,128,128]{2,1,0:T(8,128)S(1)} %get-tuple-element.22), custom_call_target="InvertDiagBlocksLowerTriangular" | custom-call | tf_op jit(solution)/shard_map/jit(_solve_triangular)/triangular_solve | solution.py:111
  89.1 1.6 fusion.42
  92.4 2.0 convolution_subtract_fusion
  94.3 12.2 %cholesky.146 = f32[128,128]{1,0:T(8,128)S(1)} custom-call(f32[128,128]{1,0:T(8,128)S(1)} %slice.378), custom_call_target="Cholesky" | custom-call | tf_op jit(solution)/shard_map/jit(cholesky)/cholesky | solution.py:110
  107.9 9.8 %custom-call.13 = f32[1,128,128]{1,2,0:T(8,128)S(1)} custom-call(f32[1,128,128]{2,1,0:T(8,128)S(1)} %get-tuple-element.20), custom_call_target="InvertDiagBlocksLowerTriangular" | custom-call | tf_op jit(solution)/shard_map/jit(_solve_triangular)/triangular_solve | solution.py:111
  119.9 1.8 convolution_subtract_fusion.1
  121.7 11.7 %cholesky.157 = f32[128,128]{1,0:T(8,128)S(1)} custom-call(f32[128,128]{1,0:T(8,128)S(1)} %slice.382), custom_call_target="Cholesky" | custom-call | tf_op jit(solution)/shard_map/jit(cholesky)/cholesky | solution.py:110
  134.1 1.3 select_bitcast_fusion.5
  135.4 9.8 %custom-call.14 = f32[1,128,128]{1,2,0:T(8,128)S(1)} custom-call(f32[1,128,128]{2,1,0:T(8,128)S(1)} %get-tuple-element.18), custom_call_target="InvertDiagBlocksLowerTriangular" | custom-call | tf_op jit(solution)/shard_map/jit(_solve_triangular)/triangular_solve | solution.py:111
  146.6 2.0 convolution_subtract_fusion.2
  149.3 11.9 %cholesky.168 = f32[128,128]{1,0:T(8,128)S(1)} custom-call(f32[128,128]{1,0:T(8,128)S(1)} %slice.387), custom_call_target="Cholesky" | custom-call | tf_op jit(solution)/shard_map/jit(cholesky)/cholesky | solution.py:110
  161.8 1.3 select_bitcast_fusion.4
  163.1 9.8 %custom-call.15 = f32[1,128,128]{1,2,0:T(8,128)S(1)} custom-call(f32[1,128,128]{2,1,0:T(8,128)S(1)} %get-tuple-element.16), custom_call_target="InvertDiagBlocksLowerTriangular" | custom-call | tf_op jit(solution)/shard_map/jit(_solve_triangular)/triangular_solve | solution.py:111
  173.2 1.3 fusion.67
  177.3 1.9 convolution_subtract_fusion.3
  179.3 11.7 %cholesky.179 = f32[128,128]{1,0:T(8,128)S(1)} custom-call(f32[128,128]{1,0:T(8,128)S(1)} %slice.393), custom_call_target="Cholesky" | custom-call | tf_op jit(solution)/shard_map/jit(cholesky)/cholesky | solution.py:110
  191.7 1.3 select_bitcast_fusion.3
  193.0 10.0 %custom-call.16 = f32[1,128,128]{1,2,0:T(8,128)S(1)} custom-call(f32[1,128,128]{2,1,0:T(8,128)S(1)} %get-tuple-element.14), custom_call_target="InvertDiagBlocksLowerTriangular" | custom-call | tf_op jit(solution)/shard_map/jit(_solve_triangular)/triangular_solve | solution.py:111
  204.3 2.3 convolution_subtract_fusion.4
  206.6 11.7 %cholesky.190 = f32[128,128]{1,0:T(8,128)S(1)} custom-call(f32[128,128]{1,0:T(8,128)S(1)} %slice.401), custom_call_target="Cholesky" | custom-call | tf_op jit(solution)/shard_map/jit(cholesky)/cholesky | solution.py:110
  219.0 1.3 select_bitcast_fusion.2
  220.3 9.8 %custom-call.17 = f32[1,128,128]{1,2,0:T(8,128)S(1)} custom-call(f32[1,128,128]{2,1,0:T(8,128)S(1)} %get-tuple-element.12), custom_call_target="InvertDiagBlocksLowerTriangular" | custom-call | tf_op jit(solution)/shard_map/jit(_solve_triangular)/triangular_solve | solution.py:111
  234.1 1.7 convolution_subtract_fusion.5
  235.8 12.1 %cholesky.201 = f32[128,128]{1,0:T(8,128)S(1)} custom-call(f32[128,128]{1,0:T(8,128)S(1)} %slice.410), custom_call_target="Cholesky" | custom-call | tf_op jit(solution)/shard_map/jit(cholesky)/cholesky | solution.py:110
  248.6 1.3 select_bitcast_fusion.1
  249.9 9.8 %custom-call.18 = f32[1,128,128]{1,2,0:T(8,128)S(1)} custom-call(f32[1,128,128]{2,1,0:T(8,128)S(1)} %get-tuple-element.10), custom_call_target="InvertDiagBlocksLowerTriangular" | custom-call | tf_op jit(solution)/shard_map/jit(_solve_triangular)/triangular_solve | solution.py:111
  261.5 1.8 convolution_subtract_fusion.6
  263.3 11.7 %cholesky.212 = f32[128,128]{1,0:T(8,128)S(1)} custom-call(f32[128,128]{1,0:T(8,128)S(1)} %convolution_subtract_fusion.6), custom_call_target="Cholesky" | custom-call | tf_op jit(solution)/shard_map/jit(cholesky)/cholesky | solution.py:110
  275.7 1.3 select_bitcast_fusion
  277.0 9.8 %custom-call.19 = f32[1,128,128]{1,2,0:T(8,128)S(1)} custom-call(f32[1,128,128]{2,1,0:T(8,128)S(1)} %get-tuple-element.8), custom_call_target="InvertDiagBlocksLowerTriangular" | custom-call | tf_op jit(solution)/shard_map/jit(_solve_triangular)/triangular_solve | solution.py:111
  287.2 1.4 fusion.69
  293.0 1.9 fusion.17
  295.0 1.9 fusion.12
  296.8 1.9 fusion.11
  298.8 2.0 fusion.135
  301.4 1.7 fusion.9
  303.6 2.0 convolution_add_fusion.5
  305.7 1.8 convolution_add_fusion.4
  307.9 1.8 convolution_add_fusion.3
  309.8 2.7 subtract_select_fusion
  313.5 3.2 fusion.15
  316.8 2.0 fusion.132
  318.8 1.7 fusion.7
  320.6 1.8 convolution_add_fusion.2
  322.3 2.2 convolution_add_fusion.1
  324.5 1.8 convolution_add_fusion
  326.4 2.5 pad_subtract_fusion
  329.9 1.3 slice.440
  331.2 6.7 %select_reduce_fusion.1 = f32[32,32,1024]{2,1,0:T(8,128)} fusion(f32[8,32,1024]{2,1,0:T(8,128)S(1)} %bitcast.169, pred[8,32,1024]{2,1,0:T(8,128)(4,1)S(1)} %copy-done.21), kind=kLoop, calls=%fused_computation.1 | loop fusion | flops 15728640 | bytes 5505024 | tf_op jit(solution)/shard_map/reduce_sum | solution.py:31
  337.9 4.4 %fusion.143 = f32[256,1024]{1,0:T(8,128)S(1)} fusion(f32[256,1024]{1,0:T(8,128)S(1)} %fusion.132, f32[1024,1024]{1,0:T(8,128)} %bitcast.165), kind=kOutput, calls=%fused_computation.269 | convolution fusion | flops 1610612736 | bytes 6291456 | tf_op jit(solution)/shard_map/dot_general | solution.py:14
  342.3 14.8 %select_reduce_fusion = f32[32,32,2048]{2,1,0:T(8,128)} fusion(f32[8,32,2048]{2,1,0:T(8,128)S(1)} %bitcast.168, pred[8,32,2048]{2,1,0:T(8,128)(4,1)S(1)} %copy-done.12), kind=kLoop, calls=%fused_computation | loop fusion | flops 31457280 | bytes 11010048 | tf_op jit(solution)/shard_map/reduce_sum | solution.py:31
  357.1 6.6 %fusion.142 = f32[256,2048]{1,0:T(8,128)S(1)} fusion(f32[256,1024]{1,0:T(8,128)S(1)} %fusion.132, f32[1024,2048]{1,0:T(8,128)} %bitcast.154), kind=kOutput, calls=%fused_computation.268 | convolution fusion | flops 3221225472 | bytes 11534336 | tf_op jit(solution)/shard_map/dot_general | solution.py:14
  363.8 2.4 fusion.104
  366.3 1.2 fusion.14
  367.4 1.1 convolution_subtract_fusion.7
  369.3 2.8 maximum_subtract_fusion
  (188 shorter events, 39.7 us)
Async XLA Ops:
  7.2 32.9 %copy-start.31 = (s32[8,8]{1,0:T(8,128)S(1)}, s32[8,8]{1,0:T(8,128)}, u32[]{:S(2)}) copy-start(s32[8,8]{1,0:T(8,128)} %param.12) | copy-start | bytes 772
  7.2 57.9 %all-gather.7.cloned.1.call-start = ((), (), s32[]{:S(2)}) async-start(), calls=%async_computation | async-start | bytes 4456448 | tf_op jit(solution)/shard_map/all_gather | solution.py:94
  9.4 110.5 %all-gather.9.cloned.1.call-start = ((), (), s32[]{:S(2)}) async-start(), calls=%async_computation.1 | async-start | bytes 4456448 | tf_op jit(solution)/shard_map/all_gather | solution.py:94
  10.2 167.1 %all-gather.11.cloned.1.call-start = ((), (), s32[]{:S(2)}) async-start(), calls=%async_computation.2 | async-start | bytes 4456448 | tf_op jit(solution)/shard_map/all_gather | solution.py:94
  10.9 223.2 %all-gather.13.cloned.1.call-start = ((), (), s32[]{:S(2)}) async-start(), calls=%async_computation.3 | async-start | bytes 4456448 | tf_op jit(solution)/shard_map/all_gather | solution.py:94
  11.5 318.4 %all-gather.15.cloned.1.call-start = ((), (), s32[]{:S(2)}) async-start(), calls=%async_computation.4 | async-start | bytes 4456448 | tf_op jit(solution)/shard_map/all_gather | solution.py:143
  148.6 0.7 copy-start.13
  179.3 53.6 %copy-start.11 = (f32[256,768]{1,0:T(8,128)S(1)}, f32[256,768]{1,0:T(8,128)}, u32[]{:S(2)}) copy-start(f32[256,768]{1,0:T(8,128)} %slice_dynamic-update-slice_fusion.5) | copy-start | bytes 2359300
  234.1 53.1 %copy-start.26 = (f32[1,128,128]{2,1,0:T(8,128)S(1)}, f32[1,128,128]{2,1,0:T(8,128)}, u32[]{:S(2)}) copy-start(f32[1,128,128]{2,1,0:T(8,128)} %get-tuple-element.42) | copy-start | bytes 196612
  286.8 2.6 copy-start.28
  287.2 3.3 copy-start.27
  289.2 1.4 copy-start.22
  289.3 1.4 copy-start.23
  292.1 0.8 copy-start.24
  292.4 2.5 copy-start.25
  292.6 6.2 %copy-start.18 = (f32[1,512,512]{2,1,0:T(8,128)}, f32[1,512,512]{2,1,0:T(8,128)S(1)}, u32[]{:S(2)}) copy-start(f32[1,512,512]{2,1,0:T(8,128)S(1)} %get-tuple-element.29) | copy-start | bytes 3145732
  292.6 24.2 %copy-start.16 = (f32[1,512,512]{2,1,0:T(8,128)}, f32[1,512,512]{2,1,0:T(8,128)S(1)}, u32[]{:S(2)}) copy-start(f32[1,512,512]{2,1,0:T(8,128)S(1)} %get-tuple-element.28) | copy-start | bytes 3145732
  293.0 3.9 %copy-start.5 = (f32[256,4096]{1,0:T(8,128)S(1)}, f32[256,4096]{1,0:T(8,128)}, u32[]{:S(2)}) copy-start(f32[256,4096]{1,0:T(8,128)} %param.10) | copy-start | bytes 12582916
  296.8 20.0 %copy-start.14 = (f32[1,512,512]{2,1,0:T(8,128)}, f32[1,512,512]{2,1,0:T(8,128)S(1)}, u32[]{:S(2)}) copy-start(f32[1,512,512]{2,1,0:T(8,128)S(1)} %fusion.12) | copy-start | bytes 3145732
  298.8 13.7 %copy-start.7 = (f32[256,1024]{1,0:T(8,128)}, f32[256,1024]{1,0:T(8,128)S(1)}, u32[]{:S(2)}) copy-start(f32[256,1024]{1,0:T(8,128)S(1)} %fusion.11) | copy-start | bytes 3145732
  298.8 2.6 copy-start.1
  301.4 2.2 copy-start.2
  303.6 2.2 copy-start.3
  305.7 2.2 copy-start.4
  309.8 3.8 copy-start
  313.5 3.3 copy-start.19
  316.8 12.0 %copy-start.9 = (f32[256,1024]{1,0:T(8,128)}, f32[256,1024]{1,0:T(8,128)S(1)}, u32[]{:S(2)}) copy-start(f32[256,1024]{1,0:T(8,128)S(1)} %fusion.15) | copy-start | bytes 3145732
  328.8 2.3 copy-start.21
  337.9 4.4 %slice-start = ((f32[256,4096]{1,0:T(8,128)}), f32[256,2048]{1,0:T(8,128)S(1)}, s32[]{:S(2)}) async-start(f32[256,4096]{1,0:T(8,128)} %all-gather.15.cloned.1.call-done), calls=%async_computation.5 | async-start | bytes 4194304 | tf_op jit(solution)/shard_map/slice | solution.py:154
  337.9 4.4 %copy-start.12 = (pred[8,32,2048]{2,1,0:T(8,128)(4,1)S(1)}, pred[8,32,2048]{2,1,0:T(8,128)(4,1)}, u32[]{:S(2)}) copy-start(pred[8,32,2048]{2,1,0:T(8,128)(4,1)} %iota_compare_fusion.2) | copy-start | bytes 1572868
  357.1 6.6 %copy-start.15 = (f32[1,512,512]{2,1,0:T(8,128)S(1)}, f32[1,512,512]{2,1,0:T(8,128)}, u32[]{:S(2)}) copy-start(f32[1,512,512]{2,1,0:T(8,128)} %copy-done.14) | copy-start | bytes 3145732
  357.1 6.6 %copy-start.17 = (f32[1,512,512]{2,1,0:T(8,128)S(1)}, f32[1,512,512]{2,1,0:T(8,128)}, u32[]{:S(2)}) copy-start(f32[1,512,512]{2,1,0:T(8,128)} %copy-done.16) | copy-start | bytes 3145732
  357.1 6.6 %copy-start.20 = (f32[1,512,512]{2,1,0:T(8,128)S(1)}, f32[1,512,512]{2,1,0:T(8,128)}, u32[]{:S(2)}) copy-start(f32[1,512,512]{2,1,0:T(8,128)} %copy-done.18) | copy-start | bytes 3145732
  363.7 2.6 copy-start.8
  363.7 2.6 copy-start.29
  363.7 3.7 copy-start.10
  363.7 3.7 copy-start.30
  363.8 4.8 %copy-start.32 = (f32[16,16]{1,0:T(8,128)S(1)}, f32[16,16]{1,0:T(8,128)}, u32[]{:S(2)}) copy-start(f32[16,16]{1,0:T(8,128)} %param.16) | copy-start | bytes 3076
  363.8 5.6 %copy-start.6 = (f32[256,4096]{1,0:T(8,128)S(1)}, f32[256,4096]{1,0:T(8,128)}, u32[]{:S(2)}) copy-start(f32[256,4096]{1,0:T(8,128)} %param.13) | copy-start | bytes 12582916
Sparse Core Ops, SparseCore 0:
  10.7 54.3 all-gather.6
  67.3 49.2 all-gather.8
  118.7 49.6 all-gather.10
  170.4 49.4 all-gather.12
  221.9 52.0 all-gather.14

commit v10 on v8

--- a/solution.py
+++ b/solution.py
@@ -68,22 +68,16 @@
     fixed_cols = fixed_rows.shape[1]
     block = min(BLOCK, rows)
     cols_count = local_block_rows * nonzero
-    lanes = max(value_cols, fixed_cols, cols_count)
+    lanes = max(value_rows, fixed_cols, cols_count)
 
     def widen(part):
         return jnp.pad(part, ((0, 0), (0, lanes - part.shape[1])))
 
     values_t = coupling_values.T
     cols_row = block_cols.reshape(1, cols_count).astype(jnp.float32)
-    packed = jnp.concatenate([widen(fixed_rows), widen(cols_row)], axis=0)
+    packed = jnp.concatenate([widen(values_t), widen(fixed_rows), widen(cols_row)], axis=0)
     pad = (-packed.shape[0]) % 8
     packed = jnp.concatenate([packed, jnp.zeros((pad, lanes), jnp.float32)], axis=0)
-    gathered = lax.all_gather(packed, "row", axis=0)
-    devices = gathered.shape[0]
-    all_fixed = gathered[:, :fixed_count, :fixed_cols].transpose(1, 0, 2)
-    all_fixed = all_fixed.reshape(fixed_count, devices * fixed_cols)
-    all_block_cols = gathered[:, fixed_count, :cols_count]
-    all_block_cols = jnp.round(all_block_cols).astype(jnp.int32).reshape(-1, nonzero)
 
     blocks = factored // block
     widths = [rows // block] * PANELS
@@ -139,7 +133,14 @@
     coupled_updates = jnp.pad(minus_below(coupled_scaled), ((0, 0), (factored, 0)))
     coupling_factor = lax.dynamic_update_slice(coupled - coupled_updates, coupled_panel, (0, 0))
 
-    all_values_t = lax.all_gather(values_t, "row", axis=1, tiled=True)
+    gathered = lax.all_gather(packed, "row", axis=1, tiled=True)
+    devices = gathered.shape[1] // lanes
+    gathered = gathered.reshape(gathered.shape[0], devices, lanes)
+    all_values_t = gathered[:value_cols, :, :value_rows].reshape(value_cols, devices * value_rows)
+    all_fixed = gathered[value_cols:value_cols + fixed_count, :, :fixed_cols]
+    all_fixed = all_fixed.reshape(fixed_count, devices * fixed_cols)
+    all_block_cols = gathered[value_cols + fixed_count, :, :cols_count]
+    all_block_cols = jnp.round(all_block_cols).astype(jnp.int32).reshape(-1, nonzero)
     all_blocks = size // width
     head_blocks = factored // width
     near_end = min(head_blocks + REACH, all_blocks)

time: 385 us -> 395 us (1.026)
  waiting for transfers between devices: 8.25 us -> 37.4 us
  blocking collectives: 25 us -> 0 us
    all_gather x4, waiting for transfers between devices: 6.32 us -> 35.4 us  [on_device(): lax.all_gather(carried_block[:, lo:hi], 'row', axis=0, tiled=True)]
    all_gather x1 -> x0, blocking collectives: 25 us -> none  [on_device(): gathered = lax.all_gather(packed, 'row', axis=0)]
    unnamed x79 -> x114, local copies, waits for them, and re-layouts: 14.2 us -> 16.1 us
  transfers between devices with their start and end apart: 5 -> 5, of which waited for: 1 -> 1; matrix products, arithmetic and copies ran while one was open for 75% -> 72% of each run, Pallas kernels for 0% -> 0%
where the time goes in v10:
time: 395 us; the launch traced here: 389 us
  other arithmetic  231 us (58%)
  matrix products  70.5 us (18%)
  waiting for transfers between devices  37.4 us (9%)
  local copies, waits for them, and re-layouts  34.8 us (9%)
  between operations  15.5 us (4%)
    another operation x24, other arithmetic, on_device(): diagonal = jnp.linalg.cholesky(panel[:block], symmetrize_input=False)  99.7 us
    another operation x16, other arithmetic, on_device(): jax.scipy.linalg.solve_triangular(diagonal, jnp.eye(block, dtype=jnp.floa...  85.9 us
    dot_general x28, matrix products, tdot(): lax.dot_general(left, right, (((1,), (1,)), ((), ())), precision=precisio...  45.4 us
    all_gather x4, waiting for transfers between devices, on_device(): lax.all_gather(carried_block[:, lo:hi], 'row', axis=0, tiled=True)  35.4 us
    reduce_sum x3, other arithmetic, assemble_t(): dense = jnp.where(hit, flipped, 0.0).sum(axis=0)  28.3 us
    unnamed x114, local copies, waits for them, and re-layouts  16.1 us
    dot_general x4, matrix products, mdot(): jnp.dot(left, right, precision=precision, preferred_element_type=jnp.floa...  15.6 us
  transfers between devices with their start and end apart: 5, of which 1 were waited for; matrix products, arithmetic and copies ran while one was open for 72% of the time, Pallas kernels for 0%

profile of v10, /device:TPU:0, one launch (start us, length us, event | category | flops | bytes accessed | tf_op | source)
XLA Modules:
  0.0 389.2 jit_solution(4830681710359560791)
XLA Ops:
  7.2 2.2 fusion.147
  11.5 1.1 copy.129
  13.5 1.5 fusion.56
  16.0 6.8 %select_reduce_fusion.2 = f32[128,32,256]{2,1,0:T(8,128)} fusion(f32[8,32,256]{2,1,0:T(8,128)S(1)} %bitcast.164, pred[8,128,256]{2,1,0:T(8,128)(4,1)S(1)} %iota_compare_fusion.5), kind=kLoop, calls=%fused_computation.2 | loop fusion | flops 15728640 | bytes 4718592 | tf_op jit(solution)/shard_map/reduce_sum | solution.py:31
  22.8 5.7 %copy.130 = f32[4096,256]{0,1:T(8,128)} copy(f32[4096,256]{1,0:T(8,128)} %bitcast.156) | data formatting | bytes 8388608 | tf_op jit(solution)/shard_map/reshape | solution.py:32
  28.6 35.4 %all-gather.6.cloned.1.call-done = f32[4096,256]{1,0:T(8,128)} async-done(((f32[256,256]{1,0:T(8,128)}), f32[4096,256]{1,0:T(8,128)}) %all-gather.6.cloned.1.call-update) | async-done | bytes 4194320 | tf_op jit(solution)/shard_map/all_gather | solution.py:88
  64.9 11.7 %cholesky.135 = f32[128,128]{1,0:T(8,128)S(1)} custom-call(f32[128,128]{1,0:T(8,128)S(1)} %slice.370), custom_call_target="Cholesky" | custom-call | tf_op jit(solution)/shard_map/jit(cholesky)/cholesky | solution.py:102
  78.0 9.8 %custom-call.12 = f32[1,128,128]{1,2,0:T(8,128)S(1)} custom-call(f32[1,128,128]{2,1,0:T(8,128)S(1)} %get-tuple-element.22), custom_call_target="InvertDiagBlocksLowerTriangular" | custom-call | tf_op jit(solution)/shard_map/jit(_solve_triangular)/triangular_solve | solution.py:103
  88.1 1.6 fusion.48
  90.6 1.9 convolution_subtract_fusion
  92.6 11.7 %cholesky.146 = f32[128,128]{1,0:T(8,128)S(1)} custom-call(f32[128,128]{1,0:T(8,128)S(1)} %slice.374), custom_call_target="Cholesky" | custom-call | tf_op jit(solution)/shard_map/jit(cholesky)/cholesky | solution.py:102
  105.6 10.0 %custom-call.13 = f32[1,128,128]{1,2,0:T(8,128)S(1)} custom-call(f32[1,128,128]{2,1,0:T(8,128)S(1)} %get-tuple-element.20), custom_call_target="InvertDiagBlocksLowerTriangular" | custom-call | tf_op jit(solution)/shard_map/jit(_solve_triangular)/triangular_solve | solution.py:103
  118.6 1.8 convolution_subtract_fusion.1
  120.4 11.7 %cholesky.157 = f32[128,128]{1,0:T(8,128)S(1)} custom-call(f32[128,128]{1,0:T(8,128)S(1)} %slice.378), custom_call_target="Cholesky" | custom-call | tf_op jit(solution)/shard_map/jit(cholesky)/cholesky | solution.py:102
  133.5 9.8 %custom-call.14 = f32[1,128,128]{1,2,0:T(8,128)S(1)} custom-call(f32[1,128,128]{2,1,0:T(8,128)S(1)} %get-tuple-element.18), custom_call_target="InvertDiagBlocksLowerTriangular" | custom-call | tf_op jit(solution)/shard_map/jit(_solve_triangular)/triangular_solve | solution.py:103
  144.1 2.0 convolution_subtract_fusion.2
  146.8 12.1 %cholesky.168 = f32[128,128]{1,0:T(8,128)S(1)} custom-call(f32[128,128]{1,0:T(8,128)S(1)} %slice.383), custom_call_target="Cholesky" | custom-call | tf_op jit(solution)/shard_map/jit(cholesky)/cholesky | solution.py:102
  160.2 9.8 %custom-call.15 = f32[1,128,128]{1,2,0:T(8,128)S(1)} custom-call(f32[1,128,128]{2,1,0:T(8,128)S(1)} %get-tuple-element.16), custom_call_target="InvertDiagBlocksLowerTriangular" | custom-call | tf_op jit(solution)/shard_map/jit(_solve_triangular)/triangular_solve | solution.py:103
  170.3 1.3 fusion.77
  173.7 1.9 convolution_subtract_fusion.3
  175.7 11.7 %cholesky.179 = f32[128,128]{1,0:T(8,128)S(1)} custom-call(f32[128,128]{1,0:T(8,128)S(1)} %slice.389), custom_call_target="Cholesky" | custom-call | tf_op jit(solution)/shard_map/jit(cholesky)/cholesky | solution.py:102
  188.7 9.9 %custom-call.16 = f32[1,128,128]{1,2,0:T(8,128)S(1)} custom-call(f32[1,128,128]{2,1,0:T(8,128)S(1)} %get-tuple-element.14), custom_call_target="InvertDiagBlocksLowerTriangular" | custom-call | tf_op jit(solution)/shard_map/jit(_solve_triangular)/triangular_solve | solution.py:103
  202.0 2.3 convolution_subtract_fusion.4
  204.4 11.7 %cholesky.190 = f32[128,128]{1,0:T(8,128)S(1)} custom-call(f32[128,128]{1,0:T(8,128)S(1)} %slice.397), custom_call_target="Cholesky" | custom-call | tf_op jit(solution)/shard_map/jit(cholesky)/cholesky | solution.py:102
  216.8 1.3 select_bitcast_fusion.2
  218.0 9.8 %custom-call.17 = f32[1,128,128]{1,2,0:T(8,128)S(1)} custom-call(f32[1,128,128]{2,1,0:T(8,128)S(1)} %get-tuple-element.12), custom_call_target="InvertDiagBlocksLowerTriangular" | custom-call | tf_op jit(solution)/shard_map/jit(_solve_triangular)/triangular_solve | solution.py:103
  238.2 1.7 convolution_subtract_fusion.5
  239.9 11.9 %cholesky.201 = f32[128,128]{1,0:T(8,128)S(1)} custom-call(f32[128,128]{1,0:T(8,128)S(1)} %slice.406), custom_call_target="Cholesky" | custom-call | tf_op jit(solution)/shard_map/jit(cholesky)/cholesky | solution.py:102
  252.5 1.3 select_bitcast_fusion.1
  253.8 9.8 %custom-call.18 = f32[1,128,128]{1,2,0:T(8,128)S(1)} custom-call(f32[1,128,128]{2,1,0:T(8,128)S(1)} %get-tuple-element.10), custom_call_target="InvertDiagBlocksLowerTriangular" | custom-call | tf_op jit(solution)/shard_map/jit(_solve_triangular)/triangular_solve | solution.py:103
  264.8 1.8 convolution_subtract_fusion.6
  266.6 11.7 %cholesky.212 = f32[128,128]{1,0:T(8,128)S(1)} custom-call(f32[128,128]{1,0:T(8,128)S(1)} %convolution_subtract_fusion.6), custom_call_target="Cholesky" | custom-call | tf_op jit(solution)/shard_map/jit(cholesky)/cholesky | solution.py:102
  279.0 1.3 select_bitcast_fusion
  280.3 9.8 %custom-call.19 = f32[1,128,128]{1,2,0:T(8,128)S(1)} custom-call(f32[1,128,128]{2,1,0:T(8,128)S(1)} %get-tuple-element.8), custom_call_target="InvertDiagBlocksLowerTriangular" | custom-call | tf_op jit(solution)/shard_map/jit(_solve_triangular)/triangular_solve | solution.py:103
  290.5 1.4 fusion.79
  292.6 1.1 fusion.44
  295.0 1.8 fusion.16
  296.8 1.8 fusion.12
  299.0 1.9 fusion.11
  301.0 2.0 fusion.144
  303.5 1.7 fusion.9
  305.7 1.9 convolution_add_fusion.5
  307.9 1.8 convolution_add_fusion.4
  310.1 1.8 convolution_add_fusion.3
  311.9 2.7 subtract_select_fusion
  314.6 1.0 constant_dynamic-update-slice_fusion.17
  315.7 3.2 fusion.18
  319.0 2.0 fusion.141
  321.0 1.7 fusion.7
  322.7 1.8 convolution_add_fusion.2
  324.5 2.0 convolution_add_fusion.1
  326.5 1.8 convolution_add_fusion
  328.3 2.5 pad_subtract_fusion
  331.9 4.2 %copy.144 = f32[35,8,16,256]{3,2,1,0:T(8,128)S(1)} copy(f32[35,8,16,256]{3,1,2,0:T(8,128)} %bitcast.159) | data formatting | bytes 9175040
  336.6 1.3 slice.436
  337.9 6.7 %select_reduce_fusion.1 = f32[32,32,1024]{2,1,0:T(8,128)} fusion(f32[8,32,1024]{2,1,0:T(8,128)S(1)} %bitcast.162, pred[8,32,1024]{2,1,0:T(8,128)(4,1)S(1)} %iota_compare_fusion.4), kind=kLoop, calls=%fused_computation.1 | loop fusion | flops 15728640 | bytes 5505024 | tf_op jit(solution)/shard_map/reduce_sum | solution.py:31
  344.6 5.2 %fusion.152 = f32[256,1024]{1,0:T(8,128)} fusion(f32[256,1024]{1,0:T(8,128)S(1)} %fusion.141, f32[1024,1024]{1,0:T(8,128)} %bitcast.157), kind=kOutput, calls=%fused_computation.271 | convolution fusion | flops 1610612736 | bytes 6291456 | tf_op jit(solution)/shard_map/dot_general | solution.py:14
  350.7 1.7 slice.434
  352.5 14.8 %select_reduce_fusion = f32[32,32,2048]{2,1,0:T(8,128)} fusion(f32[8,32,2048]{2,1,0:T(8,128)S(1)} %bitcast.160, pred[8,32,2048]{2,1,0:T(8,128)(4,1)S(1)} %iota_compare_fusion.2), kind=kLoop, calls=%fused_computation | loop fusion | flops 31457280 | bytes 11010048 | tf_op jit(solution)/shard_map/reduce_sum | solution.py:31
  367.3 6.4 %fusion.151 = f32[256,2048]{1,0:T(8,128)S(1)} fusion(f32[256,1024]{1,0:T(8,128)S(1)} %fusion.141, f32[1024,2048]{1,0:T(8,128)} %bitcast.145), kind=kOutput, calls=%fused_computation.270 | convolution fusion | flops 3221225472 | bytes 11534336 | tf_op jit(solution)/shard_map/dot_general | solution.py:14
  373.9 2.4 fusion.114
  376.4 1.2 fusion.14
  377.5 1.1 convolution_subtract_fusion.7
  379.4 2.8 maximum_subtract_fusion
  (225 shorter events, 43.7 us)
Async XLA Ops:
  7.2 8.5 %copy-start.48 = (s32[8,8]{1,0:T(8,128)S(1)}, s32[8,8]{1,0:T(8,128)}, u32[]{:S(2)}) copy-start(s32[8,8]{1,0:T(8,128)} %param.12) | copy-start | bytes 772
  7.2 56.9 %all-gather.6.cloned.1.call-start = ((), (), s32[]{:S(2)}) async-start(), calls=%async_computation | async-start | bytes 4456448 | tf_op jit(solution)/shard_map/all_gather | solution.py:88
  9.4 109.2 %all-gather.8.cloned.1.call-start = ((), (), s32[]{:S(2)}) async-start(), calls=%async_computation.1 | async-start | bytes 4456448 | tf_op jit(solution)/shard_map/all_gather | solution.py:88
  10.2 163.5 %all-gather.10.cloned.1.call-start = ((), (), s32[]{:S(2)}) async-start(), calls=%async_computation.2 | async-start | bytes 4456448 | tf_op jit(solution)/shard_map/all_gather | solution.py:88
  10.9 227.3 %all-gather.12.cloned.1.call-start = ((), (), s32[]{:S(2)}) async-start(), calls=%async_computation.3 | async-start | bytes 4456448 | tf_op jit(solution)/shard_map/all_gather | solution.py:88
  11.5 320.4 %all-gather.14.cloned.1.call-start = ((), (), s32[]{:S(2)}) async-start(), calls=%async_computation.4 | async-start | bytes 4874240 | tf_op jit(solution)/shard_map/all_gather | solution.py:136
  77.9 39.9 %copy-start.24 = (f32[128,128]{1,0:T(8,128)}, f32[128,128]{1,0:T(8,128)S(1)}, u32[]{:S(2)}) copy-start(f32[128,128]{1,0:T(8,128)S(1)} %get-tuple-element.23) | copy-start | bytes 196612
  105.6 124.2 %copy-start.27 = (f32[128,128]{1,0:T(8,128)}, f32[128,128]{1,0:T(8,128)S(1)}, u32[]{:S(2)}) copy-start(f32[128,128]{1,0:T(8,128)S(1)} %get-tuple-element.21) | copy-start | bytes 196612
  133.5 97.2 %copy-start.37 = (f32[128,128]{1,0:T(8,128)}, f32[128,128]{1,0:T(8,128)S(1)}, u32[]{:S(2)}) copy-start(f32[128,128]{1,0:T(8,128)S(1)} %get-tuple-element.19) | copy-start | bytes 196612
  146.0 0.7 copy-start.13
  160.2 71.3 %copy-start.39 = (f32[128,128]{1,0:T(8,128)}, f32[128,128]{1,0:T(8,128)S(1)}, u32[]{:S(2)}) copy-start(f32[128,128]{1,0:T(8,128)S(1)} %get-tuple-element.17) | copy-start | bytes 196612
  188.7 43.7 %copy-start.29 = (f32[128,128]{1,0:T(8,128)}, f32[128,128]{1,0:T(8,128)S(1)}, u32[]{:S(2)}) copy-start(f32[128,128]{1,0:T(8,128)S(1)} %get-tuple-element.15) | copy-start | bytes 196612
  202.0 31.3 %copy-start.25 = (f32[128,128]{1,0:T(8,128)S(1)}, f32[128,128]{1,0:T(8,128)}, u32[]{:S(2)}) copy-start(f32[128,128]{1,0:T(8,128)} %copy-done.24) | copy-start | bytes 196612
  227.9 5.4 %copy-start.30 = (f32[128,128]{1,0:T(8,128)S(1)}, f32[128,128]{1,0:T(8,128)}, u32[]{:S(2)}) copy-start(f32[128,128]{1,0:T(8,128)} %get-tuple-element.13) | copy-start | bytes 196612
  229.8 5.1 %copy-start.31 = (f32[128,128]{1,0:T(8,128)}, f32[128,128]{1,0:T(8,128)S(1)}, u32[]{:S(2)}) copy-start(f32[128,128]{1,0:T(8,128)S(1)} %cholesky.136) | copy-start | bytes 196612
  230.7 0.9 copy-start.35
  230.7 7.5 %copy-start.12 = (f32[256,768]{1,0:T(8,128)S(1)}, f32[256,768]{1,0:T(8,128)}, u32[]{:S(2)}) copy-start(f32[256,768]{1,0:T(8,128)} %get-tuple-element.42) | copy-start | bytes 2359300
  231.5 0.9 copy-start.22
  234.1 56.4 %copy-start.43 = (f32[1,128,128]{2,1,0:T(8,128)S(1)}, f32[1,128,128]{2,1,0:T(8,128)}, u32[]{:S(2)}) copy-start(f32[1,128,128]{2,1,0:T(8,128)} %get-tuple-element.34) | copy-start | bytes 196612
  263.6 29.0 %copy-start.16 = (f32[1,256,256]{2,1,0:T(8,128)S(1)}, f32[1,256,256]{2,1,0:T(8,128)}, u32[]{:S(2)}) copy-start(f32[1,256,256]{2,1,0:T(8,128)} %get-tuple-element.61) | copy-start | bytes 786436
  264.8 25.6 %copy-start.33 = (f32[128,128]{1,0:T(8,128)}, f32[128,128]{1,0:T(8,128)S(1)}, u32[]{:S(2)}) copy-start(f32[128,128]{1,0:T(8,128)S(1)} %get-tuple-element.45) | copy-start | bytes 196612
  290.4 3.9 copy-start.41
  290.4 3.9 copy-start.44
  290.5 3.9 copy-start.47
  291.9 2.4 copy-start.34
  292.5 2.3 copy-start.42
  292.5 2.4 copy-start.23
  292.5 2.4 copy-start.26
  292.5 2.4 copy-start.28
  292.5 2.4 copy-start.32
  292.5 2.4 copy-start.36
  292.5 2.4 copy-start.38
  292.5 2.4 copy-start.40
  296.8 2.2 copy-start.5
  298.7 20.2 %copy-start.14 = (f32[1,512,512]{2,1,0:T(8,128)}, f32[1,512,512]{2,1,0:T(8,128)S(1)}, u32[]{:S(2)}) copy-start(f32[1,512,512]{2,1,0:T(8,128)S(1)} %fusion.12) | copy-start | bytes 3145732
  298.9 2.1 copy-start.19
  298.9 20.1 %copy-start.17 = (f32[1,512,512]{2,1,0:T(8,128)}, f32[1,512,512]{2,1,0:T(8,128)S(1)}, u32[]{:S(2)}) copy-start(f32[1,512,512]{2,1,0:T(8,128)S(1)} %get-tuple-element.28) | copy-start | bytes 3145732
  300.9 13.6 %copy-start.7 = (f32[256,1024]{1,0:T(8,128)}, f32[256,1024]{1,0:T(8,128)S(1)}, u32[]{:S(2)}) copy-start(f32[256,1024]{1,0:T(8,128)S(1)} %fusion.11) | copy-start | bytes 3145732
  300.9 2.6 copy-start.1
  303.5 2.2 copy-start.2
  305.7 2.2 copy-start.3
  307.9 2.2 copy-start.4
  311.9 3.8 copy-start
  315.7 3.3 copy-start.20
  319.0 11.9 %copy-start.9 = (f32[256,1024]{1,0:T(8,128)}, f32[256,1024]{1,0:T(8,128)S(1)}, u32[]{:S(2)}) copy-start(f32[256,1024]{1,0:T(8,128)S(1)} %fusion.18) | copy-start | bytes 3145732
  367.3 6.4 %copy-start.15 = (f32[1,512,512]{2,1,0:T(8,128)S(1)}, f32[1,512,512]{2,1,0:T(8,128)}, u32[]{:S(2)}) copy-start(f32[1,512,512]{2,1,0:T(8,128)} %copy-done.14) | copy-start | bytes 3145732
  367.3 6.4 %copy-start.18 = (f32[1,512,512]{2,1,0:T(8,128)S(1)}, f32[1,512,512]{2,1,0:T(8,128)}, u32[]{:S(2)}) copy-start(f32[1,512,512]{2,1,0:T(8,128)} %copy-done.17) | copy-start | bytes 3145732
  367.3 6.5 %copy-start.21 = (f32[1,512,512]{2,1,0:T(8,128)S(1)}, f32[1,512,512]{2,1,0:T(8,128)}, u32[]{:S(2)}) copy-start(f32[1,512,512]{2,1,0:T(8,128)} %copy-done.19) | copy-start | bytes 3145732
  373.8 2.5 copy-start.8
  373.8 2.5 copy-start.45
  373.8 3.7 copy-start.10
  373.8 3.7 copy-start.46
  373.8 4.8 %copy-start.49 = (f32[16,16]{1,0:T(8,128)S(1)}, f32[16,16]{1,0:T(8,128)}, u32[]{:S(2)}) copy-start(f32[16,16]{1,0:T(8,128)} %param.16) | copy-start | bytes 3076
  373.9 5.6 %copy-start.6 = (f32[256,4096]{1,0:T(8,128)S(1)}, f32[256,4096]{1,0:T(8,128)}, u32[]{:S(2)}) copy-start(f32[256,4096]{1,0:T(8,128)} %param.13) | copy-start | bytes 12582916
  373.9 5.6 %copy-start.11 = (f32[256,1024]{1,0:T(8,128)S(1)}, f32[256,1024]{1,0:T(8,128)}, u32[]{:S(2)}) copy-start(f32[256,1024]{1,0:T(8,128)} %fusion.152) | copy-start | bytes 3145732
Sparse Core Ops, SparseCore 0:
  10.7 53.2 all-gather.5
  66.2 48.7 all-gather.7
  117.2 50.5 all-gather.9
  169.8 49.9 all-gather.11
  221.8 54.2 all-gather.13

commit v11 on v8

--- a/solution.py
+++ b/solution.py
@@ -20,16 +20,16 @@
     )
 
 
-def assemble_t(block_cols, values_t, col_blocks):
+def assemble_t(block_cols, values_t, col_blocks, first_block=0):
     block_rows, nonzero = block_cols.shape
     width = values_t.shape[0] // nonzero
     span = block_rows * width
     flipped = values_t.reshape(nonzero, 1, width, span)
     spread = jnp.repeat(block_cols.T, width, axis=1)
-    columns = jnp.arange(col_blocks, dtype=jnp.int32)
+    columns = jnp.arange(first_block, col_blocks, dtype=jnp.int32)
     hit = spread[:, None, None, :] == columns[None, :, None, None]
     dense = jnp.where(hit, flipped, 0.0).sum(axis=0)
-    return dense.reshape(col_blocks * width, span)
+    return dense.reshape((col_blocks - first_block) * width, span)
 
 
 def invert_lower(factor, block_inverses):
@@ -142,16 +142,33 @@
     all_values_t = lax.all_gather(values_t, "row", axis=1, tiled=True)
     all_blocks = size // width
     head_blocks = factored // width
-    near_end = min(head_blocks + REACH, all_blocks)
-    far_start = max(all_blocks - REACH, near_end)
-    spans = [(lo, hi) for lo, hi in ((0, near_end), (far_start, all_blocks)) if hi > lo]
+
+    def reach(r):
+        near = [n for n in range(head_blocks)
+                if min(abs(n - r), all_blocks - abs(n - r)) <= REACH]
+        return (min(near), max(near) + 1) if near else None
+
+    groups = []
+    for lo in range(0, all_blocks, 16):
+        hi = min(lo + 16, all_blocks)
+        hits = [reach(r) for r in range(lo, hi)]
+        hits = [h for h in hits if h is not None]
+        if not hits:
+            continue
+        cols = (min(h[0] for h in hits), max(h[1] for h in hits))
+        if groups and groups[-1][1] == lo and groups[-1][2] == cols:
+            groups[-1] = (groups[-1][0], hi, cols)
+        else:
+            groups.append((lo, hi, cols))
     pieces = []
     at = 0
-    for lo, hi in spans:
+    for lo, hi, (first, last) in groups:
         if lo > at:
             pieces.append(jnp.zeros((rows, (lo - at) * width), jnp.float32))
-        head_t = assemble_t(all_block_cols[lo:hi], all_values_t[:, lo * width:hi * width], head_blocks)
-        pieces.append(mdot(coupled_scaled, head_t, HIGH))
+        head_t = assemble_t(
+            all_block_cols[lo:hi], all_values_t[:, lo * width:hi * width], last, first
+        )
+        pieces.append(mdot(coupled_scaled[:, first * width:last * width], head_t, HIGH))
         at = hi
     if at < all_blocks:
         pieces.append(jnp.zeros((rows, (all_blocks - at) * width), jnp.float32))

time: 385 us -> 369 us (0.958)
  other arithmetic: 229 us -> 220 us
  matrix products: 69.1 us -> 65.1 us
    reduce_sum x3 -> x5, other arithmetic: 29.7 us -> 21.1 us  [assemble_t(): dense = jnp.where(hit, flipped, 0.0).sum(axis=0)]
    dot_general x4 -> x6, matrix products: 15 us -> 10.9 us  [mdot(): jnp.dot(left, right, precision=precision, preferred_element_type=jnp.floa...]
    unnamed x79 -> x72, local copies, waits for them, and re-layouts: 14.2 us -> 13.6 us
  transfers between devices with their start and end apart: 5 -> 5, of which waited for: 1 -> 1; matrix products, arithmetic and copies ran while one was open for 75% -> 78% of each run, Pallas kernels for 0% -> 0%
where the time goes in v11:
time: 369 us; the launch traced here: 363 us
  other arithmetic  220 us (60%)
  matrix products  65.1 us (18%)
  local copies, waits for them, and re-layouts  30.5 us (8%)
  blocking collectives  25 us (7%)
  between operations  15.1 us (4%)
  waiting for transfers between devices  7.29 us (2%)
    another operation x24, other arithmetic, on_device(): diagonal = jnp.linalg.cholesky(panel[:block], symmetrize_input=False)  100 us
    another operation x16, other arithmetic, on_device(): jax.scipy.linalg.solve_triangular(diagonal, jnp.eye(block, dtype=jnp.floa...  84.5 us
    dot_general x28, matrix products, tdot(): lax.dot_general(left, right, (((1,), (1,)), ((), ())), precision=precisio...  46 us
    all_gather x1, blocking collectives, on_device(): gathered = lax.all_gather(packed, 'row', axis=0)  25 us
    reduce_sum x5, other arithmetic, assemble_t(): dense = jnp.where(hit, flipped, 0.0).sum(axis=0)  21.1 us
    unnamed x72, local copies, waits for them, and re-layouts  13.6 us
    dot_general x6, matrix products, mdot(): jnp.dot(left, right, precision=precision, preferred_element_type=jnp.floa...  10.9 us
  transfers between devices with their start and end apart: 5, of which 1 were waited for; matrix products, arithmetic and copies ran while one was open for 78% of the time, Pallas kernels for 0%

profile of v11, /device:TPU:0, one launch (start us, length us, event | category | flops | bytes accessed | tf_op | source)
XLA Modules:
  0.0 363.0 jit_solution(10042871251395699462)
XLA Ops:
  7.2 2.2 fusion.149
  11.5 1.8 copy.136
  15.0 25.0 %all-gather = f32[384,256]{1,0:T(8,128)S(1)} all-gather(f32[24,256]{1,0:T(8,128)S(1)} %fusion.127), channel_id=2, replica_groups=mesh['hyper'=2,'row'=16] {'row'}, dimensions={0}, use_global_device_ids=true | all-gather | bytes 417792 | tf_op jit(solution)/shard_map/all_gather | solution.py:81
  40.5 8.3 %select_reduce_fusion.1 = f32[128,32,256]{2,1,0:T(8,128)} fusion(f32[8,32,256]{2,1,0:T(8,128)} %bitcast.184, pred[8,128,256]{2,1,0:T(8,128)(4,1)S(1)} %iota_compare_fusion.4), kind=kLoop, calls=%fused_computation.1 | loop fusion | flops 15728640 | bytes 4718592 | tf_op jit(solution)/shard_map/reduce_sum | solution.py:31
  48.8 5.8 %copy.137 = f32[4096,256]{0,1:T(8,128)} copy(f32[4096,256]{1,0:T(8,128)} %bitcast.177) | data formatting | bytes 8388608 | tf_op jit(solution)/shard_map/reshape | solution.py:32
  55.0 1.0 iota_compare_fusion.2
  59.8 5.3 %all-gather.7.cloned.1.call-done = f32[4096,256]{1,0:T(8,128)} async-done(((f32[256,256]{1,0:T(8,128)}), f32[4096,256]{1,0:T(8,128)}) %all-gather.7.cloned.1.call-update) | async-done | bytes 4194320 | tf_op jit(solution)/shard_map/all_gather | solution.py:94
  66.0 11.7 %cholesky.135 = f32[128,128]{1,0:T(8,128)S(1)} custom-call(f32[128,128]{1,0:T(8,128)S(1)} %slice.401), custom_call_target="Cholesky" | custom-call | tf_op jit(solution)/shard_map/jit(cholesky)/cholesky | solution.py:108
  79.0 9.8 %custom-call.12 = f32[1,128,128]{1,2,0:T(8,128)S(1)} custom-call(f32[1,128,128]{2,1,0:T(8,128)S(1)} %get-tuple-element.22), custom_call_target="InvertDiagBlocksLowerTriangular" | custom-call | tf_op jit(solution)/shard_map/jit(_solve_triangular)/triangular_solve | solution.py:109
  89.1 1.6 fusion.50
  91.7 2.0 convolution_subtract_fusion
  93.7 12.1 %cholesky.146 = f32[128,128]{1,0:T(8,128)S(1)} custom-call(f32[128,128]{1,0:T(8,128)S(1)} %slice.405), custom_call_target="Cholesky" | custom-call | tf_op jit(solution)/shard_map/jit(cholesky)/cholesky | solution.py:108
  107.1 9.8 %custom-call.13 = f32[1,128,128]{1,2,0:T(8,128)S(1)} custom-call(f32[1,128,128]{2,1,0:T(8,128)S(1)} %get-tuple-element.20), custom_call_target="InvertDiagBlocksLowerTriangular" | custom-call | tf_op jit(solution)/shard_map/jit(_solve_triangular)/triangular_solve | solution.py:109
  120.0 1.8 convolution_subtract_fusion.1
  121.8 11.7 %cholesky.157 = f32[128,128]{1,0:T(8,128)S(1)} custom-call(f32[128,128]{1,0:T(8,128)S(1)} %slice.409), custom_call_target="Cholesky" | custom-call | tf_op jit(solution)/shard_map/jit(cholesky)/cholesky | solution.py:108
  134.2 1.3 select_bitcast_fusion.5
  135.5 9.8 %custom-call.14 = f32[1,128,128]{1,2,0:T(8,128)S(1)} custom-call(f32[1,128,128]{2,1,0:T(8,128)S(1)} %get-tuple-element.18), custom_call_target="InvertDiagBlocksLowerTriangular" | custom-call | tf_op jit(solution)/shard_map/jit(_solve_triangular)/triangular_solve | solution.py:109
  146.1 2.0 convolution_subtract_fusion.2
  148.8 11.9 %cholesky.168 = f32[128,128]{1,0:T(8,128)S(1)} custom-call(f32[128,128]{1,0:T(8,128)S(1)} %slice.414), custom_call_target="Cholesky" | custom-call | tf_op jit(solution)/shard_map/jit(cholesky)/cholesky | solution.py:108
  162.0 9.8 %custom-call.15 = f32[1,128,128]{1,2,0:T(8,128)S(1)} custom-call(f32[1,128,128]{2,1,0:T(8,128)S(1)} %get-tuple-element.16), custom_call_target="InvertDiagBlocksLowerTriangular" | custom-call | tf_op jit(solution)/shard_map/jit(_solve_triangular)/triangular_solve | solution.py:109
  172.1 1.3 fusion.77
  175.5 1.9 convolution_subtract_fusion.3
  177.4 11.7 %cholesky.179 = f32[128,128]{1,0:T(8,128)S(1)} custom-call(f32[128,128]{1,0:T(8,128)S(1)} %slice.420), custom_call_target="Cholesky" | custom-call | tf_op jit(solution)/shard_map/jit(cholesky)/cholesky | solution.py:108
  190.5 10.0 %custom-call.16 = f32[1,128,128]{1,2,0:T(8,128)S(1)} custom-call(f32[1,128,128]{2,1,0:T(8,128)S(1)} %get-tuple-element.14), custom_call_target="InvertDiagBlocksLowerTriangular" | custom-call | tf_op jit(solution)/shard_map/jit(_solve_triangular)/triangular_solve | solution.py:109
  202.8 1.0 constant_dynamic-update-slice_fusion
  203.8 2.3 convolution_subtract_fusion.4
  206.1 11.7 %cholesky.190 = f32[128,128]{1,0:T(8,128)S(1)} custom-call(f32[128,128]{1,0:T(8,128)S(1)} %slice.428), custom_call_target="Cholesky" | custom-call | tf_op jit(solution)/shard_map/jit(cholesky)/cholesky | solution.py:108
  219.2 9.8 %custom-call.17 = f32[1,128,128]{1,2,0:T(8,128)S(1)} custom-call(f32[1,128,128]{2,1,0:T(8,128)S(1)} %get-tuple-element.12), custom_call_target="InvertDiagBlocksLowerTriangular" | custom-call | tf_op jit(solution)/shard_map/jit(_solve_triangular)/triangular_solve | solution.py:109
  232.6 0.9 constant_dynamic-update-slice_fusion.1
  233.5 2.0 convolution_subtract_fusion.5
  235.6 12.1 %cholesky.201 = f32[128,128]{1,0:T(8,128)S(1)} custom-call(f32[128,128]{1,0:T(8,128)S(1)} %slice.437), custom_call_target="Cholesky" | custom-call | tf_op jit(solution)/shard_map/jit(cholesky)/cholesky | solution.py:108
  249.0 9.8 %custom-call.18 = f32[1,128,128]{1,2,0:T(8,128)S(1)} custom-call(f32[1,128,128]{2,1,0:T(8,128)S(1)} %get-tuple-element.10), custom_call_target="InvertDiagBlocksLowerTriangular" | custom-call | tf_op jit(solution)/shard_map/jit(_solve_triangular)/triangular_solve | solution.py:109
  260.7 1.8 convolution_subtract_fusion.6
  262.5 11.7 %cholesky.212 = f32[128,128]{1,0:T(8,128)S(1)} custom-call(f32[128,128]{1,0:T(8,128)S(1)} %convolution_subtract_fusion.6), custom_call_target="Cholesky" | custom-call | tf_op jit(solution)/shard_map/jit(cholesky)/cholesky | solution.py:108
  275.6 9.8 %custom-call.19 = f32[1,128,128]{1,2,0:T(8,128)S(1)} custom-call(f32[1,128,128]{2,1,0:T(8,128)S(1)} %get-tuple-element.8), custom_call_target="InvertDiagBlocksLowerTriangular" | custom-call | tf_op jit(solution)/shard_map/jit(_solve_triangular)/triangular_solve | solution.py:109
  290.0 1.8 fusion.16
  292.4 1.9 fusion.12
  294.2 1.9 fusion.11
  296.2 2.1 fusion.145
  298.4 1.7 fusion.9
  300.6 2.2 convolution_add_fusion.5
  302.8 1.8 convolution_add_fusion.4
  304.9 1.8 convolution_add_fusion.3
  306.8 2.7 subtract_select_fusion
  309.4 1.0 constant_dynamic-update-slice_fusion.17
  310.6 3.6 fusion.18
  314.2 3.3 fusion.142
  317.5 1.7 fusion.7
  319.2 1.8 convolution_add_fusion.2
  321.0 1.8 convolution_add_fusion.1
  322.8 1.8 convolution_add_fusion
  324.6 2.5 pad_subtract_fusion
  327.1 1.0 constant_dynamic-update-slice_fusion.16
  328.1 1.4 slice-done
  329.5 8.3 %select_reduce_fusion = f32[32,32,1536]{2,1,0:T(8,128)S(1)} fusion(f32[8,32,1536]{2,1,0:T(8,128)S(1)} %bitcast.180, pred[8,32,1536]{2,1,0:T(8,128)(4,1)S(1)} %copy-done.8), kind=kLoop, calls=%fused_computation | loop fusion | flops 23592960 | bytes 8257536 | tf_op jit(solution)/shard_map/reduce_sum | solution.py:31
  337.9 3.0 convolution_dynamic-update-slice_fusion
  341.1 1.1 select_reduce_fusion.4
  343.1 2.3 fusion.114
  345.4 1.1 fusion.14
  346.5 1.1 convolution_subtract_fusion.7
  348.5 1.1 select_reduce_fusion.3
  350.2 2.3 select_reduce_fusion.2
  352.6 1.2 convolution_dynamic-update-slice_fusion.1
  353.8 2.5 sub.48
  (199 shorter events, 43.4 us)
Async XLA Ops:
  7.2 33.0 %copy-start.26 = (s32[8,8]{1,0:T(8,128)S(1)}, s32[8,8]{1,0:T(8,128)}, u32[]{:S(2)}) copy-start(s32[8,8]{1,0:T(8,128)} %param.12) | copy-start | bytes 772
  7.2 58.0 %all-gather.7.cloned.1.call-start = ((), (), s32[]{:S(2)}) async-start(), calls=%async_computation | async-start | bytes 4456448 | tf_op jit(solution)/shard_map/all_gather | solution.py:94
  9.4 110.6 %all-gather.9.cloned.1.call-start = ((), (), s32[]{:S(2)}) async-start(), calls=%async_computation.1 | async-start | bytes 4456448 | tf_op jit(solution)/shard_map/all_gather | solution.py:94
  10.2 165.3 %all-gather.11.cloned.1.call-start = ((), (), s32[]{:S(2)}) async-start(), calls=%async_computation.2 | async-start | bytes 4456448 | tf_op jit(solution)/shard_map/all_gather | solution.py:94
  10.9 222.6 %all-gather.13.cloned.1.call-start = ((), (), s32[]{:S(2)}) async-start(), calls=%async_computation.3 | async-start | bytes 4456448 | tf_op jit(solution)/shard_map/all_gather | solution.py:94
  11.5 316.6 %all-gather.15.cloned.1.call-start = ((), (), s32[]{:S(2)}) async-start(), calls=%async_computation.4 | async-start | bytes 4456448 | tf_op jit(solution)/shard_map/all_gather | solution.py:142
  148.0 0.7 copy-start.9
  203.8 81.9 %copy-start.22 = (f32[1,128,128]{2,1,0:T(8,128)S(1)}, f32[1,128,128]{2,1,0:T(8,128)}, u32[]{:S(2)}) copy-start(f32[1,128,128]{2,1,0:T(8,128)} %get-tuple-element.37) | copy-start | bytes 196612
  285.4 2.2 copy-start.23
  289.1 0.8 copy-start.19
  289.5 6.6 %copy-start.12 = (f32[1,512,512]{2,1,0:T(8,128)}, f32[1,512,512]{2,1,0:T(8,128)S(1)}, u32[]{:S(2)}) copy-start(f32[1,512,512]{2,1,0:T(8,128)S(1)} %get-tuple-element.31) | copy-start | bytes 3145732
  289.5 6.6 %copy-start.15 = (f32[1,512,512]{2,1,0:T(8,128)}, f32[1,512,512]{2,1,0:T(8,128)S(1)}, u32[]{:S(2)}) copy-start(f32[1,512,512]{2,1,0:T(8,128)S(1)} %get-tuple-element.32) | copy-start | bytes 3145732
  291.9 2.4 copy-start.5
  294.2 16.3 %copy-start.10 = (f32[1,512,512]{2,1,0:T(8,128)}, f32[1,512,512]{2,1,0:T(8,128)S(1)}, u32[]{:S(2)}) copy-start(f32[1,512,512]{2,1,0:T(8,128)S(1)} %fusion.12) | copy-start | bytes 3145732
  296.2 2.2 copy-start.1
  298.4 2.2 copy-start.2
  300.6 2.2 copy-start.3
  302.7 2.2 copy-start.4
  306.8 3.8 %copy-start = (f32[4096,256]{0,1:T(8,128)S(1)}, f32[4096,256]{0,1:T(8,128)}, u32[]{:S(2)}) copy-start(f32[4096,256]{0,1:T(8,128)} %copy.137) | copy-start | bytes 12582916
  310.6 3.6 copy-start.13
  310.6 3.6 copy-start.16
  327.1 1.1 copy-start.8
  328.1 1.4 slice-start
  337.9 3.1 copy-start.6
  337.9 3.2 copy-start.21
  340.9 2.1 copy-start.11
  340.9 2.1 copy-start.14
  340.9 2.1 copy-start.17
  343.0 2.4 copy-start.24
  343.0 3.5 copy-start.25
  343.0 4.7 %copy-start.27 = (f32[16,16]{1,0:T(8,128)S(1)}, f32[16,16]{1,0:T(8,128)}, u32[]{:S(2)}) copy-start(f32[16,16]{1,0:T(8,128)} %param.16) | copy-start | bytes 3076
  343.0 5.4 %copy-start.20 = (pred[8,16,512]{2,1,0:T(8,128)(4,1)S(1)}, pred[8,16,512]{2,1,0:T(8,128)(4,1)}, u32[]{:S(2)}) copy-start(pred[8,16,512]{2,1,0:T(8,128)(4,1)} %iota_compare_fusion.6) | copy-start | bytes 196612
  345.4 4.8 %copy-start.18 = (pred[8,32,512]{2,1,0:T(8,128)(4,1)S(1)}, pred[8,32,512]{2,1,0:T(8,128)(4,1)}, u32[]{:S(2)}) copy-start(pred[8,32,512]{2,1,0:T(8,128)(4,1)} %iota_compare_fusion.5) | copy-start | bytes 393220
  349.6 4.2 %copy-start.7 = (f32[256,4096]{1,0:T(8,128)S(1)}, f32[256,4096]{1,0:T(8,128)}, u32[]{:S(2)}) copy-start(f32[256,4096]{1,0:T(8,128)} %param.13) | copy-start | bytes 12582916
Sparse Core Ops, SparseCore 0:
  10.7 54.3 all-gather.6
  67.3 48.9 all-gather.8
  118.5 50.2 all-gather.10
  170.8 49.8 all-gather.12
  222.7 52.8 all-gather.14

commit v12 on v11

--- a/solution.py
+++ b/solution.py
@@ -149,8 +149,8 @@
         return (min(near), max(near) + 1) if near else None
 
     groups = []
-    for lo in range(0, all_blocks, 16):
-        hi = min(lo + 16, all_blocks)
+    for lo in range(0, all_blocks, 8):
+        hi = min(lo + 8, all_blocks)
         hits = [reach(r) for r in range(lo, hi)]
         hits = [h for h in hits if h is not None]
         if not hits:

time: 369 us -> 370 us (level)
  waiting for transfers between devices: 7.29 us -> 3.59 us
    all_gather x4, waiting for transfers between devices: 5.35 us -> 1.65 us  [on_device(): lax.all_gather(carried_block[:, lo:hi], 'row', axis=0, tiled=True)]
    reduce_sum x5 -> x9, other arithmetic: 21.1 us -> 19.4 us  [assemble_t(): dense = jnp.where(hit, flipped, 0.0).sum(axis=0)]
    dot_general x6 -> x10, matrix products: 10.9 us -> 11.3 us  [mdot(): jnp.dot(left, right, precision=precision, preferred_element_type=jnp.floa...]
    unnamed x72 -> x78, local copies, waits for them, and re-layouts: 13.6 us -> 13.6 us
  transfers between devices with their start and end apart: 5 -> 5, of which waited for: 1 -> 1; matrix products, arithmetic and copies ran while one was open for 78% -> 79% of each run, Pallas kernels for 0% -> 0%
where the time goes in v12:
time: 370 us; the launch traced here: 363 us
  other arithmetic  220 us (59%)
  matrix products  65.4 us (18%)
  local copies, waits for them, and re-layouts  33.8 us (9%)
  blocking collectives  25 us (7%)
  between operations  15.2 us (4%)
    another operation x24, other arithmetic, on_device(): diagonal = jnp.linalg.cholesky(panel[:block], symmetrize_input=False)  99.9 us
    another operation x16, other arithmetic, on_device(): jax.scipy.linalg.solve_triangular(diagonal, jnp.eye(block, dtype=jnp.floa...  84.5 us
    dot_general x28, matrix products, tdot(): lax.dot_general(left, right, (((1,), (1,)), ((), ())), precision=precisio...  45.8 us
    all_gather x1, blocking collectives, on_device(): gathered = lax.all_gather(packed, 'row', axis=0)  25 us
    reduce_sum x9, other arithmetic, assemble_t(): dense = jnp.where(hit, flipped, 0.0).sum(axis=0)  19.4 us
    unnamed x78, local copies, waits for them, and re-layouts  13.6 us
    dot_general x10, matrix products, mdot(): jnp.dot(left, right, precision=precision, preferred_element_type=jnp.floa...  11.3 us
  transfers between devices with their start and end apart: 5, of which 1 were waited for; matrix products, arithmetic and copies ran while one was open for 79% of the time, Pallas kernels for 0%

profile of v12, /device:TPU:0, one launch (start us, length us, event | category | flops | bytes accessed | tf_op | source)
XLA Modules:
  0.0 363.0 jit_solution(9758792468472203438)
XLA Ops:
  7.2 2.2 fusion.154
  11.5 1.8 copy.160
  15.0 25.0 %all-gather = f32[384,256]{1,0:T(8,128)S(1)} all-gather(f32[24,256]{1,0:T(8,128)S(1)} %fusion.131), channel_id=2, replica_groups=mesh['hyper'=2,'row'=16] {'row'}, dimensions={0}, use_global_device_ids=true | all-gather | bytes 417792 | tf_op jit(solution)/shard_map/all_gather | solution.py:81
  41.1 8.2 %select_reduce_fusion.1 = f32[128,32,256]{2,1,0:T(8,128)} fusion(f32[8,32,256]{2,1,0:T(8,128)} %bitcast.191, pred[8,128,256]{2,1,0:T(8,128)(4,1)S(1)} %iota_compare_fusion.4), kind=kLoop, calls=%fused_computation.1 | loop fusion | flops 15728640 | bytes 4718592 | tf_op jit(solution)/shard_map/reduce_sum | solution.py:31
  49.4 5.8 %copy.161 = f32[4096,256]{0,1:T(8,128)} copy(f32[4096,256]{1,0:T(8,128)} %bitcast.184) | data formatting | bytes 8388608 | tf_op jit(solution)/shard_map/reshape | solution.py:32
  55.6 0.9 iota_compare_fusion.2
  63.4 1.6 all-gather.7.cloned.1.call-done
  65.9 11.7 %cholesky.135 = f32[128,128]{1,0:T(8,128)S(1)} custom-call(f32[128,128]{1,0:T(8,128)S(1)} %slice.463), custom_call_target="Cholesky" | custom-call | tf_op jit(solution)/shard_map/jit(cholesky)/cholesky | solution.py:108
  79.0 9.8 %custom-call.12 = f32[1,128,128]{1,2,0:T(8,128)S(1)} custom-call(f32[1,128,128]{2,1,0:T(8,128)S(1)} %get-tuple-element.29), custom_call_target="InvertDiagBlocksLowerTriangular" | custom-call | tf_op jit(solution)/shard_map/jit(_solve_triangular)/triangular_solve | solution.py:109
  89.1 1.6 fusion.52
  91.6 1.9 convolution_subtract_fusion
  93.6 12.1 %cholesky.146 = f32[128,128]{1,0:T(8,128)S(1)} custom-call(f32[128,128]{1,0:T(8,128)S(1)} %slice.467), custom_call_target="Cholesky" | custom-call | tf_op jit(solution)/shard_map/jit(cholesky)/cholesky | solution.py:108
  107.0 9.8 %custom-call.13 = f32[1,128,128]{1,2,0:T(8,128)S(1)} custom-call(f32[1,128,128]{2,1,0:T(8,128)S(1)} %get-tuple-element.27), custom_call_target="InvertDiagBlocksLowerTriangular" | custom-call | tf_op jit(solution)/shard_map/jit(_solve_triangular)/triangular_solve | solution.py:109
  119.9 1.8 convolution_subtract_fusion.1
  121.7 11.7 %cholesky.157 = f32[128,128]{1,0:T(8,128)S(1)} custom-call(f32[128,128]{1,0:T(8,128)S(1)} %slice.471), custom_call_target="Cholesky" | custom-call | tf_op jit(solution)/shard_map/jit(cholesky)/cholesky | solution.py:108
  134.1 1.3 select_bitcast_fusion.5
  135.3 9.8 %custom-call.14 = f32[1,128,128]{1,2,0:T(8,128)S(1)} custom-call(f32[1,128,128]{2,1,0:T(8,128)S(1)} %get-tuple-element.25), custom_call_target="InvertDiagBlocksLowerTriangular" | custom-call | tf_op jit(solution)/shard_map/jit(_solve_triangular)/triangular_solve | solution.py:109
  145.9 2.0 convolution_subtract_fusion.2
  148.6 11.8 %cholesky.168 = f32[128,128]{1,0:T(8,128)S(1)} custom-call(f32[128,128]{1,0:T(8,128)S(1)} %slice.476), custom_call_target="Cholesky" | custom-call | tf_op jit(solution)/shard_map/jit(cholesky)/cholesky | solution.py:108
  161.7 9.8 %custom-call.15 = f32[1,128,128]{1,2,0:T(8,128)S(1)} custom-call(f32[1,128,128]{2,1,0:T(8,128)S(1)} %get-tuple-element.23), custom_call_target="InvertDiagBlocksLowerTriangular" | custom-call | tf_op jit(solution)/shard_map/jit(_solve_triangular)/triangular_solve | solution.py:109
  171.9 1.3 fusion.77
  175.3 1.9 convolution_subtract_fusion.3
  177.2 11.7 %cholesky.179 = f32[128,128]{1,0:T(8,128)S(1)} custom-call(f32[128,128]{1,0:T(8,128)S(1)} %slice.482), custom_call_target="Cholesky" | custom-call | tf_op jit(solution)/shard_map/jit(cholesky)/cholesky | solution.py:108
  190.3 10.0 %custom-call.16 = f32[1,128,128]{1,2,0:T(8,128)S(1)} custom-call(f32[1,128,128]{2,1,0:T(8,128)S(1)} %get-tuple-element.21), custom_call_target="InvertDiagBlocksLowerTriangular" | custom-call | tf_op jit(solution)/shard_map/jit(_solve_triangular)/triangular_solve | solution.py:109
  202.6 1.0 constant_dynamic-update-slice_fusion
  203.6 2.3 convolution_subtract_fusion.4
  206.0 11.7 %cholesky.190 = f32[128,128]{1,0:T(8,128)S(1)} custom-call(f32[128,128]{1,0:T(8,128)S(1)} %slice.490), custom_call_target="Cholesky" | custom-call | tf_op jit(solution)/shard_map/jit(cholesky)/cholesky | solution.py:108
  219.0 9.8 %custom-call.17 = f32[1,128,128]{1,2,0:T(8,128)S(1)} custom-call(f32[1,128,128]{2,1,0:T(8,128)S(1)} %get-tuple-element.19), custom_call_target="InvertDiagBlocksLowerTriangular" | custom-call | tf_op jit(solution)/shard_map/jit(_solve_triangular)/triangular_solve | solution.py:109
  232.4 0.9 constant_dynamic-update-slice_fusion.1
  233.3 2.0 convolution_subtract_fusion.5
  235.4 12.1 %cholesky.201 = f32[128,128]{1,0:T(8,128)S(1)} custom-call(f32[128,128]{1,0:T(8,128)S(1)} %slice.499), custom_call_target="Cholesky" | custom-call | tf_op jit(solution)/shard_map/jit(cholesky)/cholesky | solution.py:108
  248.8 9.8 %custom-call.18 = f32[1,128,128]{1,2,0:T(8,128)S(1)} custom-call(f32[1,128,128]{2,1,0:T(8,128)S(1)} %get-tuple-element.17), custom_call_target="InvertDiagBlocksLowerTriangular" | custom-call | tf_op jit(solution)/shard_map/jit(_solve_triangular)/triangular_solve | solution.py:109
  259.6 0.9 constant_dynamic-update-slice_fusion.2
  260.5 1.8 convolution_subtract_fusion.6
  262.3 11.7 %cholesky.212 = f32[128,128]{1,0:T(8,128)S(1)} custom-call(f32[128,128]{1,0:T(8,128)S(1)} %convolution_subtract_fusion.6), custom_call_target="Cholesky" | custom-call | tf_op jit(solution)/shard_map/jit(cholesky)/cholesky | solution.py:108
  275.3 9.8 %custom-call.19 = f32[1,128,128]{1,2,0:T(8,128)S(1)} custom-call(f32[1,128,128]{2,1,0:T(8,128)S(1)} %get-tuple-element.15), custom_call_target="InvertDiagBlocksLowerTriangular" | custom-call | tf_op jit(solution)/shard_map/jit(_solve_triangular)/triangular_solve | solution.py:109
  289.8 1.8 fusion.16
  292.1 1.9 fusion.12
  294.0 1.9 fusion.11
  296.0 2.1 fusion.150
  298.1 1.7 fusion.9
  300.3 2.2 convolution_add_fusion.5
  302.5 1.8 convolution_add_fusion.4
  304.7 1.8 convolution_add_fusion.3
  306.6 2.7 subtract_select_fusion
  309.2 1.0 constant_dynamic-update-slice_fusion.17
  310.3 3.6 fusion.18
  314.0 3.3 fusion.147
  317.2 1.7 fusion.7
  319.0 1.8 convolution_add_fusion.2
  320.8 1.8 convolution_add_fusion.1
  322.5 1.8 convolution_add_fusion
  324.4 2.5 pad_subtract_fusion
  326.8 1.0 constant_dynamic-update-slice_fusion.16
  327.9 1.4 slice.527
  329.3 6.7 %select_reduce_fusion = f32[32,32,1280]{2,1,0:T(8,128)S(1)} fusion(f32[8,32,1280]{2,1,0:T(8,128)S(1)} %bitcast.186, pred[8,32,1280]{2,1,0:T(8,128)(4,1)S(1)} %copy-done.8), kind=kLoop, calls=%fused_computation | loop fusion | flops 19660800 | bytes 6881280 | tf_op jit(solution)/shard_map/reduce_sum | solution.py:31
  336.1 2.8 convolution_dynamic-update-slice_fusion
  338.9 1.6 fusion.153
  340.6 0.8 select_reduce_fusion.4
  343.7 2.3 fusion.118
  346.0 1.1 fusion.14
  347.2 1.1 convolution_subtract_fusion.7
  352.0 1.1 select_reduce_fusion.2
  353.8 2.5 sub.48
  (233 shorter events, 50.2 us)
Async XLA Ops:
  7.2 33.6 %copy-start.29 = (s32[8,8]{1,0:T(8,128)S(1)}, s32[8,8]{1,0:T(8,128)}, u32[]{:S(2)}) copy-start(s32[8,8]{1,0:T(8,128)} %param.12) | copy-start | bytes 772
  7.2 57.9 %all-gather.7.cloned.1.call-start = ((), (), s32[]{:S(2)}) async-start(), calls=%async_computation | async-start | bytes 4456448 | tf_op jit(solution)/shard_map/all_gather | solution.py:94
  9.4 110.5 %all-gather.9.cloned.1.call-start = ((), (), s32[]{:S(2)}) async-start(), calls=%async_computation.1 | async-start | bytes 4456448 | tf_op jit(solution)/shard_map/all_gather | solution.py:94
  10.2 165.1 %all-gather.11.cloned.1.call-start = ((), (), s32[]{:S(2)}) async-start(), calls=%async_computation.2 | async-start | bytes 4456448 | tf_op jit(solution)/shard_map/all_gather | solution.py:94
  10.9 222.4 %all-gather.13.cloned.1.call-start = ((), (), s32[]{:S(2)}) async-start(), calls=%async_computation.3 | async-start | bytes 4456448 | tf_op jit(solution)/shard_map/all_gather | solution.py:94
  11.5 316.4 %all-gather.15.cloned.1.call-start = ((), (), s32[]{:S(2)}) async-start(), calls=%async_computation.4 | async-start | bytes 4456448 | tf_op jit(solution)/shard_map/all_gather | solution.py:142
  147.9 0.7 copy-start.7
  203.6 81.8 %copy-start.18 = (f32[1,128,128]{2,1,0:T(8,128)S(1)}, f32[1,128,128]{2,1,0:T(8,128)}, u32[]{:S(2)}) copy-start(f32[1,128,128]{2,1,0:T(8,128)} %get-tuple-element.48) | copy-start | bytes 196612
  285.1 2.2 copy-start.25
  288.8 0.8 copy-start.17
  289.3 6.6 %copy-start.11 = (f32[1,512,512]{2,1,0:T(8,128)}, f32[1,512,512]{2,1,0:T(8,128)S(1)}, u32[]{:S(2)}) copy-start(f32[1,512,512]{2,1,0:T(8,128)S(1)} %get-tuple-element.42) | copy-start | bytes 3145732
  289.3 6.6 %copy-start.14 = (f32[1,512,512]{2,1,0:T(8,128)}, f32[1,512,512]{2,1,0:T(8,128)S(1)}, u32[]{:S(2)}) copy-start(f32[1,512,512]{2,1,0:T(8,128)S(1)} %get-tuple-element.43) | copy-start | bytes 3145732
  289.8 2.1 copy-start.28
  291.6 2.4 copy-start.5
  294.0 16.3 %copy-start.9 = (f32[1,512,512]{2,1,0:T(8,128)}, f32[1,512,512]{2,1,0:T(8,128)S(1)}, u32[]{:S(2)}) copy-start(f32[1,512,512]{2,1,0:T(8,128)S(1)} %fusion.12) | copy-start | bytes 3145732
  296.0 2.2 copy-start.1
  298.1 2.2 copy-start.2
  300.3 2.2 copy-start.3
  302.5 2.2 copy-start.4
  306.6 3.8 %copy-start = (f32[4096,256]{0,1:T(8,128)S(1)}, f32[4096,256]{0,1:T(8,128)}, u32[]{:S(2)}) copy-start(f32[4096,256]{0,1:T(8,128)} %copy.161) | copy-start | bytes 12582916
  310.3 3.6 copy-start.12
  310.3 3.6 copy-start.15
  326.8 2.5 copy-start.8
  336.1 4.5 %copy-start.21 = (pred[8,24,256]{2,1,0:T(8,128)(4,1)S(1)}, pred[8,24,256]{2,1,0:T(8,128)(4,1)}, u32[]{:S(2)}) copy-start(pred[8,24,256]{2,1,0:T(8,128)(4,1)} %broadcast_compare_fusion) | copy-start | bytes 147460
  338.9 3.1 copy-start.23
  338.9 4.0 %copy-start.24 = (pred[8,8,256]{2,1,0:T(8,128)(4,1)S(1)}, pred[8,8,256]{2,1,0:T(8,128)(4,1)}, u32[]{:S(2)}) copy-start(pred[8,8,256]{2,1,0:T(8,128)(4,1)} %broadcast_compare_fusion.2) | copy-start | bytes 49156
  340.6 3.0 copy-start.10
  340.6 3.0 copy-start.13
  340.6 3.0 copy-start.16
  343.6 2.4 copy-start.26
  343.6 3.5 copy-start.27
  343.6 4.7 %copy-start.30 = (f32[16,16]{1,0:T(8,128)S(1)}, f32[16,16]{1,0:T(8,128)}, u32[]{:S(2)}) copy-start(f32[16,16]{1,0:T(8,128)} %param.16) | copy-start | bytes 3076
  343.6 6.0 %copy-start.22 = (pred[8,16,256]{2,1,0:T(8,128)(4,1)S(1)}, pred[8,16,256]{2,1,0:T(8,128)(4,1)}, u32[]{:S(2)}) copy-start(pred[8,16,256]{2,1,0:T(8,128)(4,1)} %iota_compare_fusion.7) | copy-start | bytes 98308
  346.0 4.6 %copy-start.20 = (pred[8,24,256]{2,1,0:T(8,128)(4,1)S(1)}, pred[8,24,256]{2,1,0:T(8,128)(4,1)}, u32[]{:S(2)}) copy-start(pred[8,24,256]{2,1,0:T(8,128)(4,1)} %iota_compare_fusion.6) | copy-start | bytes 147460
  346.0 6.0 %copy-start.19 = (pred[8,32,256]{2,1,0:T(8,128)(4,1)S(1)}, pred[8,32,256]{2,1,0:T(8,128)(4,1)}, u32[]{:S(2)}) copy-start(pred[8,32,256]{2,1,0:T(8,128)(4,1)} %iota_compare_fusion.5) | copy-start | bytes 196612
  350.2 3.6 copy-start.6
Sparse Core Ops, SparseCore 0:
  10.7 54.2 all-gather.6
  67.2 48.7 all-gather.8
  118.2 50.5 all-gather.10
  170.8 49.4 all-gather.12
  222.3 52.8 all-gather.14

commit v13 on v11

--- a/solution.py
+++ b/solution.py
@@ -165,8 +165,12 @@
     for lo, hi, (first, last) in groups:
         if lo > at:
             pieces.append(jnp.zeros((rows, (lo - at) * width), jnp.float32))
+        skip = int(all(r < first or r >= last for r in range(lo, hi)))
         head_t = assemble_t(
-            all_block_cols[lo:hi], all_values_t[:, lo * width:hi * width], last, first
+            all_block_cols[lo:hi, skip:],
+            all_values_t[skip * width:, lo * width:hi * width],
+            last,
+            first,
         )
         pieces.append(mdot(coupled_scaled[:, first * width:last * width], head_t, HIGH))
         at = hi

time: 369 us -> 369 us (level)
  no operation moved by 1% of the time
where the time goes in v13:
time: 369 us; the launch traced here: 362 us
  other arithmetic  219 us (59%)
  matrix products  65.1 us (18%)
  local copies, waits for them, and re-layouts  30.6 us (8%)
  blocking collectives  25 us (7%)
  between operations  15.1 us (4%)
  waiting for transfers between devices  7.1 us (2%)
    another operation x24, other arithmetic, on_device(): diagonal = jnp.linalg.cholesky(panel[:block], symmetrize_input=False)  99.6 us
    another operation x16, other arithmetic, on_device(): jax.scipy.linalg.solve_triangular(diagonal, jnp.eye(block, dtype=jnp.floa...  84.7 us
    dot_general x28, matrix products, tdot(): lax.dot_general(left, right, (((1,), (1,)), ((), ())), precision=precisio...  46.1 us
    all_gather x1, blocking collectives, on_device(): gathered = lax.all_gather(packed, 'row', axis=0)  25 us
    reduce_sum x5, other arithmetic, assemble_t(): dense = jnp.where(hit, flipped, 0.0).sum(axis=0)  20.3 us
    unnamed x72, local copies, waits for them, and re-layouts  13.5 us
    dot_general x6, matrix products, mdot(): jnp.dot(left, right, precision=precision, preferred_element_type=jnp.floa...  10.9 us
  transfers between devices with their start and end apart: 5, of which 1 were waited for; matrix products, arithmetic and copies ran while one was open for 78% of the time, Pallas kernels for 0%

profile of v13, /device:TPU:0, one launch (start us, length us, event | category | flops | bytes accessed | tf_op | source)
XLA Modules:
  0.0 362.1 jit_solution(2379414486390568570)
XLA Ops:
  7.2 2.2 fusion.149
  11.5 1.8 copy.135
  15.0 25.0 %all-gather = f32[384,256]{1,0:T(8,128)S(1)} all-gather(f32[24,256]{1,0:T(8,128)S(1)} %fusion.127), channel_id=2, replica_groups=mesh['hyper'=2,'row'=16] {'row'}, dimensions={0}, use_global_device_ids=true | all-gather | bytes 417792 | tf_op jit(solution)/shard_map/all_gather | solution.py:81
  40.6 8.3 %select_reduce_fusion.1 = f32[128,32,256]{2,1,0:T(8,128)} fusion(f32[8,32,256]{2,1,0:T(8,128)} %bitcast.183, pred[8,128,256]{2,1,0:T(8,128)(4,1)S(1)} %iota_compare_fusion.4), kind=kLoop, calls=%fused_computation.1 | loop fusion | flops 15728640 | bytes 4718592 | tf_op jit(solution)/shard_map/reduce_sum | solution.py:31
  48.8 6.0 %copy.136 = f32[4096,256]{0,1:T(8,128)} copy(f32[4096,256]{1,0:T(8,128)} %bitcast.176) | data formatting | bytes 8388608 | tf_op jit(solution)/shard_map/reshape | solution.py:32
  55.3 1.0 iota_compare_fusion.2
  59.9 5.2 %all-gather.7.cloned.1.call-done = f32[4096,256]{1,0:T(8,128)} async-done(((f32[256,256]{1,0:T(8,128)}), f32[4096,256]{1,0:T(8,128)}) %all-gather.7.cloned.1.call-update) | async-done | bytes 4194320 | tf_op jit(solution)/shard_map/all_gather | solution.py:94
  65.9 11.7 %cholesky.135 = f32[128,128]{1,0:T(8,128)S(1)} custom-call(f32[128,128]{1,0:T(8,128)S(1)} %slice.386), custom_call_target="Cholesky" | custom-call | tf_op jit(solution)/shard_map/jit(cholesky)/cholesky | solution.py:108
  79.0 9.8 %custom-call.12 = f32[1,128,128]{1,2,0:T(8,128)S(1)} custom-call(f32[1,128,128]{2,1,0:T(8,128)S(1)} %get-tuple-element.22), custom_call_target="InvertDiagBlocksLowerTriangular" | custom-call | tf_op jit(solution)/shard_map/jit(_solve_triangular)/triangular_solve | solution.py:109
  89.1 1.6 fusion.50
  91.7 1.9 convolution_subtract_fusion
  93.6 11.8 %cholesky.146 = f32[128,128]{1,0:T(8,128)S(1)} custom-call(f32[128,128]{1,0:T(8,128)S(1)} %slice.390), custom_call_target="Cholesky" | custom-call | tf_op jit(solution)/shard_map/jit(cholesky)/cholesky | solution.py:108
  106.8 9.8 %custom-call.13 = f32[1,128,128]{1,2,0:T(8,128)S(1)} custom-call(f32[1,128,128]{2,1,0:T(8,128)S(1)} %get-tuple-element.20), custom_call_target="InvertDiagBlocksLowerTriangular" | custom-call | tf_op jit(solution)/shard_map/jit(_solve_triangular)/triangular_solve | solution.py:109
  119.6 1.8 convolution_subtract_fusion.1
  121.4 11.7 %cholesky.157 = f32[128,128]{1,0:T(8,128)S(1)} custom-call(f32[128,128]{1,0:T(8,128)S(1)} %slice.394), custom_call_target="Cholesky" | custom-call | tf_op jit(solution)/shard_map/jit(cholesky)/cholesky | solution.py:108
  133.8 1.3 select_bitcast_fusion.5
  135.1 9.8 %custom-call.14 = f32[1,128,128]{1,2,0:T(8,128)S(1)} custom-call(f32[1,128,128]{2,1,0:T(8,128)S(1)} %get-tuple-element.18), custom_call_target="InvertDiagBlocksLowerTriangular" | custom-call | tf_op jit(solution)/shard_map/jit(_solve_triangular)/triangular_solve | solution.py:109
  145.7 2.0 convolution_subtract_fusion.2
  148.4 11.9 %cholesky.168 = f32[128,128]{1,0:T(8,128)S(1)} custom-call(f32[128,128]{1,0:T(8,128)S(1)} %slice.399), custom_call_target="Cholesky" | custom-call | tf_op jit(solution)/shard_map/jit(cholesky)/cholesky | solution.py:108
  161.6 9.8 %custom-call.15 = f32[1,128,128]{1,2,0:T(8,128)S(1)} custom-call(f32[1,128,128]{2,1,0:T(8,128)S(1)} %get-tuple-element.16), custom_call_target="InvertDiagBlocksLowerTriangular" | custom-call | tf_op jit(solution)/shard_map/jit(_solve_triangular)/triangular_solve | solution.py:109
  171.7 1.3 fusion.77
  175.1 1.9 convolution_subtract_fusion.3
  177.1 11.7 %cholesky.179 = f32[128,128]{1,0:T(8,128)S(1)} custom-call(f32[128,128]{1,0:T(8,128)S(1)} %slice.405), custom_call_target="Cholesky" | custom-call | tf_op jit(solution)/shard_map/jit(cholesky)/cholesky | solution.py:108
  190.2 10.2 %custom-call.16 = f32[1,128,128]{1,2,0:T(8,128)S(1)} custom-call(f32[1,128,128]{2,1,0:T(8,128)S(1)} %get-tuple-element.14), custom_call_target="InvertDiagBlocksLowerTriangular" | custom-call | tf_op jit(solution)/shard_map/jit(_solve_triangular)/triangular_solve | solution.py:109
  202.7 1.0 constant_dynamic-update-slice_fusion
  203.7 2.3 convolution_subtract_fusion.4
  206.0 11.7 %cholesky.190 = f32[128,128]{1,0:T(8,128)S(1)} custom-call(f32[128,128]{1,0:T(8,128)S(1)} %slice.413), custom_call_target="Cholesky" | custom-call | tf_op jit(solution)/shard_map/jit(cholesky)/cholesky | solution.py:108
  219.0 9.8 %custom-call.17 = f32[1,128,128]{1,2,0:T(8,128)S(1)} custom-call(f32[1,128,128]{2,1,0:T(8,128)S(1)} %get-tuple-element.12), custom_call_target="InvertDiagBlocksLowerTriangular" | custom-call | tf_op jit(solution)/shard_map/jit(_solve_triangular)/triangular_solve | solution.py:109
  232.4 1.0 constant_dynamic-update-slice_fusion.1
  233.4 2.0 convolution_subtract_fusion.5
  235.5 11.9 %cholesky.201 = f32[128,128]{1,0:T(8,128)S(1)} custom-call(f32[128,128]{1,0:T(8,128)S(1)} %slice.422), custom_call_target="Cholesky" | custom-call | tf_op jit(solution)/shard_map/jit(cholesky)/cholesky | solution.py:108
  248.7 9.8 %custom-call.18 = f32[1,128,128]{1,2,0:T(8,128)S(1)} custom-call(f32[1,128,128]{2,1,0:T(8,128)S(1)} %get-tuple-element.10), custom_call_target="InvertDiagBlocksLowerTriangular" | custom-call | tf_op jit(solution)/shard_map/jit(_solve_triangular)/triangular_solve | solution.py:109
  260.3 1.8 convolution_subtract_fusion.6
  262.1 11.7 %cholesky.212 = f32[128,128]{1,0:T(8,128)S(1)} custom-call(f32[128,128]{1,0:T(8,128)S(1)} %convolution_subtract_fusion.6), custom_call_target="Cholesky" | custom-call | tf_op jit(solution)/shard_map/jit(cholesky)/cholesky | solution.py:108
  275.2 9.8 %custom-call.19 = f32[1,128,128]{1,2,0:T(8,128)S(1)} custom-call(f32[1,128,128]{2,1,0:T(8,128)S(1)} %get-tuple-element.8), custom_call_target="InvertDiagBlocksLowerTriangular" | custom-call | tf_op jit(solution)/shard_map/jit(_solve_triangular)/triangular_solve | solution.py:109
  289.6 1.8 fusion.16
  292.0 1.9 fusion.12
  293.9 1.9 fusion.11
  295.8 2.1 fusion.145
  298.0 1.7 fusion.9
  300.2 2.2 convolution_add_fusion.5
  302.4 1.8 convolution_add_fusion.4
  304.6 1.8 convolution_add_fusion.3
  306.5 2.7 subtract_select_fusion
  309.1 1.0 constant_dynamic-update-slice_fusion.17
  310.2 3.6 fusion.18
  313.9 3.3 fusion.142
  317.1 1.7 fusion.7
  318.9 1.8 convolution_add_fusion.2
  320.6 2.0 convolution_add_fusion.1
  322.6 1.8 convolution_add_fusion
  324.5 2.5 pad_subtract_fusion
  326.9 1.0 constant_dynamic-update-slice_fusion.16
  328.0 1.4 slice-done
  329.4 8.2 %select_reduce_fusion = f32[32,32,1536]{2,1,0:T(8,128)S(1)} fusion(f32[8,32,1536]{2,1,0:T(8,128)S(1)} %bitcast.179, pred[8,32,1536]{2,1,0:T(8,128)(4,1)S(1)} %copy-done.8), kind=kLoop, calls=%fused_computation | loop fusion | flops 23592960 | bytes 8257536 | tf_op jit(solution)/shard_map/reduce_sum | solution.py:31
  337.6 3.0 convolution_dynamic-update-slice_fusion
  340.8 1.0 select_reduce_fusion.4
  342.5 2.3 fusion.114
  344.9 1.1 fusion.14
  346.1 1.1 convolution_subtract_fusion.7
  348.0 1.0 select_reduce_fusion.3
  349.6 2.0 select_reduce_fusion.2
  351.6 1.2 convolution_dynamic-update-slice_fusion.1
  352.8 2.5 sub.48
  (197 shorter events, 43.2 us)
Async XLA Ops:
  7.2 33.0 %copy-start.26 = (s32[8,8]{1,0:T(8,128)S(1)}, s32[8,8]{1,0:T(8,128)}, u32[]{:S(2)}) copy-start(s32[8,8]{1,0:T(8,128)} %param.12) | copy-start | bytes 772
  7.2 57.9 %all-gather.7.cloned.1.call-start = ((), (), s32[]{:S(2)}) async-start(), calls=%async_computation | async-start | bytes 4456448 | tf_op jit(solution)/shard_map/all_gather | solution.py:94
  9.4 110.2 %all-gather.9.cloned.1.call-start = ((), (), s32[]{:S(2)}) async-start(), calls=%async_computation.1 | async-start | bytes 4456448 | tf_op jit(solution)/shard_map/all_gather | solution.py:94
  10.2 165.0 %all-gather.11.cloned.1.call-start = ((), (), s32[]{:S(2)}) async-start(), calls=%async_computation.2 | async-start | bytes 4456448 | tf_op jit(solution)/shard_map/all_gather | solution.py:94
  10.9 222.5 %all-gather.13.cloned.1.call-start = ((), (), s32[]{:S(2)}) async-start(), calls=%async_computation.3 | async-start | bytes 4456448 | tf_op jit(solution)/shard_map/all_gather | solution.py:94
  11.5 316.5 %all-gather.15.cloned.1.call-start = ((), (), s32[]{:S(2)}) async-start(), calls=%async_computation.4 | async-start | bytes 4456448 | tf_op jit(solution)/shard_map/all_gather | solution.py:142
  147.6 0.7 copy-start.9
  203.7 81.7 %copy-start.20 = (f32[1,128,128]{2,1,0:T(8,128)S(1)}, f32[1,128,128]{2,1,0:T(8,128)}, u32[]{:S(2)}) copy-start(f32[1,128,128]{2,1,0:T(8,128)} %get-tuple-element.37) | copy-start | bytes 196612
  285.0 2.2 copy-start.23
  288.7 0.8 copy-start.19
  289.2 6.6 %copy-start.12 = (f32[1,512,512]{2,1,0:T(8,128)}, f32[1,512,512]{2,1,0:T(8,128)S(1)}, u32[]{:S(2)}) copy-start(f32[1,512,512]{2,1,0:T(8,128)S(1)} %get-tuple-element.31) | copy-start | bytes 3145732
  289.2 6.6 %copy-start.15 = (f32[1,512,512]{2,1,0:T(8,128)}, f32[1,512,512]{2,1,0:T(8,128)S(1)}, u32[]{:S(2)}) copy-start(f32[1,512,512]{2,1,0:T(8,128)S(1)} %get-tuple-element.32) | copy-start | bytes 3145732
  291.5 2.4 copy-start.5
  293.8 16.3 %copy-start.10 = (f32[1,512,512]{2,1,0:T(8,128)}, f32[1,512,512]{2,1,0:T(8,128)S(1)}, u32[]{:S(2)}) copy-start(f32[1,512,512]{2,1,0:T(8,128)S(1)} %fusion.12) | copy-start | bytes 3145732
  295.8 2.2 copy-start.1
  298.0 2.2 copy-start.2
  300.2 2.2 copy-start.3
  302.4 2.2 copy-start.4
  306.5 3.8 %copy-start = (f32[4096,256]{0,1:T(8,128)S(1)}, f32[4096,256]{0,1:T(8,128)}, u32[]{:S(2)}) copy-start(f32[4096,256]{0,1:T(8,128)} %copy.136) | copy-start | bytes 12582916
  310.2 3.6 copy-start.13
  310.2 3.6 copy-start.16
  326.9 1.1 copy-start.8
  328.0 1.4 slice-start
  337.6 3.0 copy-start.6
  337.6 3.2 copy-start.22
  340.6 1.9 copy-start.11
  340.6 1.9 copy-start.14
  340.6 1.9 copy-start.17
  342.5 2.4 copy-start.24
  342.5 3.5 copy-start.25
  342.5 4.7 %copy-start.27 = (f32[16,16]{1,0:T(8,128)S(1)}, f32[16,16]{1,0:T(8,128)}, u32[]{:S(2)}) copy-start(f32[16,16]{1,0:T(8,128)} %param.16) | copy-start | bytes 3076
  342.5 5.4 %copy-start.21 = (pred[7,16,512]{2,1,0:T(8,128)(4,1)S(1)}, pred[7,16,512]{2,1,0:T(8,128)(4,1)}, u32[]{:S(2)}) copy-start(pred[7,16,512]{2,1,0:T(8,128)(4,1)} %iota_compare_fusion.6) | copy-start | bytes 172036
  344.9 4.7 %copy-start.18 = (pred[7,32,512]{2,1,0:T(8,128)(4,1)S(1)}, pred[7,32,512]{2,1,0:T(8,128)(4,1)}, u32[]{:S(2)}) copy-start(pred[7,32,512]{2,1,0:T(8,128)(4,1)} %iota_compare_fusion.5) | copy-start | bytes 344068
  348.9 3.9 %copy-start.7 = (f32[256,4096]{1,0:T(8,128)S(1)}, f32[256,4096]{1,0:T(8,128)}, u32[]{:S(2)}) copy-start(f32[256,4096]{1,0:T(8,128)} %param.13) | copy-start | bytes 12582916
Sparse Core Ops, SparseCore 0:
  10.7 54.2 all-gather.6
  67.2 48.9 all-gather.8
  118.4 50.2 all-gather.10
  170.7 49.4 all-gather.12
  222.1 52.2 all-gather.14

commit v14 on v13

--- a/solution.py
+++ b/solution.py
@@ -156,16 +156,16 @@
         if not hits:
             continue
         cols = (min(h[0] for h in hits), max(h[1] for h in hits))
+        cols = cols + (int(all(r < cols[0] or r >= cols[1] for r in range(lo, hi))),)
         if groups and groups[-1][1] == lo and groups[-1][2] == cols:
             groups[-1] = (groups[-1][0], hi, cols)
         else:
             groups.append((lo, hi, cols))
     pieces = []
     at = 0
-    for lo, hi, (first, last) in groups:
+    for lo, hi, (first, last, skip) in groups:
         if lo > at:
             pieces.append(jnp.zeros((rows, (lo - at) * width), jnp.float32))
-        skip = int(all(r < first or r >= last for r in range(lo, hi)))
         head_t = assemble_t(
             all_block_cols[lo:hi, skip:],
             all_values_t[skip * width:, lo * width:hi * width],

time: 369 us -> 376 us (1.019)
    dot_general x6 -> x7, matrix products: 10.9 us -> 13.4 us  [mdot(): jnp.dot(left, right, precision=precision, preferred_element_type=jnp.floa...]
    reduce_sum x5 -> x6, other arithmetic: 20.3 us -> 22.8 us  [assemble_t(): dense = jnp.where(hit, flipped, 0.0).sum(axis=0)]
  transfers between devices with their start and end apart: 5 -> 5, of which waited for: 1 -> 1; matrix products, arithmetic and copies ran while one was open for 78% -> 77% of each run, Pallas kernels for 0% -> 0%
where the time goes in v14:
time: 376 us; the launch traced here: 370 us
  other arithmetic  222 us (59%)
  matrix products  67.7 us (18%)
  local copies, waits for them, and re-layouts  33 us (9%)
  blocking collectives  25.1 us (7%)
  between operations  15.3 us (4%)
  waiting for transfers between devices  6.56 us (2%)
    another operation x24, other arithmetic, on_device(): diagonal = jnp.linalg.cholesky(panel[:block], symmetrize_input=False)  99.9 us
    another operation x16, other arithmetic, on_device(): jax.scipy.linalg.solve_triangular(diagonal, jnp.eye(block, dtype=jnp.floa...  84.5 us
    dot_general x28, matrix products, tdot(): lax.dot_general(left, right, (((1,), (1,)), ((), ())), precision=precisio...  45.9 us
    all_gather x1, blocking collectives, on_device(): gathered = lax.all_gather(packed, 'row', axis=0)  25.1 us
    reduce_sum x6, other arithmetic, assemble_t(): dense = jnp.where(hit, flipped, 0.0).sum(axis=0)  22.8 us
    unnamed x72, local copies, waits for them, and re-layouts  13.6 us
    dot_general x7, matrix products, mdot(): jnp.dot(left, right, precision=precision, preferred_element_type=jnp.floa...  13.4 us
  transfers between devices with their start and end apart: 5, of which 1 were waited for; matrix products, arithmetic and copies ran while one was open for 77% of the time, Pallas kernels for 0%

profile of v14, /device:TPU:0, one launch (start us, length us, event | category | flops | bytes accessed | tf_op | source)
XLA Modules:
  0.0 369.6 jit_solution(4619282518648629001)
XLA Ops:
  7.2 2.2 fusion.149
  11.5 1.8 copy.138
  15.0 25.1 %all-gather = f32[384,256]{1,0:T(8,128)S(1)} all-gather(f32[24,256]{1,0:T(8,128)S(1)} %fusion.127), channel_id=2, replica_groups=mesh['hyper'=2,'row'=16] {'row'}, dimensions={0}, use_global_device_ids=true | all-gather | bytes 417792 | tf_op jit(solution)/shard_map/all_gather | solution.py:81
  40.6 8.3 %select_reduce_fusion.1 = f32[128,32,256]{2,1,0:T(8,128)} fusion(f32[8,32,256]{2,1,0:T(8,128)} %bitcast.190, pred[8,128,256]{2,1,0:T(8,128)(4,1)S(1)} %iota_compare_fusion.4), kind=kLoop, calls=%fused_computation.1 | loop fusion | flops 15728640 | bytes 4718592 | tf_op jit(solution)/shard_map/reduce_sum | solution.py:31
  48.9 5.7 %copy.139 = f32[4096,256]{0,1:T(8,128)} copy(f32[4096,256]{1,0:T(8,128)} %bitcast.182) | data formatting | bytes 8388608 | tf_op jit(solution)/shard_map/reshape | solution.py:32
  60.5 4.6 %all-gather.7.cloned.1.call-done = f32[4096,256]{1,0:T(8,128)} async-done(((f32[256,256]{1,0:T(8,128)}), f32[4096,256]{1,0:T(8,128)}) %all-gather.7.cloned.1.call-update) | async-done | bytes 4194320 | tf_op jit(solution)/shard_map/all_gather | solution.py:94
  65.9 11.7 %cholesky.135 = f32[128,128]{1,0:T(8,128)S(1)} custom-call(f32[128,128]{1,0:T(8,128)S(1)} %slice.394), custom_call_target="Cholesky" | custom-call | tf_op jit(solution)/shard_map/jit(cholesky)/cholesky | solution.py:108
  79.0 9.8 %custom-call.12 = f32[1,128,128]{1,2,0:T(8,128)S(1)} custom-call(f32[1,128,128]{2,1,0:T(8,128)S(1)} %get-tuple-element.22), custom_call_target="InvertDiagBlocksLowerTriangular" | custom-call | tf_op jit(solution)/shard_map/jit(_solve_triangular)/triangular_solve | solution.py:109
  89.1 1.6 fusion.50
  91.6 1.9 convolution_subtract_fusion
  93.6 11.9 %cholesky.146 = f32[128,128]{1,0:T(8,128)S(1)} custom-call(f32[128,128]{1,0:T(8,128)S(1)} %slice.398), custom_call_target="Cholesky" | custom-call | tf_op jit(solution)/shard_map/jit(cholesky)/cholesky | solution.py:108
  106.8 9.8 %custom-call.13 = f32[1,128,128]{1,2,0:T(8,128)S(1)} custom-call(f32[1,128,128]{2,1,0:T(8,128)S(1)} %get-tuple-element.20), custom_call_target="InvertDiagBlocksLowerTriangular" | custom-call | tf_op jit(solution)/shard_map/jit(_solve_triangular)/triangular_solve | solution.py:109
  119.7 1.8 convolution_subtract_fusion.1
  121.5 11.7 %cholesky.157 = f32[128,128]{1,0:T(8,128)S(1)} custom-call(f32[128,128]{1,0:T(8,128)S(1)} %slice.402), custom_call_target="Cholesky" | custom-call | tf_op jit(solution)/shard_map/jit(cholesky)/cholesky | solution.py:108
  133.9 1.3 select_bitcast_fusion.5
  135.2 9.8 %custom-call.14 = f32[1,128,128]{1,2,0:T(8,128)S(1)} custom-call(f32[1,128,128]{2,1,0:T(8,128)S(1)} %get-tuple-element.18), custom_call_target="InvertDiagBlocksLowerTriangular" | custom-call | tf_op jit(solution)/shard_map/jit(_solve_triangular)/triangular_solve | solution.py:109
  145.7 2.0 convolution_subtract_fusion.2
  148.4 12.1 %cholesky.168 = f32[128,128]{1,0:T(8,128)S(1)} custom-call(f32[128,128]{1,0:T(8,128)S(1)} %slice.407), custom_call_target="Cholesky" | custom-call | tf_op jit(solution)/shard_map/jit(cholesky)/cholesky | solution.py:108
  161.9 9.8 %custom-call.15 = f32[1,128,128]{1,2,0:T(8,128)S(1)} custom-call(f32[1,128,128]{2,1,0:T(8,128)S(1)} %get-tuple-element.16), custom_call_target="InvertDiagBlocksLowerTriangular" | custom-call | tf_op jit(solution)/shard_map/jit(_solve_triangular)/triangular_solve | solution.py:109
  172.0 1.3 fusion.77
  175.4 1.9 convolution_subtract_fusion.3
  177.3 11.7 %cholesky.179 = f32[128,128]{1,0:T(8,128)S(1)} custom-call(f32[128,128]{1,0:T(8,128)S(1)} %slice.413), custom_call_target="Cholesky" | custom-call | tf_op jit(solution)/shard_map/jit(cholesky)/cholesky | solution.py:108
  190.4 10.0 %custom-call.16 = f32[1,128,128]{1,2,0:T(8,128)S(1)} custom-call(f32[1,128,128]{2,1,0:T(8,128)S(1)} %get-tuple-element.14), custom_call_target="InvertDiagBlocksLowerTriangular" | custom-call | tf_op jit(solution)/shard_map/jit(_solve_triangular)/triangular_solve | solution.py:109
  202.7 1.0 constant_dynamic-update-slice_fusion
  203.7 2.3 convolution_subtract_fusion.4
  206.0 11.7 %cholesky.190 = f32[128,128]{1,0:T(8,128)S(1)} custom-call(f32[128,128]{1,0:T(8,128)S(1)} %slice.421), custom_call_target="Cholesky" | custom-call | tf_op jit(solution)/shard_map/jit(cholesky)/cholesky | solution.py:108
  219.1 9.8 %custom-call.17 = f32[1,128,128]{1,2,0:T(8,128)S(1)} custom-call(f32[1,128,128]{2,1,0:T(8,128)S(1)} %get-tuple-element.12), custom_call_target="InvertDiagBlocksLowerTriangular" | custom-call | tf_op jit(solution)/shard_map/jit(_solve_triangular)/triangular_solve | solution.py:109
  233.4 2.0 convolution_subtract_fusion.5
  235.4 11.9 %cholesky.201 = f32[128,128]{1,0:T(8,128)S(1)} custom-call(f32[128,128]{1,0:T(8,128)S(1)} %slice.430), custom_call_target="Cholesky" | custom-call | tf_op jit(solution)/shard_map/jit(cholesky)/cholesky | solution.py:108
  248.7 9.8 %custom-call.18 = f32[1,128,128]{1,2,0:T(8,128)S(1)} custom-call(f32[1,128,128]{2,1,0:T(8,128)S(1)} %get-tuple-element.10), custom_call_target="InvertDiagBlocksLowerTriangular" | custom-call | tf_op jit(solution)/shard_map/jit(_solve_triangular)/triangular_solve | solution.py:109
  260.4 1.8 convolution_subtract_fusion.6
  262.2 11.7 %cholesky.212 = f32[128,128]{1,0:T(8,128)S(1)} custom-call(f32[128,128]{1,0:T(8,128)S(1)} %convolution_subtract_fusion.6), custom_call_target="Cholesky" | custom-call | tf_op jit(solution)/shard_map/jit(cholesky)/cholesky | solution.py:108
  275.2 9.8 %custom-call.19 = f32[1,128,128]{1,2,0:T(8,128)S(1)} custom-call(f32[1,128,128]{2,1,0:T(8,128)S(1)} %get-tuple-element.8), custom_call_target="InvertDiagBlocksLowerTriangular" | custom-call | tf_op jit(solution)/shard_map/jit(_solve_triangular)/triangular_solve | solution.py:109
  289.6 1.8 fusion.16
  292.0 1.9 fusion.12
  293.9 1.9 fusion.11
  295.9 2.1 fusion.145
  298.1 1.7 fusion.9
  300.2 1.9 convolution_add_fusion.5
  302.4 1.8 convolution_add_fusion.4
  304.6 1.8 convolution_add_fusion.3
  306.5 2.7 subtract_select_fusion
  309.1 1.0 constant_dynamic-update-slice_fusion.17
  310.2 3.6 fusion.18
  313.9 3.3 fusion.142
  317.2 1.7 fusion.7
  318.9 1.8 convolution_add_fusion.2
  320.7 2.0 convolution_add_fusion.1
  322.7 1.8 convolution_add_fusion
  324.5 2.5 pad_subtract_fusion
  327.0 1.0 constant_dynamic-update-slice_fusion.16
  328.0 2.3 slice.458
  330.3 8.3 %select_reduce_fusion = f32[32,32,1024]{2,1,0:T(8,128)} fusion(f32[8,32,1024]{2,1,0:T(8,128)} %bitcast.188, pred[8,32,1024]{2,1,0:T(8,128)(4,1)S(1)} %copy-done.16), kind=kLoop, calls=%fused_computation | loop fusion | flops 15728640 | bytes 5505024 | tf_op jit(solution)/shard_map/reduce_sum | solution.py:31
  338.7 4.3 %convolution_dynamic-update-slice_fusion = f32[256,4096]{1,0:T(8,128)S(1)} fusion(f32[256,1024]{1,0:T(8,128)S(1)} %fusion.142, f32[1024,1024]{1,0:T(8,128)} %bitcast.181), kind=kOutput, calls=%fused_computation.29 | convolution fusion | flops 1610612736 | bytes 6291456 | tf_op jit(solution)/shard_map/dot_general | solution.py:14
  342.9 1.6 fusion.148
  344.5 2.3 select_reduce_fusion.3
  346.8 1.2 convolution_dynamic-update-slice_fusion.4
  348.1 1.0 select_reduce_fusion.5
  349.8 2.3 fusion.114
  352.2 1.1 fusion.14
  353.3 1.1 convolution_subtract_fusion.7
  356.9 2.0 select_reduce_fusion.2
  358.9 1.2 convolution_dynamic-update-slice_fusion.1
  360.1 2.5 sub.48
  (202 shorter events, 47.0 us)
Async XLA Ops:
  7.2 33.0 %copy-start.26 = (s32[8,8]{1,0:T(8,128)S(1)}, s32[8,8]{1,0:T(8,128)}, u32[]{:S(2)}) copy-start(s32[8,8]{1,0:T(8,128)} %param.12) | copy-start | bytes 772
  7.2 57.9 %all-gather.7.cloned.1.call-start = ((), (), s32[]{:S(2)}) async-start(), calls=%async_computation | async-start | bytes 4456448 | tf_op jit(solution)/shard_map/all_gather | solution.py:94
  9.4 110.3 %all-gather.9.cloned.1.call-start = ((), (), s32[]{:S(2)}) async-start(), calls=%async_computation.1 | async-start | bytes 4456448 | tf_op jit(solution)/shard_map/all_gather | solution.py:94
  10.2 165.2 %all-gather.11.cloned.1.call-start = ((), (), s32[]{:S(2)}) async-start(), calls=%async_computation.2 | async-start | bytes 4456448 | tf_op jit(solution)/shard_map/all_gather | solution.py:94
  10.9 222.5 %all-gather.13.cloned.1.call-start = ((), (), s32[]{:S(2)}) async-start(), calls=%async_computation.3 | async-start | bytes 4456448 | tf_op jit(solution)/shard_map/all_gather | solution.py:94
  11.5 316.5 %all-gather.15.cloned.1.call-start = ((), (), s32[]{:S(2)}) async-start(), calls=%async_computation.4 | async-start | bytes 4456448 | tf_op jit(solution)/shard_map/all_gather | solution.py:142
  147.7 0.7 copy-start.7
  203.7 81.7 %copy-start.20 = (f32[1,128,128]{2,1,0:T(8,128)S(1)}, f32[1,128,128]{2,1,0:T(8,128)}, u32[]{:S(2)}) copy-start(f32[1,128,128]{2,1,0:T(8,128)} %get-tuple-element.38) | copy-start | bytes 196612
  285.0 2.2 copy-start.23
  288.7 0.8 copy-start.19
  289.2 6.7 %copy-start.10 = (f32[1,512,512]{2,1,0:T(8,128)}, f32[1,512,512]{2,1,0:T(8,128)S(1)}, u32[]{:S(2)}) copy-start(f32[1,512,512]{2,1,0:T(8,128)S(1)} %get-tuple-element.32) | copy-start | bytes 3145732
  289.2 6.7 %copy-start.13 = (f32[1,512,512]{2,1,0:T(8,128)}, f32[1,512,512]{2,1,0:T(8,128)S(1)}, u32[]{:S(2)}) copy-start(f32[1,512,512]{2,1,0:T(8,128)S(1)} %get-tuple-element.33) | copy-start | bytes 3145732
  291.5 2.4 copy-start.5
  293.9 16.3 %copy-start.8 = (f32[1,512,512]{2,1,0:T(8,128)}, f32[1,512,512]{2,1,0:T(8,128)S(1)}, u32[]{:S(2)}) copy-start(f32[1,512,512]{2,1,0:T(8,128)S(1)} %fusion.12) | copy-start | bytes 3145732
  295.9 2.2 copy-start.1
  298.1 2.2 copy-start.2
  300.2 2.2 copy-start.3
  302.4 2.2 copy-start.4
  306.5 3.8 %copy-start = (f32[4096,256]{0,1:T(8,128)S(1)}, f32[4096,256]{0,1:T(8,128)}, u32[]{:S(2)}) copy-start(f32[4096,256]{0,1:T(8,128)} %copy.139) | copy-start | bytes 12582916
  310.2 3.6 copy-start.11
  310.2 3.6 copy-start.14
  327.0 3.4 copy-start.16
  338.7 5.9 %copy-start.18 = (pred[7,32,512]{2,1,0:T(8,128)(4,1)S(1)}, pred[7,32,512]{2,1,0:T(8,128)(4,1)}, u32[]{:S(2)}) copy-start(pred[7,32,512]{2,1,0:T(8,128)(4,1)} %iota_compare_fusion.6) | copy-start | bytes 344068
  342.9 5.1 %copy-start.22 = (pred[7,16,512]{2,1,0:T(8,128)(4,1)S(1)}, pred[7,16,512]{2,1,0:T(8,128)(4,1)}, u32[]{:S(2)}) copy-start(pred[7,16,512]{2,1,0:T(8,128)(4,1)} %broadcast_compare_fusion) | copy-start | bytes 172036
  346.8 3.0 copy-start.9
  346.8 3.0 copy-start.12
  346.8 3.0 copy-start.15
  349.8 2.4 copy-start.24
  349.8 3.5 copy-start.25
  349.8 4.7 %copy-start.27 = (f32[16,16]{1,0:T(8,128)S(1)}, f32[16,16]{1,0:T(8,128)}, u32[]{:S(2)}) copy-start(f32[16,16]{1,0:T(8,128)} %param.16) | copy-start | bytes 3076
  349.8 5.4 %copy-start.21 = (pred[7,16,512]{2,1,0:T(8,128)(4,1)S(1)}, pred[7,16,512]{2,1,0:T(8,128)(4,1)}, u32[]{:S(2)}) copy-start(pred[7,16,512]{2,1,0:T(8,128)(4,1)} %iota_compare_fusion.7) | copy-start | bytes 172036
  352.2 4.7 %copy-start.17 = (pred[7,32,512]{2,1,0:T(8,128)(4,1)S(1)}, pred[7,32,512]{2,1,0:T(8,128)(4,1)}, u32[]{:S(2)}) copy-start(pred[7,32,512]{2,1,0:T(8,128)(4,1)} %iota_compare_fusion.5) | copy-start | bytes 344068
  356.2 3.9 %copy-start.6 = (f32[256,4096]{1,0:T(8,128)S(1)}, f32[256,4096]{1,0:T(8,128)}, u32[]{:S(2)}) copy-start(f32[256,4096]{1,0:T(8,128)} %param.13) | copy-start | bytes 12582916
Sparse Core Ops, SparseCore 0:
  10.7 54.2 all-gather.6
  67.2 49.5 all-gather.8
  119.0 49.7 all-gather.10
  170.8 49.4 all-gather.12
  222.3 53.3 all-gather.14
